TPU v7x, 512 devices: a whole 4x8x8 slice. The times are simulated.
512 devices in a mesh: seq: 128 (over z, y, core), tensor: 4 (over x).
Axes of the slice: x: 4, y: 8, z: 8, core: 2. Of those that a mesh axis runs over, the one named last changes fastest.
Arguments:
- hidden_in: bfloat16 [32768, 2048], P('seq', 'tensor'), may hold values from -6 to 6
- norm_gain: bfloat16 [2048], replicated, may hold values from 0.5 to 1.5
- query_weight: bfloat16 [2048, 2048], P(None, 'tensor'), may hold values from -2 to 2
- keyval_weight: bfloat16 [2048, 2048], P(None, 'tensor'), may hold values from -8 to 8
- output_weight: bfloat16 [2048, 2048], P('tensor'), may hold values from -0.125 to 0.125
- segment_ids: int32 [32768], P('seq'), may hold values from -1 to 127, as said below
- request_lengths: int32 [128], replicated, may hold values from 1 to 512, as said below
- request_owner: int32 [128], replicated, may hold values from 0 to 127, each once
- cache_slots: int32 [128], replicated, may hold values from 0 to 1
Outputs:
- attended: bfloat16 [32768, 2048], P('seq', 'tensor')
- kv_cache: bfloat16 [256, 512, 2048], P('seq', None, 'tensor')
Inputs may be any that keep to these rules, and one draw needn't show every extreme that they name: `segment_ids`: in the packed stream (position t = i * 128 + s for row i of index s of seq) the requests follow one another in order, request r taking request_lengths[r] consecutive positions from start[r]; positions from 28672 on hold -1. `request_lengths`: they sum to 28672; the largest is exactly 512.
All inputs are finite; a program needn't handle non-finite values.
Results may differ from a plain program's by a relative error of at most 0.012.
The roundings to bfloat16 on the way count: a program that leaves them out, or rounds other values in their place, can miss the bound.
Values may be sent and summed in bfloat16 or wider, within the bound.
No kernel may reach another device: no remote copies, remote signals or barrier semaphores. Data moves between devices by JAX's collectives and lax.ppermute only.
A program may use at most 64 MiB of HBM per device.

v0:
```python
import jax
import jax.numpy as jnp
from jax import lax
from jax.sharding import PartitionSpec as P

HEADS = 8
KV_HEADS = 4
HD = 256
SLOTS_DEV = 2
MAXLEN = 512


EPSILON = 1e-06
ROPE_BASE = 1000042.0
CHUNKS = 1


def rotate_rows(values, head_size, first_pos):
    row_count = values.shape[0]
    shaped = values.reshape(row_count, -1, head_size)
    half_size = head_size // 2
    frequency = ROPE_BASE ** (jnp.arange(half_size, dtype=jnp.float32) * (-2.0 / head_size))
    positions = (first_pos + jnp.arange(row_count, dtype=jnp.int32)).astype(jnp.float32)
    angles = positions[:, None] * frequency[None, :]
    cosine_table = jnp.cos(angles)[:, None, :]
    sine_table = jnp.sin(angles)[:, None, :]
    first_half = shaped[..., :half_size]
    second_half = shaped[..., half_size:]
    turned = jnp.concatenate(
        [
            first_half * cosine_table - second_half * sine_table,
            second_half * cosine_table + first_half * sine_table,
        ],
        axis=-1,
    )
    return turned.reshape(values.shape)


def normalize(rows_in, gain):
    widened = rows_in.astype(jnp.float32)
    inverse_rms = lax.rsqrt(jnp.mean(widened * widened, axis=-1, keepdims=True) + EPSILON)
    return (widened * inverse_rms * gain.astype(jnp.float32)).astype(jnp.bfloat16)


def attend(query_block, start_row, key_rows, value_rows, length):
    row_count = query_block.shape[0]
    scores = jnp.dot(query_block, key_rows.T, preferred_element_type=jnp.float32) * key_rows.shape[
        1
    ] ** (-0.5)
    query_pos = start_row + jnp.arange(row_count, dtype=jnp.int32)[:, None]
    key_pos = jnp.arange(key_rows.shape[0], dtype=jnp.int32)[None, :]
    allowed = (key_pos <= query_pos) & (key_pos < length)
    scores = jnp.where(allowed, scores, -jnp.inf)
    row_top = jnp.max(scores, axis=-1, keepdims=True)
    powered = jnp.exp(scores - row_top)
    weights = (powered / jnp.sum(powered, axis=-1, keepdims=True)).astype(jnp.bfloat16)
    return jnp.dot(weights, value_rows, preferred_element_type=jnp.float32).astype(jnp.bfloat16)


def to_request(received, shift_by):
    rolled = jnp.roll(received, -shift_by, axis=0)
    return jnp.swapaxes(rolled, 0, 1).reshape(-1, received.shape[2])


def from_request(request_rows, shift_by, source_count):
    shaped = request_rows.reshape(-1, source_count, request_rows.shape[1])
    return jnp.roll(jnp.swapaxes(shaped, 0, 1), shift_by, axis=0)


def body(
    hidden_in,
    norm_gain,
    query_weight,
    keyval_weight,
    output_weight,
    segment_ids,
    request_lengths,
    request_owner,
    cache_slots,
):
    source_count = lax.axis_size("seq")
    source_pos = lax.axis_index("seq")
    local_rows = hidden_in.shape[0]
    capacity = MAXLEN // source_count
    chunk_slots = capacity // CHUNKS
    chunk_rows = chunk_slots * source_count
    request_ids = jnp.arange(source_count, dtype=jnp.int32)
    starts = jnp.cumsum(request_lengths) - request_lengths
    first_row = jnp.maximum((starts - source_pos + source_count - 1) // source_count, 0)
    owner_match = request_owner[None, :] == request_ids[:, None]
    owned_by = jnp.sum(jnp.where(owner_match, request_ids[None, :], 0), axis=1)
    send_first = jnp.sum(jnp.where(owner_match, first_row[None, :], 0), axis=1)
    row_index = send_first[:, None] + jnp.arange(capacity, dtype=jnp.int32)[None, :]
    safe_index = jnp.minimum(row_index, local_rows - 1)
    live_send = (row_index < local_rows) & (segment_ids[safe_index] == owned_by[:, None])
    owned_request = jnp.sum(jnp.where(request_owner == source_pos, request_ids, 0))
    own_match = request_ids == owned_request
    own_start = jnp.sum(jnp.where(own_match, starts, 0))
    own_length = jnp.sum(jnp.where(own_match, request_lengths, 0))
    own_slot = jnp.sum(jnp.where(own_match, cache_slots, 0))
    shift_by = own_start % source_count
    picked = jnp.where(live_send[:, :, None], hidden_in[safe_index], jnp.zeros((), jnp.bfloat16))
    head_count = query_weight.shape[1] // HD
    per_group = HEADS // KV_HEADS
    block_count = keyval_weight.shape[1] // HD
    key_chunks = []
    value_chunks = []
    cached_chunks = []
    returned_chunks = []
    for chunk in range(CHUNKS):
        chunk_first = chunk * chunk_rows
        arrived = lax.all_to_all(
            picked[:, chunk * chunk_slots : (chunk + 1) * chunk_slots],
            "seq",
            split_axis=0,
            concat_axis=0,
            tiled=True,
        )
        narrow_rows = to_request(arrived, shift_by)
        full_rows = lax.all_gather(narrow_rows, "tensor", axis=1, tiled=True)
        normed = normalize(full_rows, norm_gain)
        queries = jnp.dot(normed, query_weight, preferred_element_type=jnp.float32)
        keyvals = jnp.dot(normed, keyval_weight, preferred_element_type=jnp.float32)
        rotated_query = rotate_rows(queries, HD, chunk_first).astype(jnp.bfloat16)
        own_blocks = []
        for block_index in range(block_count):
            plain_block = keyvals[:, block_index * HD : (block_index + 1) * HD]
            if block_index % 2 == 0:
                own_blocks.append(rotate_rows(plain_block, HD, chunk_first).astype(jnp.bfloat16))
            else:
                own_blocks.append(plain_block.astype(jnp.bfloat16))
        own_cached = jnp.concatenate(own_blocks, axis=1)
        cached_chunks.append(own_cached)
        key_chunks.append(own_cached[:, 0:HD])
        value_chunks.append(own_cached[:, HD : 2 * HD])
        key_rows = jnp.concatenate(key_chunks, axis=0)
        value_rows = jnp.concatenate(value_chunks, axis=0)
        head_outputs = []
        for head_index in range(head_count):
            head_outputs.append(
                attend(
                    rotated_query[:, head_index * HD : (head_index + 1) * HD],
                    chunk_first,
                    key_rows,
                    value_rows,
                    own_length,
                )
            )
        attention_rows = jnp.concatenate(head_outputs, axis=1)
        outgoing = from_request(attention_rows, shift_by, source_count)
        returned_chunks.append(
            lax.all_to_all(outgoing, "seq", split_axis=0, concat_axis=0, tiled=True)
        )
    returned = jnp.concatenate(returned_chunks, axis=1)
    segment_match = segment_ids[:, None] == request_ids[None, :]
    row_owner = jnp.sum(jnp.where(segment_match, request_owner[None, :], 0), axis=1)
    row_first = jnp.sum(jnp.where(segment_match, first_row[None, :], 0), axis=1)
    slot_pos = jnp.arange(local_rows, dtype=jnp.int32) - row_first
    usable = (segment_ids >= 0) & (slot_pos >= 0) & (slot_pos < capacity)
    flat_index = row_owner * capacity + jnp.clip(slot_pos, 0, capacity - 1)
    flattened = returned.reshape(-1, returned.shape[2])
    local_attention = jnp.where(usable[:, None], flattened[flat_index], jnp.zeros((), returned.dtype))
    partial_sum = jnp.dot(local_attention, output_weight, preferred_element_type=jnp.float32)
    attended = lax.psum_scatter(
        partial_sum.astype(jnp.bfloat16), "tensor", scatter_dimension=1, tiled=True
    )
    all_cached = jnp.concatenate(cached_chunks, axis=0)
    slot_ids = jnp.arange(SLOTS_DEV, dtype=jnp.int32)
    cache_table = jnp.where(
        (slot_ids == own_slot)[:, None, None], all_cached[None], jnp.zeros((), jnp.bfloat16)
    )
    return (attended, cache_table)


def solution(mesh):
    in_specs = (
        P("seq", "tensor"),
        P(),
        P(None, "tensor"),
        P(None, "tensor"),
        P("tensor", None),
        P("seq"),
        P(),
        P(),
        P(),
    )
    out_specs = (P("seq", "tensor"), P("seq", None, "tensor"))
    return jax.shard_map(body, mesh=mesh, in_specs=in_specs, out_specs=out_specs, check_vma=False)
```

profile of v0, /device:TPU:1, one launch (start us, length us, event | category | flops | bytes accessed | tf_op | source)
XLA Modules:
  0.0 164.3 jit_solution(13765148701509135680)
XLA Ops:
  7.2 0.9 copy.31
  8.4 1.3 fusion.28
  9.7 2.0 %select_reduce_fusion.6 = (s32[]{:T(128)}, s32[]{:T(128)}, s32[128]{0:T(128)S(1)}) fusion(s32[128]{0:T(128)} %param.17, s32[]{:T(128)} %fusion.28, s32[128]{0:T(128)S(1)} %reduce, s32[]{:T(128)S(6)} %axis_index.15), kind=kLoop, calls=%fused_computation.84 | loop fusion | flops 3070 | bytes 1552 | tf_op jit(solution)/shard_map/reduce_sum | solution.py:99
  12.7 2.0 %gather_fusion.1 = bf16[512,512]{1,0:T(8,128)(2,1)S(1)} fusion(bf16[256,512]{1,0:T(8,128)(2,1)S(1)} %copy-done.2, s32[1024]{0:T(1024)S(1)} %pad_clamp_fusion.1), kind=kCustom, calls=%fused_computation.1 | custom fusion | bytes 1050624 | tf_op jit(solution)/shard_map/gather | solution.py:102
  14.8 3.5 %gather_fusion = s32[512]{0:T(512)S(1)} fusion(s32[256]{0:T(256)S(1)} %copy-done.1, s32[1024]{0:T(1024)S(1)} %pad_clamp_fusion.1), kind=kCustom, calls=%fused_computation | custom fusion | bytes 6144 | tf_op jit(solution)/shard_map/gather | solution.py:95
  18.6 1.1 broadcast_select_fusion.1
  19.7 18.6 %all-to-all-start = ((bf16[128,4,512]{2,1,0:T(4,128)(2,1)}), bf16[128,4,512]{2,1,0:T(4,128)(2,1)S(1)}, u32[]{:S(2)}, u32[]{:S(2)}) async-start(bf16[128,4,512]{2,1,0:T(4,128)(2,1)} %broadcast_select_fusion.1), calls=%async_computation | async-start | bytes 1048576 | tf_op jit(solution)/shard_map/all_to_all | solution.py:112
  40.6 18.2 %all-to-all-done = bf16[128,4,512]{2,1,0:T(4,128)(2,1)S(1)} async-done(((bf16[128,4,512]{2,1,0:T(4,128)(2,1)}), bf16[128,4,512]{2,1,0:T(4,128)(2,1)S(1)}, u32[]{:S(2)}, u32[]{:S(2)}) %all-to-all-start) | async-done | bytes 524320 | tf_op jit(solution)/shard_map/all_to_all | solution.py:112
  59.0 1.2 fusion.13
  60.9 1.0 multiply_cosine_fusion.1
  61.9 27.1 %all-gather.2.cloned.1.call-done = bf16[512,2048]{1,0:T(8,128)(2,1)} async-done(((bf16[512,512]{1,0:T(8,128)(2,1)}), bf16[512,2048]{1,0:T(8,128)(2,1)}) %all-gather.2.cloned.1.call-update) | async-done | bytes 2097168 | tf_op jit(solution)/shard_map/all_gather | solution.py:120
  89.0 2.2 %fusion = f32[512]{0:T(512)S(1)} fusion(bf16[512,2048]{1,0:T(8,128)(2,1)} %all-gather.2.cloned.1.call-done), kind=kLoop, calls=%fused_computation.5 | loop fusion | flops 3145216 | bytes 2099200 | tf_op jit(solution)/shard_map/reduce_sum | solution.py:41
  91.2 3.2 %fusion.8 = f32[512,512]{0,1:T(8,128)S(1)} fusion(bf16[2048,512]{1,0:T(8,128)(2,1)} %param.14, bf16[512,2048]{1,0:T(8,128)(2,1)S(1)} %copy-done.3, f32[2048]{0:T(1024)S(1)} %convert_element_type.56, f32[512]{0:T(512)S(1)} %add_rsqrt_fusion), kind=kOutput, calls=%fused_computation.28 | convolution fusion | flops 1077936128 | bytes 5253120 | tf_op jit(solution)/shard_map/dot_general | solution.py:123
  94.5 1.2 fusion.19
  95.6 1.4 fusion.10
  100.0 1.2 copy.38
  101.1 14.3 %all-to-all-start.1 = ((bf16[128,4,512]{2,1,0:T(4,128)(2,1)}), bf16[128,4,512]{2,1,0:T(4,128)(2,1)S(1)}, u32[]{:S(2)}, u32[]{:S(2)}) async-start(bf16[128,4,512]{2,1,0:T(4,128)(2,1)} %copy.38), calls=%async_computation.1 | async-start | bytes 1048576 | tf_op jit(solution)/shard_map/all_to_all | solution.py:152
  115.8 20.2 %all-to-all-done.1 = bf16[128,4,512]{2,1,0:T(4,128)(2,1)S(1)} async-done(((bf16[128,4,512]{2,1,0:T(4,128)(2,1)}), bf16[128,4,512]{2,1,0:T(4,128)(2,1)S(1)}, u32[]{:S(2)}, u32[]{:S(2)}) %all-to-all-start.1) | async-done | bytes 524320 | tf_op jit(solution)/shard_map/all_to_all | solution.py:152
  136.1 1.2 gather_fusion.2
  137.3 1.8 %convolution_convert_fusion = bf16[256,2048]{1,0:T(8,128)(2,1)} fusion(bf16[512,2048]{1,0:T(8,128)(2,1)S(1)} %copy-done, bf16[256,512]{1,0:T(8,128)(2,1)S(1)} %gather_fusion.2, pred[256]{0:T(512)(128)(4,1)S(1)} %compare_and_fusion), kind=kOutput, calls=%fused_computation.8 | convolution fusion | flops 537526272 | bytes 3408128 | tf_op jit(solution)/shard_map/dot_general | solution.py:163
  139.1 1.3 select_reduce_fusion.4
  141.1 1.1 slice.61
  142.5 1.1 broadcast_select_fusion
  143.6 13.9 %reduce-scatter.2.cloned.1.call-done = bf16[256,512]{1,0:T(8,128)(2,1)} async-done(((bf16[256,2048]{1,0:T(8,128)(2,1)}), bf16[256,512]{1,0:T(8,128)(2,1)}) %reduce-scatter.2.cloned.1.call-update) | async-done | bytes 262160 | tf_op jit(solution)/shard_map/reduce_scatter | solution.py:164
  (59 shorter events, 6.9 us)
Async XLA Ops:
  7.2 130.1 %copy-start = (bf16[512,2048]{1,0:T(8,128)(2,1)S(1)}, bf16[512,2048]{1,0:T(8,128)(2,1)}, u32[]{:S(2)}) copy-start(bf16[512,2048]{1,0:T(8,128)(2,1)} %param.15) | copy-start | bytes 6291460
  7.2 5.5 %copy-start.2 = (bf16[256,512]{1,0:T(8,128)(2,1)S(1)}, bf16[256,512]{1,0:T(8,128)(2,1)}, u32[]{:S(2)}) copy-start(bf16[256,512]{1,0:T(8,128)(2,1)} %param.11) | copy-start | bytes 786436
  12.7 2.1 %copy-start.1 = (s32[256]{0:T(256)S(1)}, s32[256]{0:T(256)}, u32[]{:S(2)}) copy-start(s32[256]{0:T(256)} %param.16) | copy-start | bytes 3076
  19.7 40.5 %copy-start.5 = (bf16[2048]{0:T(1024)(128)(2,1)S(1)}, bf16[2048]{0:T(1024)(128)(2,1)}, u32[]{:S(2)}) copy-start(bf16[2048]{0:T(1024)(128)(2,1)} %param.12) | copy-start | bytes 12292
  19.7 39.1 %all-to-all-start = ((bf16[128,4,512]{2,1,0:T(4,128)(2,1)}), bf16[128,4,512]{2,1,0:T(4,128)(2,1)S(1)}, u32[]{:S(2)}, u32[]{:S(2)}) async-start(bf16[128,4,512]{2,1,0:T(4,128)(2,1)} %broadcast_select_fusion.1), calls=%async_computation | async-start | bytes 1048576 | tf_op jit(solution)/shard_map/all_to_all | solution.py:112
  38.3 50.7 %all-gather.2.cloned.1.call-start = ((), (), s32[]{:S(2)}) async-start(), calls=%async_computation.3 | async-start | bytes 2621440 | tf_op jit(solution)/shard_map/all_gather | solution.py:120
  89.0 2.2 %copy-start.3 = (bf16[512,2048]{1,0:T(8,128)(2,1)S(1)}, bf16[512,2048]{1,0:T(8,128)(2,1)}, u32[]{:S(2)}) copy-start(bf16[512,2048]{1,0:T(8,128)(2,1)} %all-gather.2.cloned.1.call-done) | copy-start | bytes 6291460
  91.2 4.4 %copy-start.7 = (bf16[2048,512]{1,0:T(8,128)(2,1)S(1)}, bf16[2048,512]{1,0:T(8,128)(2,1)}, u32[]{:S(2)}) copy-start(bf16[2048,512]{1,0:T(8,128)(2,1)} %param.13) | copy-start | bytes 6291460
  94.4 4.5 %copy-start.4 = (f32[512,512]{0,1:T(8,128)}, f32[512,512]{0,1:T(8,128)S(1)}, u32[]{:S(2)}) copy-start(f32[512,512]{0,1:T(8,128)S(1)} %fusion.8) | copy-start | bytes 3145732
  99.3 16.2 %copy-start.6 = (s32[128]{0:T(128)S(1)}, s32[128]{0:T(128)}, u32[]{:S(2)}) copy-start(s32[128]{0:T(128)} %param.18) | copy-start | bytes 1540
  101.1 34.9 %all-to-all-start.1 = ((bf16[128,4,512]{2,1,0:T(4,128)(2,1)}), bf16[128,4,512]{2,1,0:T(4,128)(2,1)S(1)}, u32[]{:S(2)}, u32[]{:S(2)}) async-start(bf16[128,4,512]{2,1,0:T(4,128)(2,1)} %copy.38), calls=%async_computation.1 | async-start | bytes 1048576 | tf_op jit(solution)/shard_map/all_to_all | solution.py:152
  115.4 42.1 %reduce-scatter.2.cloned.1.call-start = ((), (), s32[]{:S(2)}) async-start(), calls=%async_computation.4 | async-start | bytes 1310720 | tf_op jit(solution)/shard_map/reduce_scatter | solution.py:164
  137.3 1.8 %copy-start.8 = (s32[128]{0:T(128)S(1)}, s32[128]{0:T(128)}, u32[]{:S(2)}) copy-start(s32[128]{0:T(128)} %param.19) | copy-start | bytes 1540
Sparse Core Ops, SparseCore 0:
  60.3 28.6 all-gather.1
  139.2 18.2 reduce-scatter.1
where the time goes:
time: 166 us; the launch traced here: 164 us
  waiting for transfers between devices  79.4 us (48%)
  starting transfers between devices  33.1 us (20%)
  between operations  16.6 us (10%)
  other arithmetic  16.5 us (10%)
  local copies, waits for them, and re-layouts  10.9 us (7%)
  matrix products  7.85 us (5%)
    all_gather x1, waiting for transfers between devices, body(): full_rows = lax.all_gather(narrow_rows, 'tensor', axis=1, tiled=True)  27.1 us
    all_to_all x1, waiting for transfers between devices, body(): lax.all_to_all(outgoing, 'seq', split_axis=0, concat_axis=0, tiled=True)  20.2 us
    all_to_all x1, starting transfers between devices, body(): lax.all_to_all(picked[:, chunk * chunk_slots:(chunk + 1) * chunk_slots],...  18.6 us
    all_to_all x1, waiting for transfers between devices, body(): lax.all_to_all(picked[:, chunk * chunk_slots:(chunk + 1) * chunk_slots],...  18.2 us
    all_to_all x1, starting transfers between devices, body(): lax.all_to_all(outgoing, 'seq', split_axis=0, concat_axis=0, tiled=True)  14.3 us
    reduce_scatter x1, waiting for transfers between devices, body(): lax.psum_scatter(partial_sum.astype(jnp.bfloat16), 'tensor', scatter_dime...  13.9 us
    gather x2, local copies, waits for them, and re-layouts, body(): segment_ids[safe_index] == owned_by[:, None]  3.62 us
  transfers between devices with their start and end apart: 4, of which 4 were waited for; matrix products, arithmetic and copies ran while one was open for 4% of the time, Pallas kernels for 0%

commit v1 on v0

--- a/solution.py
+++ b/solution.py
@@ -1,7 +1,7 @@
 import jax
 import jax.numpy as jnp
 from jax import lax
-from jax.sharding import PartitionSpec as P
+from jax.sharding import Mesh, PartitionSpec as P
 
 HEADS = 8
 KV_HEADS = 4
@@ -13,6 +13,7 @@
 EPSILON = 1e-06
 ROPE_BASE = 1000042.0
 CHUNKS = 1
+LO_SIZE = 16
 
 
 def rotate_rows(values, head_size, first_pos):
@@ -57,6 +58,18 @@
     return jnp.dot(weights, value_rows, preferred_element_type=jnp.float32).astype(jnp.bfloat16)
 
 
+SEQ_AXES = ("seq_hi", "seq_lo")
+
+
+def seq_all_to_all(values):
+    hi = lax.axis_size("seq_hi")
+    lo = lax.axis_size("seq_lo")
+    shaped = values.reshape((hi, lo) + values.shape[1:])
+    shaped = lax.all_to_all(shaped, "seq_lo", split_axis=1, concat_axis=1, tiled=True)
+    shaped = lax.all_to_all(shaped, "seq_hi", split_axis=0, concat_axis=0, tiled=True)
+    return shaped.reshape(values.shape)
+
+
 def to_request(received, shift_by):
     rolled = jnp.roll(received, -shift_by, axis=0)
     return jnp.swapaxes(rolled, 0, 1).reshape(-1, received.shape[2])
@@ -78,8 +91,8 @@
     request_owner,
     cache_slots,
 ):
-    source_count = lax.axis_size("seq")
-    source_pos = lax.axis_index("seq")
+    source_count = lax.axis_size(SEQ_AXES)
+    source_pos = lax.axis_index(SEQ_AXES)
     local_rows = hidden_in.shape[0]
     capacity = MAXLEN // source_count
     chunk_slots = capacity // CHUNKS
@@ -109,13 +122,7 @@
     returned_chunks = []
     for chunk in range(CHUNKS):
         chunk_first = chunk * chunk_rows
-        arrived = lax.all_to_all(
-            picked[:, chunk * chunk_slots : (chunk + 1) * chunk_slots],
-            "seq",
-            split_axis=0,
-            concat_axis=0,
-            tiled=True,
-        )
+        arrived = seq_all_to_all(picked[:, chunk * chunk_slots : (chunk + 1) * chunk_slots])
         narrow_rows = to_request(arrived, shift_by)
         full_rows = lax.all_gather(narrow_rows, "tensor", axis=1, tiled=True)
         normed = normalize(full_rows, norm_gain)
@@ -148,9 +155,7 @@
             )
         attention_rows = jnp.concatenate(head_outputs, axis=1)
         outgoing = from_request(attention_rows, shift_by, source_count)
-        returned_chunks.append(
-            lax.all_to_all(outgoing, "seq", split_axis=0, concat_axis=0, tiled=True)
-        )
+        returned_chunks.append(seq_all_to_all(outgoing))
     returned = jnp.concatenate(returned_chunks, axis=1)
     segment_match = segment_ids[:, None] == request_ids[None, :]
     row_owner = jnp.sum(jnp.where(segment_match, request_owner[None, :], 0), axis=1)
@@ -173,16 +178,22 @@
 
 
 def solution(mesh):
+    seq_size = mesh.shape["seq"]
+    lo_size = LO_SIZE if seq_size % LO_SIZE == 0 else seq_size
+    split_mesh = Mesh(
+        mesh.devices.reshape(seq_size // lo_size, lo_size, mesh.shape["tensor"]),
+        SEQ_AXES + ("tensor",),
+    )
     in_specs = (
-        P("seq", "tensor"),
+        P(SEQ_AXES, "tensor"),
         P(),
         P(None, "tensor"),
         P(None, "tensor"),
         P("tensor", None),
-        P("seq"),
+        P(SEQ_AXES),
         P(),
         P(),
         P(),
     )
-    out_specs = (P("seq", "tensor"), P("seq", None, "tensor"))
-    return jax.shard_map(body, mesh=mesh, in_specs=in_specs, out_specs=out_specs, check_vma=False)
+    out_specs = (P(SEQ_AXES, "tensor"), P(SEQ_AXES, None, "tensor"))
+    return jax.shard_map(body, mesh=split_mesh, in_specs=in_specs, out_specs=out_specs, check_vma=False)

time: 166 us -> 194 us (1.17)
  blocking collectives: 0 us -> 51.2 us
  starting transfers between devices: 33.1 us -> 16.6 us
  waiting for transfers between devices: 79.4 us -> 72 us
    all_to_all x0 -> x2, blocking collectives: none -> 51.2 us  [seq_all_to_all(): lax.all_to_all(shaped, 'seq_lo', split_axis=1, concat_axis=1, tiled=True)]
    all_to_all x2, starting transfers between devices: 32.8 us -> 16.5 us  [seq_all_to_all(): lax.all_to_all(shaped, 'seq_hi', split_axis=0, concat_axis=0, tiled=True)]
    all_to_all x2, waiting for transfers between devices: 38.5 us -> 32.6 us  [seq_all_to_all(): lax.all_to_all(shaped, 'seq_hi', split_axis=0, concat_axis=0, tiled=True)]
    all_to_all x1 -> x4, local copies, waits for them, and re-layouts: 0.09 us -> 2.59 us  [the longest x2 2.08 us: seq_all_to_all(): lax.all_to_all(shaped, 'seq_lo', split_axis=1, concat_axis=1, tiled=True)]
  transfers between devices with their start and end apart: 4 -> 4, of which waited for: 4 -> 4; matrix products, arithmetic and copies ran while one was open for 4% -> 3% of each run, Pallas kernels for 0% -> 0%
where the time goes in v1:
time: 194 us; the launch traced here: 193 us
  waiting for transfers between devices  72 us (37%)
  blocking collectives  51.2 us (26%)
  starting transfers between devices  16.6 us (9%)
  between operations  16.6 us (9%)
  other arithmetic  15.7 us (8%)
  local copies, waits for them, and re-layouts  12.7 us (7%)
  matrix products  7.85 us (4%)
    all_to_all x2, blocking collectives, seq_all_to_all(): lax.all_to_all(shaped, 'seq_lo', split_axis=1, concat_axis=1, tiled=True)  51.2 us
    all_to_all x2, waiting for transfers between devices, seq_all_to_all(): lax.all_to_all(shaped, 'seq_hi', split_axis=0, concat_axis=0, tiled=True)  32.6 us
    all_gather x1, waiting for transfers between devices, body(): full_rows = lax.all_gather(narrow_rows, 'tensor', axis=1, tiled=True)  26.4 us
    all_to_all x2, starting transfers between devices, seq_all_to_all(): lax.all_to_all(shaped, 'seq_hi', split_axis=0, concat_axis=0, tiled=True)  16.5 us
    reduce_scatter x1, waiting for transfers between devices, body(): lax.psum_scatter(partial_sum.astype(jnp.bfloat16), 'tensor', scatter_dime...  12.9 us
  transfers between devices with their start and end apart: 4, of which 4 were waited for; matrix products, arithmetic and copies ran while one was open for 3% of the time, Pallas kernels for 0%

profile of v1, /device:TPU:1, one launch (start us, length us, event | category | flops | bytes accessed | tf_op | source)
XLA Modules:
  0.0 192.6 jit_solution(2838189700613120853)
XLA Ops:
  8.4 1.3 fusion.28
  9.7 2.0 %select_reduce_fusion.6 = (s32[]{:T(128)}, s32[]{:T(128)}, s32[128]{0:T(128)S(1)}) fusion(s32[128]{0:T(128)} %param.17, s32[]{:T(128)} %fusion.28, s32[128]{0:T(128)S(1)} %reduce, s32[]{:T(128)S(6)} %add.105), kind=kLoop, calls=%fused_computation.84 | loop fusion | flops 3070 | bytes 1552 | tf_op jit(solution)/shard_map/reduce_sum | solution.py:112
  12.8 2.0 %gather_fusion.1 = bf16[512,512]{1,0:T(8,128)(2,1)S(1)} fusion(bf16[256,512]{1,0:T(8,128)(2,1)S(1)} %copy-done.2, s32[1024]{0:T(1024)S(1)} %pad_clamp_fusion.1), kind=kCustom, calls=%fused_computation.1 | custom fusion | bytes 1050624 | tf_op jit(solution)/shard_map/gather | solution.py:115
  14.9 3.5 %gather_fusion = s32[512]{0:T(512)S(1)} fusion(s32[256]{0:T(256)S(1)} %copy-done.1, s32[1024]{0:T(1024)S(1)} %pad_clamp_fusion.1), kind=kCustom, calls=%fused_computation | custom fusion | bytes 6144 | tf_op jit(solution)/shard_map/gather | solution.py:108
  19.1 26.7 %all_to_all.20 = bf16[8,16,4,512]{3,2,0,1:T(4,128)(2,1)S(1)} all-to-all(bf16[8,16,4,512]{3,2,0,1:T(4,128)(2,1)S(1)} %copy_select_fusion), channel_id=1, replica_groups=mesh['seq_hi'=8,'seq_lo'=16,'tensor'=4] {'seq_lo'}, dimensions={1} | all-to-all | bytes 1048576 | tf_op jit(solution)/shard_map/all_to_all | solution.py:68
  45.8 1.0 copy.40
  46.8 9.2 %all-to-all-start.1 = ((bf16[8,16,4,512]{3,2,1,0:T(4,128)(2,1)}), bf16[8,16,4,512]{3,2,1,0:T(4,128)(2,1)S(1)}, u32[]{:S(2)}, u32[]{:S(2)}) async-start(bf16[8,16,4,512]{3,2,1,0:T(4,128)(2,1)} %copy.40), calls=%async_computation.1 | async-start | bytes 1048576 | tf_op jit(solution)/shard_map/all_to_all | solution.py:69
  58.2 15.4 %all-to-all-done.1 = bf16[8,16,4,512]{3,2,1,0:T(4,128)(2,1)S(1)} async-done(((bf16[8,16,4,512]{3,2,1,0:T(4,128)(2,1)}), bf16[8,16,4,512]{3,2,1,0:T(4,128)(2,1)S(1)}, u32[]{:S(2)}, u32[]{:S(2)}) %all-to-all-start.1) | async-done | bytes 524320 | tf_op jit(solution)/shard_map/all_to_all | solution.py:69
  73.7 1.2 fusion.13
  76.6 26.4 %all-gather.2.cloned.1.call-done = bf16[512,2048]{1,0:T(8,128)(2,1)} async-done(((bf16[512,512]{1,0:T(8,128)(2,1)}), bf16[512,2048]{1,0:T(8,128)(2,1)}) %all-gather.2.cloned.1.call-update) | async-done | bytes 2097168 | tf_op jit(solution)/shard_map/all_gather | solution.py:127
  103.0 2.2 %fusion = f32[512]{0:T(512)S(1)} fusion(bf16[512,2048]{1,0:T(8,128)(2,1)} %all-gather.2.cloned.1.call-done), kind=kLoop, calls=%fused_computation.5 | loop fusion | flops 3145216 | bytes 2099200 | tf_op jit(solution)/shard_map/reduce_sum | solution.py:42
  105.3 3.2 %fusion.8 = f32[512,512]{0,1:T(8,128)S(1)} fusion(bf16[2048,512]{1,0:T(8,128)(2,1)} %param.14, bf16[512,2048]{1,0:T(8,128)(2,1)S(1)} %copy-done.3, f32[2048]{0:T(1024)S(1)} %convert_element_type.56, f32[512]{0:T(512)S(1)} %add_rsqrt_fusion), kind=kOutput, calls=%fused_computation.28 | convolution fusion | flops 1077936128 | bytes 5253120 | tf_op jit(solution)/shard_map/dot_general | solution.py:130
  108.5 1.2 fusion.19
  109.7 1.4 fusion.10
  114.3 24.5 %all_to_all.21 = bf16[8,16,4,512]{3,0,2,1:T(8,128)(2,1)S(1)} all-to-all(bf16[8,16,4,512]{3,0,2,1:T(8,128)(2,1)S(1)} %copy.43), channel_id=1, replica_groups=mesh['seq_hi'=8,'seq_lo'=16,'tensor'=4] {'seq_lo'}, dimensions={1} | all-to-all | bytes 1048576 | tf_op jit(solution)/shard_map/all_to_all | solution.py:68
  138.8 1.1 copy.44
  139.9 7.3 %all-to-all-start.3 = ((bf16[8,16,4,512]{3,1,2,0:T(8,128)(2,1)}), bf16[8,16,4,512]{3,1,2,0:T(8,128)(2,1)S(1)}, u32[]{:S(2)}, u32[]{:S(2)}) async-start(bf16[8,16,4,512]{3,1,2,0:T(8,128)(2,1)} %copy.44), calls=%async_computation.3 | async-start | bytes 1048576 | tf_op jit(solution)/shard_map/all_to_all | solution.py:69
  147.5 17.2 %all-to-all-done.3 = bf16[8,16,4,512]{3,1,2,0:T(8,128)(2,1)S(1)} async-done(((bf16[8,16,4,512]{3,1,2,0:T(8,128)(2,1)}), bf16[8,16,4,512]{3,1,2,0:T(8,128)(2,1)S(1)}, u32[]{:S(2)}, u32[]{:S(2)}) %all-to-all-start.3) | async-done | bytes 524320 | tf_op jit(solution)/shard_map/all_to_all | solution.py:69
  165.3 1.2 gather_fusion.2
  166.5 1.8 convolution_convert_fusion
  168.3 1.3 select_reduce_fusion.4
  170.3 1.1 slice.61
  171.6 1.1 broadcast_select_fusion
  172.8 12.9 %reduce-scatter.2.cloned.1.call-done = bf16[256,512]{1,0:T(8,128)(2,1)} async-done(((bf16[256,2048]{1,0:T(8,128)(2,1)}), bf16[256,512]{1,0:T(8,128)(2,1)}) %reduce-scatter.2.cloned.1.call-update) | async-done | bytes 262160 | tf_op jit(solution)/shard_map/reduce_scatter | solution.py:169
  (67 shorter events, 9.8 us)
Async XLA Ops:
  7.2 159.3 %copy-start = (bf16[512,2048]{1,0:T(8,128)(2,1)S(1)}, bf16[512,2048]{1,0:T(8,128)(2,1)}, u32[]{:S(2)}) copy-start(bf16[512,2048]{1,0:T(8,128)(2,1)} %param.15) | copy-start | bytes 6291460
  7.2 5.6 %copy-start.2 = (bf16[256,512]{1,0:T(8,128)(2,1)S(1)}, bf16[256,512]{1,0:T(8,128)(2,1)}, u32[]{:S(2)}) copy-start(bf16[256,512]{1,0:T(8,128)(2,1)} %param.11) | copy-start | bytes 786436
  12.8 2.1 %copy-start.1 = (s32[256]{0:T(256)S(1)}, s32[256]{0:T(256)}, u32[]{:S(2)}) copy-start(s32[256]{0:T(256)} %param.16) | copy-start | bytes 3076
  46.8 28.2 %copy-start.5 = (bf16[2048]{0:T(1024)(128)(2,1)S(1)}, bf16[2048]{0:T(1024)(128)(2,1)}, u32[]{:S(2)}) copy-start(bf16[2048]{0:T(1024)(128)(2,1)} %param.12) | copy-start | bytes 12292
  46.8 26.8 %all-to-all-start.1 = ((bf16[8,16,4,512]{3,2,1,0:T(4,128)(2,1)}), bf16[8,16,4,512]{3,2,1,0:T(4,128)(2,1)S(1)}, u32[]{:S(2)}, u32[]{:S(2)}) async-start(bf16[8,16,4,512]{3,2,1,0:T(4,128)(2,1)} %copy.40), calls=%async_computation.1 | async-start | bytes 1048576 | tf_op jit(solution)/shard_map/all_to_all | solution.py:69
  56.0 47.0 %all-gather.2.cloned.1.call-start = ((), (), s32[]{:S(2)}) async-start(), calls=%async_computation.5 | async-start | bytes 2621440 | tf_op jit(solution)/shard_map/all_gather | solution.py:127
  103.0 2.2 %copy-start.3 = (bf16[512,2048]{1,0:T(8,128)(2,1)S(1)}, bf16[512,2048]{1,0:T(8,128)(2,1)}, u32[]{:S(2)}) copy-start(bf16[512,2048]{1,0:T(8,128)(2,1)} %all-gather.2.cloned.1.call-done) | copy-start | bytes 6291460
  105.3 4.4 %copy-start.7 = (bf16[2048,512]{1,0:T(8,128)(2,1)S(1)}, bf16[2048,512]{1,0:T(8,128)(2,1)}, u32[]{:S(2)}) copy-start(bf16[2048,512]{1,0:T(8,128)(2,1)} %param.13) | copy-start | bytes 6291460
  108.5 4.5 %copy-start.4 = (f32[512,512]{0,1:T(8,128)}, f32[512,512]{0,1:T(8,128)S(1)}, u32[]{:S(2)}) copy-start(f32[512,512]{0,1:T(8,128)S(1)} %fusion.8) | copy-start | bytes 3145732
  114.0 33.2 %copy-start.6 = (s32[128]{0:T(128)S(1)}, s32[128]{0:T(128)}, u32[]{:S(2)}) copy-start(s32[128]{0:T(128)} %param.18) | copy-start | bytes 1540
  139.9 24.8 %all-to-all-start.3 = ((bf16[8,16,4,512]{3,1,2,0:T(8,128)(2,1)}), bf16[8,16,4,512]{3,1,2,0:T(8,128)(2,1)S(1)}, u32[]{:S(2)}, u32[]{:S(2)}) async-start(bf16[8,16,4,512]{3,1,2,0:T(8,128)(2,1)} %copy.44), calls=%async_computation.3 | async-start | bytes 1048576 | tf_op jit(solution)/shard_map/all_to_all | solution.py:69
  147.2 38.5 %reduce-scatter.2.cloned.1.call-start = ((), (), s32[]{:S(2)}) async-start(), calls=%async_computation.6 | async-start | bytes 1310720 | tf_op jit(solution)/shard_map/reduce_scatter | solution.py:169
  166.5 1.8 copy-start.8
Sparse Core Ops, SparseCore 0:
  75.0 27.9 all-gather.1
  168.4 17.3 reduce-scatter.1

commit v2 on v0

--- a/solution.py
+++ b/solution.py
@@ -65,6 +65,30 @@
 def from_request(request_rows, shift_by, source_count):
     shaped = request_rows.reshape(-1, source_count, request_rows.shape[1])
     return jnp.roll(jnp.swapaxes(shaped, 0, 1), shift_by, axis=0)
+
+
+def ring_gather(narrow, axis_name):
+    count = lax.axis_size(axis_name)
+    position = lax.axis_index(axis_name)
+    stacked = [narrow]
+    for shift in range(1, count):
+        perm = [(index, (index - shift) % count) for index in range(count)]
+        stacked.append(lax.ppermute(narrow, axis_name, perm))
+    ordered = jnp.roll(jnp.stack(stacked, axis=0), position, axis=0)
+    return jnp.concatenate([ordered[index] for index in range(count)], axis=1)
+
+
+def ring_reduce_scatter(partial_rows, axis_name):
+    count = lax.axis_size(axis_name)
+    position = lax.axis_index(axis_name)
+    width = partial_rows.shape[1] // count
+    blocks = partial_rows.astype(jnp.bfloat16).reshape(partial_rows.shape[0], count, width)
+    total = lax.dynamic_index_in_dim(blocks, position, 1, keepdims=False).astype(jnp.float32)
+    for shift in range(1, count):
+        perm = [(index, (index + shift) % count) for index in range(count)]
+        outgoing = lax.dynamic_index_in_dim(blocks, (position + shift) % count, 1, keepdims=False)
+        total = total + lax.ppermute(outgoing, axis_name, perm).astype(jnp.float32)
+    return total.astype(jnp.bfloat16)
 
 
 def body(
@@ -117,7 +141,7 @@
             tiled=True,
         )
         narrow_rows = to_request(arrived, shift_by)
-        full_rows = lax.all_gather(narrow_rows, "tensor", axis=1, tiled=True)
+        full_rows = ring_gather(narrow_rows, "tensor")
         normed = normalize(full_rows, norm_gain)
         queries = jnp.dot(normed, query_weight, preferred_element_type=jnp.float32)
         keyvals = jnp.dot(normed, keyval_weight, preferred_element_type=jnp.float32)
@@ -161,9 +185,7 @@
     flattened = returned.reshape(-1, returned.shape[2])
     local_attention = jnp.where(usable[:, None], flattened[flat_index], jnp.zeros((), returned.dtype))
     partial_sum = jnp.dot(local_attention, output_weight, preferred_element_type=jnp.float32)
-    attended = lax.psum_scatter(
-        partial_sum.astype(jnp.bfloat16), "tensor", scatter_dimension=1, tiled=True
-    )
+    attended = ring_reduce_scatter(partial_sum, "tensor")
     all_cached = jnp.concatenate(cached_chunks, axis=0)
     slot_ids = jnp.arange(SLOTS_DEV, dtype=jnp.int32)
     cache_table = jnp.where(

time: 166 us -> 152 us (0.916)
  between operations: 16.6 us -> 3.38 us
  waiting for transfers between devices: 79.4 us -> 67.1 us
  starting transfers between devices: 33.1 us -> 42 us
  local copies, waits for them, and re-layouts: 10.9 us -> 18.5 us
  other arithmetic: 16.5 us -> 14.3 us
  matrix products: 7.85 us -> 6.13 us
    ppermute x0 -> x6, waiting for transfers between devices: none -> 31 us  [the longest x3 21.3 us: ring_gather(): stacked.append(lax.ppermute(narrow, axis_name, perm))]
    all_gather x1 -> x0, waiting for transfers between devices: 27.1 us -> none  [body(): full_rows = lax.all_gather(narrow_rows, 'tensor', axis=1, tiled=True)]
    ppermute x0 -> x6, starting transfers between devices: none -> 17.9 us  [the longest x3 9.5 us: ring_gather(): stacked.append(lax.ppermute(narrow, axis_name, perm))]
    reduce_scatter x1 -> x0, waiting for transfers between devices: 13.9 us -> none  [body(): lax.psum_scatter(partial_sum.astype(jnp.bfloat16), 'tensor', scatter_dime...]
    all_to_all x1, starting transfers between devices: 14.3 us -> 5.63 us  [body(): lax.all_to_all(outgoing, 'seq', split_axis=0, concat_axis=0, tiled=True)]
    unnamed x19 -> x31, local copies, waits for them, and re-layouts: 1.25 us -> 3.85 us
    all_to_all x1, waiting for transfers between devices: 20.2 us -> 17.7 us  [body(): lax.all_to_all(outgoing, 'seq', split_axis=0, concat_axis=0, tiled=True)]
    dynamic_slice x0 -> x1, local copies, waits for them, and re-layouts: none -> 2.17 us  [ring_reduce_scatter(): lax.dynamic_index_in_dim(blocks, position, 1, keepdims=False)]
  transfers between devices with their start and end apart: 4 -> 8, of which waited for: 4 -> 6; matrix products, arithmetic and copies ran while one was open for 4% -> 5% of each run, Pallas kernels for 0% -> 0%
where the time goes in v2:
time: 152 us; the launch traced here: 151 us
  waiting for transfers between devices  67.1 us (44%)
  starting transfers between devices  42 us (28%)
  local copies, waits for them, and re-layouts  18.5 us (12%)
  other arithmetic  14.3 us (9%)
  matrix products  6.13 us (4%)
  between operations  3.38 us (2%)
    ppermute x3, waiting for transfers between devices, ring_gather(): stacked.append(lax.ppermute(narrow, axis_name, perm))  21.3 us
    all_to_all x1, waiting for transfers between devices, body(): lax.all_to_all(picked[:, chunk * chunk_slots:(chunk + 1) * chunk_slots],...  18.5 us
    all_to_all x1, starting transfers between devices, body(): lax.all_to_all(picked[:, chunk * chunk_slots:(chunk + 1) * chunk_slots],...  18.4 us
    all_to_all x1, waiting for transfers between devices, body(): lax.all_to_all(outgoing, 'seq', split_axis=0, concat_axis=0, tiled=True)  17.7 us
    ppermute x3, waiting for transfers between devices, ring_reduce_scatter(): total = total + lax.ppermute(outgoing, axis_name, perm).astype(jnp.float32)  9.63 us
    ppermute x3, starting transfers between devices, ring_gather(): stacked.append(lax.ppermute(narrow, axis_name, perm))  9.5 us
    ppermute x3, starting transfers between devices, ring_reduce_scatter(): total = total + lax.ppermute(outgoing, axis_name, perm).astype(jnp.float32)  8.41 us
    all_to_all x1, starting transfers between devices, body(): lax.all_to_all(outgoing, 'seq', split_axis=0, concat_axis=0, tiled=True)  5.63 us
  transfers between devices with their start and end apart: 8, of which 6 were waited for; matrix products, arithmetic and copies ran while one was open for 5% of the time, Pallas kernels for 0%

profile of v2, /device:TPU:1, one launch (start us, length us, event | category | flops | bytes accessed | tf_op | source)
XLA Modules:
  0.0 151.3 jit_solution(6959831486762084610)
XLA Ops:
  1.8 1.3 fusion.31
  3.2 2.1 %select_reduce_fusion.6 = (s32[]{:T(128)}, s32[]{:T(128)}, s32[128]{0:T(128)S(1)}, s32[]{:T(128)}) fusion(s32[128]{0:T(128)} %param.17, s32[]{:T(128)} %fusion.31, s32[128]{0:T(128)S(1)} %reduce, s32[]{:T(128)S(6)} %axis_index.27, s32[128]{0:T(128)} %param.19), kind=kLoop, calls=%fused_computation.109 | loop fusion | flops 3325 | bytes 2068 | tf_op jit(solution)/shard_map/reduce_sum | solution.py:123
  6.2 3.5 %gather_fusion = s32[512]{0:T(512)S(1)} fusion(s32[256]{0:T(256)S(1)} %copy-done.1, s32[1024]{0:T(1024)S(1)} %pad_clamp_fusion.1), kind=kCustom, calls=%fused_computation | custom fusion | bytes 6144 | tf_op jit(solution)/shard_map/gather | solution.py:119
  9.9 2.0 %gather_fusion.1 = bf16[512,512]{1,0:T(8,128)(2,1)S(1)} fusion(bf16[256,512]{1,0:T(8,128)(2,1)S(1)} %copy-done.2, s32[1024]{0:T(1024)S(1)} %pad_clamp_fusion.1), kind=kCustom, calls=%fused_computation.1 | custom fusion | bytes 1050624 | tf_op jit(solution)/shard_map/gather | solution.py:126
  13.3 18.4 %all-to-all-start = ((bf16[128,4,512]{2,1,0:T(4,128)(2,1)}), bf16[128,4,512]{2,1,0:T(4,128)(2,1)S(1)}, u32[]{:S(2)}, u32[]{:S(2)}) async-start(bf16[128,4,512]{2,1,0:T(4,128)(2,1)} %broadcast_select_fusion.1), calls=%async_computation | async-start | bytes 1048576 | tf_op jit(solution)/shard_map/all_to_all | solution.py:136
  33.8 18.5 %all-to-all-done = bf16[128,4,512]{2,1,0:T(4,128)(2,1)S(1)} async-done(((bf16[128,4,512]{2,1,0:T(4,128)(2,1)}), bf16[128,4,512]{2,1,0:T(4,128)(2,1)S(1)}, u32[]{:S(2)}, u32[]{:S(2)}) %all-to-all-start) | async-done | bytes 524320 | tf_op jit(solution)/shard_map/all_to_all | solution.py:136
  52.8 4.4 %collective-permute-start = (bf16[512,512]{1,0:T(8,128)(2,1)S(1)}, bf16[512,512]{1,0:T(8,128)(2,1)S(1)}, u32[]{:S(2)}, u32[]{:S(2)}) collective-permute-start(bf16[512,512]{1,0:T(8,128)(2,1)S(1)} %bitcast.60), channel_id=1, source_target_pairs={{0,3},{1,0},{2,1},{3,2},{4,7},{5,4},{6,5},{7,6},{8,11},{9,8},{10,9... | collective-permute-start | bytes 1572872 | tf_op jit(solution)/shard_map/ppermute | solution.py:76
  57.2 1.8 %multiply_cosine_fusion.1 = (f32[512,128]{0,1:T(8,128)S(1)}, f32[512,128]{0,1:T(8,128)}) fusion(f32[128]{0:T(128)S(1)} %multiply_power_fusion, f32[512]{0:T(512)S(1)} %iota_convert_fusion), kind=kLoop, calls=%fused_computation.58 | loop fusion | flops 65536 | bytes 526848 | tf_op jit(solution)/shard_map/cos | solution.py:25
  58.9 2.4 %collective-permute-start.1 = (bf16[512,512]{1,0:T(8,128)(2,1)S(1)}, bf16[512,512]{1,0:T(8,128)(2,1)}, u32[]{:S(2)}, u32[]{:S(2)}) collective-permute-start(bf16[512,512]{1,0:T(8,128)(2,1)S(1)} %bitcast.61), channel_id=1, source_target_pairs={{0,2},{1,3},{2,0},{3,1},{4,6},{5,7},{6,4},{7,5},{8,10},{9,11},{10,... | collective-permute-start | bytes 1572872 | tf_op jit(solution)/shard_map/ppermute | solution.py:76
  62.2 2.7 %collective-permute-start.2 = (bf16[512,512]{1,0:T(8,128)(2,1)S(1)}, bf16[512,512]{1,0:T(8,128)(2,1)S(1)}, u32[]{:S(2)}, u32[]{:S(2)}) collective-permute-start(bf16[512,512]{1,0:T(8,128)(2,1)S(1)} %bitcast.62), channel_id=1, source_target_pairs={{0,1},{1,2},{2,3},{3,0},{4,5},{5,6},{6,7},{7,4},{8,9},{9,10},{10,1... | collective-permute-start | bytes 1572872 | tf_op jit(solution)/shard_map/ppermute | solution.py:76
  65.0 14.9 %collective-permute-done = bf16[512,512]{1,0:T(8,128)(2,1)S(1)} collective-permute-done((bf16[512,512]{1,0:T(8,128)(2,1)S(1)}, bf16[512,512]{1,0:T(8,128)(2,1)S(1)}, u32[]{:S(2)}, u32[]{:S(2)}) %collective-permute-start) | collective-permute-done | bytes 524320 | tf_op jit(solution)/shard_map/ppermute | solution.py:76
  81.1 6.4 %collective-permute-done.2 = bf16[512,512]{1,0:T(8,128)(2,1)S(1)} collective-permute-done((bf16[512,512]{1,0:T(8,128)(2,1)S(1)}, bf16[512,512]{1,0:T(8,128)(2,1)S(1)}, u32[]{:S(2)}, u32[]{:S(2)}) %collective-permute-start.2) | collective-permute-done | bytes 524320 | tf_op jit(solution)/shard_map/ppermute | solution.py:76
  89.5 1.5 fusion.8
  92.3 1.4 fusion.10
  97.8 5.6 %all-to-all-start.1 = ((bf16[128,4,512]{2,1,0:T(4,128)(2,1)}), bf16[128,4,512]{2,1,0:T(4,128)(2,1)S(1)}, u32[]{:S(2)}, u32[]{:S(2)}) async-start(bf16[128,4,512]{2,1,0:T(4,128)(2,1)} %copy.55), calls=%async_computation.1 | async-start | bytes 1048576 | tf_op jit(solution)/shard_map/all_to_all | solution.py:176
  106.4 17.7 %all-to-all-done.1 = bf16[128,4,512]{2,1,0:T(4,128)(2,1)S(1)} async-done(((bf16[128,4,512]{2,1,0:T(4,128)(2,1)}), bf16[128,4,512]{2,1,0:T(4,128)(2,1)S(1)}, u32[]{:S(2)}, u32[]{:S(2)}) %all-to-all-start.1) | async-done | bytes 524320 | tf_op jit(solution)/shard_map/all_to_all | solution.py:176
  125.4 1.7 %convolution_convert_fusion = bf16[256,2048]{1,0:T(8,128)(2,1)} fusion(bf16[512,2048]{1,0:T(8,128)(2,1)S(1)} %copy-done, bf16[256,512]{1,0:T(8,128)(2,1)S(1)} %gather_fusion.2, pred[256]{0:T(512)(128)(4,1)S(1)} %compare_and_fusion), kind=kOutput, calls=%fused_computation.8 | convolution fusion | flops 537526272 | bytes 3408128 | tf_op jit(solution)/shard_map/dot_general | solution.py:187
  127.1 1.8 %reshape.305 = bf16[256,4,512]{2,1,0:T(4,128)(2,1)S(1)} reshape(bf16[256,2048]{1,0:T(8,128)(2,1)} %convolution_convert_fusion) | data formatting | bytes 2097152 | tf_op jit(solution)/shard_map/reshape | solution.py:85
  129.0 2.2 %constant_dynamic-slice_fusion.3 = (bf16[256,1,512]{2,1,0:T(2,128)(2,1)S(1)}, bf16[256,1,512]{2,1,0:T(2,128)(2,1)S(1)}, bf16[256,1,512]{2,1,0:T(2,128)(2,1)S(1)}, bf16[256,1,512]{2,1,0:T(2,128)(2,1)S(1)}) fusion(bf16[256,4,512]{2,1,0:T(4,128)(2,1)S(1)} %reshape.305, s32[]{:T(128)S(6)} %select_n.140, s32[]{:T(128)S(6)} %select_n.144, s32[]{:T(128)S(6)} %select_n.142, ...), kind=kLoop, calls=%fused_computation.94 | loop fusion | bytes 2097168 | tf_op jit(solution)/shard_map/jit(dynamic_index_in_dim)/dynamic_slice | solution.py:86
  131.2 1.9 %collective-permute-start.3 = (bf16[256,512]{1,0:T(8,128)(2,1)S(1)}, bf16[256,512]{1,0:T(8,128)(2,1)S(1)}, u32[]{:S(2)}, u32[]{:S(2)}) collective-permute-start(bf16[256,512]{1,0:T(8,128)(2,1)S(1)} %bitcast.69), channel_id=1, source_target_pairs={{0,1},{1,2},{2,3},{3,0},{4,5},{5,6},{6,7},{7,4},{8,9},{9,10},{10,1... | collective-permute-start | bytes 786440 | tf_op jit(solution)/shard_map/ppermute | solution.py:90
  133.2 3.4 %collective-permute-start.4 = (bf16[256,512]{1,0:T(8,128)(2,1)S(1)}, bf16[256,512]{1,0:T(8,128)(2,1)S(1)}, u32[]{:S(2)}, u32[]{:S(2)}) collective-permute-start(bf16[256,512]{1,0:T(8,128)(2,1)S(1)} %bitcast.70), channel_id=1, source_target_pairs={{0,2},{1,3},{2,0},{3,1},{4,6},{5,7},{6,4},{7,5},{8,10},{9,11},{10,... | collective-permute-start | bytes 786440 | tf_op jit(solution)/shard_map/ppermute | solution.py:90
  136.6 3.1 %collective-permute-start.5 = (bf16[256,512]{1,0:T(8,128)(2,1)S(1)}, bf16[256,512]{1,0:T(8,128)(2,1)S(1)}, u32[]{:S(2)}, u32[]{:S(2)}) collective-permute-start(bf16[256,512]{1,0:T(8,128)(2,1)S(1)} %bitcast.71), channel_id=1, source_target_pairs={{0,3},{1,0},{2,1},{3,2},{4,7},{5,4},{6,5},{7,6},{8,11},{9,8},{10,9... | collective-permute-start | bytes 786440 | tf_op jit(solution)/shard_map/ppermute | solution.py:90
  140.9 7.3 %collective-permute-done.3 = bf16[256,512]{1,0:T(8,128)(2,1)S(1)} collective-permute-done((bf16[256,512]{1,0:T(8,128)(2,1)S(1)}, bf16[256,512]{1,0:T(8,128)(2,1)S(1)}, u32[]{:S(2)}, u32[]{:S(2)}) %collective-permute-start.3) | collective-permute-done | bytes 262176 | tf_op jit(solution)/shard_map/ppermute | solution.py:90
  148.2 2.3 %collective-permute-done.5 = bf16[256,512]{1,0:T(8,128)(2,1)S(1)} collective-permute-done((bf16[256,512]{1,0:T(8,128)(2,1)S(1)}, bf16[256,512]{1,0:T(8,128)(2,1)S(1)}, u32[]{:S(2)}, u32[]{:S(2)}) %collective-permute-start.5) | collective-permute-done | bytes 262176 | tf_op jit(solution)/shard_map/ppermute | solution.py:90
  (81 shorter events, 19.6 us)
Async XLA Ops:
  0.6 124.7 %copy-start = (bf16[512,2048]{1,0:T(8,128)(2,1)S(1)}, bf16[512,2048]{1,0:T(8,128)(2,1)}, u32[]{:S(2)}) copy-start(bf16[512,2048]{1,0:T(8,128)(2,1)} %param.15) | copy-start | bytes 6291460
  0.6 5.6 %copy-start.1 = (s32[256]{0:T(256)S(1)}, s32[256]{0:T(256)}, u32[]{:S(2)}) copy-start(s32[256]{0:T(256)} %param.16) | copy-start | bytes 3076
  6.2 3.7 %copy-start.2 = (bf16[256,512]{1,0:T(8,128)(2,1)S(1)}, bf16[256,512]{1,0:T(8,128)(2,1)}, u32[]{:S(2)}) copy-start(bf16[256,512]{1,0:T(8,128)(2,1)} %param.11) | copy-start | bytes 786436
  11.9 50.1 %copy-start.6 = (bf16[2048]{0:T(1024)(128)(2,1)S(1)}, bf16[2048]{0:T(1024)(128)(2,1)}, u32[]{:S(2)}) copy-start(bf16[2048]{0:T(1024)(128)(2,1)} %param.12) | copy-start | bytes 12292
  11.9 50.1 %copy-start.7 = (s32[128]{0:T(128)S(1)}, s32[128]{0:T(128)}, u32[]{:S(2)}) copy-start(s32[128]{0:T(128)} %param.18) | copy-start | bytes 1540
  13.3 39.0 %all-to-all-start = ((bf16[128,4,512]{2,1,0:T(4,128)(2,1)}), bf16[128,4,512]{2,1,0:T(4,128)(2,1)S(1)}, u32[]{:S(2)}, u32[]{:S(2)}) async-start(bf16[128,4,512]{2,1,0:T(4,128)(2,1)} %broadcast_select_fusion.1), calls=%async_computation | async-start | bytes 1048576 | tf_op jit(solution)/shard_map/all_to_all | solution.py:136
  52.8 27.2 %collective-permute-start = (bf16[512,512]{1,0:T(8,128)(2,1)S(1)}, bf16[512,512]{1,0:T(8,128)(2,1)S(1)}, u32[]{:S(2)}, u32[]{:S(2)}) collective-permute-start(bf16[512,512]{1,0:T(8,128)(2,1)S(1)} %bitcast.60), channel_id=1, source_target_pairs={{0,3},{1,0},{2,1},{3,2},{4,7},{5,4},{6,5},{7,6},{8,11},{9,8},{10,9... | collective-permute-start | bytes 1572872 | tf_op jit(solution)/shard_map/ppermute | solution.py:76
  58.9 21.0 %collective-permute-start.1 = (bf16[512,512]{1,0:T(8,128)(2,1)S(1)}, bf16[512,512]{1,0:T(8,128)(2,1)}, u32[]{:S(2)}, u32[]{:S(2)}) collective-permute-start(bf16[512,512]{1,0:T(8,128)(2,1)S(1)} %bitcast.61), channel_id=1, source_target_pairs={{0,2},{1,3},{2,0},{3,1},{4,6},{5,7},{6,4},{7,5},{8,10},{9,11},{10,... | collective-permute-start | bytes 1572872 | tf_op jit(solution)/shard_map/ppermute | solution.py:76
  62.2 25.2 %collective-permute-start.2 = (bf16[512,512]{1,0:T(8,128)(2,1)S(1)}, bf16[512,512]{1,0:T(8,128)(2,1)S(1)}, u32[]{:S(2)}, u32[]{:S(2)}) collective-permute-start(bf16[512,512]{1,0:T(8,128)(2,1)S(1)} %bitcast.62), channel_id=1, source_target_pairs={{0,1},{1,2},{2,3},{3,0},{4,5},{5,6},{6,7},{7,4},{8,9},{9,10},{10,1... | collective-permute-start | bytes 1572872 | tf_op jit(solution)/shard_map/ppermute | solution.py:76
  87.6 1.9 %copy-start.8 = (bf16[2048,512]{1,0:T(8,128)(2,1)S(1)}, bf16[2048,512]{1,0:T(8,128)(2,1)}, u32[]{:S(2)}) copy-start(bf16[2048,512]{1,0:T(8,128)(2,1)} %param.14) | copy-start | bytes 6291460
  89.5 2.7 %copy-start.9 = (bf16[2048,512]{1,0:T(8,128)(2,1)S(1)}, bf16[2048,512]{1,0:T(8,128)(2,1)}, u32[]{:S(2)}) copy-start(bf16[2048,512]{1,0:T(8,128)(2,1)} %param.13) | copy-start | bytes 6291460
  91.0 4.5 %copy-start.5 = (f32[512,512]{0,1:T(8,128)}, f32[512,512]{0,1:T(8,128)S(1)}, u32[]{:S(2)}) copy-start(f32[512,512]{0,1:T(8,128)S(1)} %fusion.8) | copy-start | bytes 3145732
  92.2 1.5 copy-start.4
  97.8 26.3 %all-to-all-start.1 = ((bf16[128,4,512]{2,1,0:T(4,128)(2,1)}), bf16[128,4,512]{2,1,0:T(4,128)(2,1)S(1)}, u32[]{:S(2)}, u32[]{:S(2)}) async-start(bf16[128,4,512]{2,1,0:T(4,128)(2,1)} %copy.55), calls=%async_computation.1 | async-start | bytes 1048576 | tf_op jit(solution)/shard_map/all_to_all | solution.py:176
  129.0 10.8 %copy-start.3 = (bf16[512,512]{1,0:T(8,128)(2,1)S(1)}, bf16[512,512]{1,0:T(8,128)(2,1)}, u32[]{:S(2)}) copy-start(bf16[512,512]{1,0:T(8,128)(2,1)} %copy.53) | copy-start | bytes 1572868
  131.2 17.0 %collective-permute-start.3 = (bf16[256,512]{1,0:T(8,128)(2,1)S(1)}, bf16[256,512]{1,0:T(8,128)(2,1)S(1)}, u32[]{:S(2)}, u32[]{:S(2)}) collective-permute-start(bf16[256,512]{1,0:T(8,128)(2,1)S(1)} %bitcast.69), channel_id=1, source_target_pairs={{0,1},{1,2},{2,3},{3,0},{4,5},{5,6},{6,7},{7,4},{8,9},{9,10},{10,1... | collective-permute-start | bytes 786440 | tf_op jit(solution)/shard_map/ppermute | solution.py:90
  133.2 15.0 %collective-permute-start.4 = (bf16[256,512]{1,0:T(8,128)(2,1)S(1)}, bf16[256,512]{1,0:T(8,128)(2,1)S(1)}, u32[]{:S(2)}, u32[]{:S(2)}) collective-permute-start(bf16[256,512]{1,0:T(8,128)(2,1)S(1)} %bitcast.70), channel_id=1, source_target_pairs={{0,2},{1,3},{2,0},{3,1},{4,6},{5,7},{6,4},{7,5},{8,10},{9,11},{10,... | collective-permute-start | bytes 786440 | tf_op jit(solution)/shard_map/ppermute | solution.py:90
  136.6 13.9 %collective-permute-start.5 = (bf16[256,512]{1,0:T(8,128)(2,1)S(1)}, bf16[256,512]{1,0:T(8,128)(2,1)S(1)}, u32[]{:S(2)}, u32[]{:S(2)}) collective-permute-start(bf16[256,512]{1,0:T(8,128)(2,1)S(1)} %bitcast.71), channel_id=1, source_target_pairs={{0,3},{1,0},{2,1},{3,2},{4,7},{5,4},{6,5},{7,6},{8,11},{9,8},{10,9... | collective-permute-start | bytes 786440 | tf_op jit(solution)/shard_map/ppermute | solution.py:90

commit v3 on v0

--- a/solution.py
+++ b/solution.py
@@ -65,6 +65,63 @@
 def from_request(request_rows, shift_by, source_count):
     shaped = request_rows.reshape(-1, source_count, request_rows.shape[1])
     return jnp.roll(jnp.swapaxes(shaped, 0, 1), shift_by, axis=0)
+
+
+def ring_blocks(narrow, axis_name):
+    count = lax.axis_size(axis_name)
+    blocks = [narrow]
+    for shift in range(1, count):
+        perm = [(index, (index - shift) % count) for index in range(count)]
+        blocks.append(lax.ppermute(narrow, axis_name, perm))
+    return blocks
+
+
+def project_blocks(blocks, gain, query_weight, keyval_weight, axis_name):
+    count = lax.axis_size(axis_name)
+    position = lax.axis_index(axis_name)
+    width = blocks[0].shape[1]
+    widened = [block.astype(jnp.float32) for block in blocks]
+    squares = sum(jnp.sum(block * block, axis=-1, keepdims=True) for block in widened)
+    inverse_rms = lax.rsqrt(squares / (width * count) + EPSILON)
+    queries = None
+    keyvals = None
+    for shift, block in enumerate(widened):
+        first = ((position + shift) % count) * width
+        block_gain = lax.dynamic_slice_in_dim(gain, first, width, 0).astype(jnp.float32)
+        normed = (block * inverse_rms * block_gain).astype(jnp.bfloat16)
+        query_part = jnp.dot(
+            normed,
+            lax.dynamic_slice_in_dim(query_weight, first, width, 0),
+            preferred_element_type=jnp.float32,
+        )
+        keyval_part = jnp.dot(
+            normed,
+            lax.dynamic_slice_in_dim(keyval_weight, first, width, 0),
+            preferred_element_type=jnp.float32,
+        )
+        queries = query_part if queries is None else queries + query_part
+        keyvals = keyval_part if keyvals is None else keyvals + keyval_part
+    return queries, keyvals
+
+
+def ring_output(local_attention, output_weight, axis_name):
+    count = lax.axis_size(axis_name)
+    position = lax.axis_index(axis_name)
+    width = output_weight.shape[1] // count
+    total = None
+    for shift in range(count):
+        first = ((position + shift) % count) * width
+        part = jnp.dot(
+            local_attention,
+            lax.dynamic_slice_in_dim(output_weight, first, width, 1),
+            preferred_element_type=jnp.float32,
+        ).astype(jnp.bfloat16)
+        if shift == 0:
+            total = part.astype(jnp.float32)
+        else:
+            perm = [(index, (index + shift) % count) for index in range(count)]
+            total = total + lax.ppermute(part, axis_name, perm).astype(jnp.float32)
+    return total.astype(jnp.bfloat16)
 
 
 def body(
@@ -88,18 +145,31 @@
     starts = jnp.cumsum(request_lengths) - request_lengths
     first_row = jnp.maximum((starts - source_pos + source_count - 1) // source_count, 0)
     owner_match = request_owner[None, :] == request_ids[:, None]
-    owned_by = jnp.sum(jnp.where(owner_match, request_ids[None, :], 0), axis=1)
     send_first = jnp.sum(jnp.where(owner_match, first_row[None, :], 0), axis=1)
+    send_start = jnp.sum(jnp.where(owner_match, starts[None, :], 0), axis=1)
+    send_length = jnp.sum(jnp.where(owner_match, request_lengths[None, :], 0), axis=1)
     row_index = send_first[:, None] + jnp.arange(capacity, dtype=jnp.int32)[None, :]
-    safe_index = jnp.minimum(row_index, local_rows - 1)
-    live_send = (row_index < local_rows) & (segment_ids[safe_index] == owned_by[:, None])
+    stream_pos = row_index * source_count + source_pos
+    live_send = (
+        (row_index < local_rows)
+        & (stream_pos >= send_start[:, None])
+        & (stream_pos < (send_start + send_length)[:, None])
+    )
+    local_ids = jnp.arange(local_rows, dtype=jnp.int32)
+    select = (
+        (row_index.reshape(-1)[:, None] == local_ids[None, :]) & live_send.reshape(-1)[:, None]
+    ).astype(jnp.bfloat16)
     owned_request = jnp.sum(jnp.where(request_owner == source_pos, request_ids, 0))
     own_match = request_ids == owned_request
     own_start = jnp.sum(jnp.where(own_match, starts, 0))
     own_length = jnp.sum(jnp.where(own_match, request_lengths, 0))
     own_slot = jnp.sum(jnp.where(own_match, cache_slots, 0))
     shift_by = own_start % source_count
-    picked = jnp.where(live_send[:, :, None], hidden_in[safe_index], jnp.zeros((), jnp.bfloat16))
+    picked = (
+        jnp.dot(select, hidden_in, preferred_element_type=jnp.float32)
+        .astype(jnp.bfloat16)
+        .reshape(source_count, capacity, hidden_in.shape[1])
+    )
     head_count = query_weight.shape[1] // HD
     per_group = HEADS // KV_HEADS
     block_count = keyval_weight.shape[1] // HD
@@ -117,10 +187,9 @@
             tiled=True,
         )
         narrow_rows = to_request(arrived, shift_by)
-        full_rows = lax.all_gather(narrow_rows, "tensor", axis=1, tiled=True)
-        normed = normalize(full_rows, norm_gain)
-        queries = jnp.dot(normed, query_weight, preferred_element_type=jnp.float32)
-        keyvals = jnp.dot(normed, keyval_weight, preferred_element_type=jnp.float32)
+        queries, keyvals = project_blocks(
+            ring_blocks(narrow_rows, "tensor"), norm_gain, query_weight, keyval_weight, "tensor"
+        )
         rotated_query = rotate_rows(queries, HD, chunk_first).astype(jnp.bfloat16)
         own_blocks = []
         for block_index in range(block_count):
@@ -152,18 +221,11 @@
             lax.all_to_all(outgoing, "seq", split_axis=0, concat_axis=0, tiled=True)
         )
     returned = jnp.concatenate(returned_chunks, axis=1)
-    segment_match = segment_ids[:, None] == request_ids[None, :]
-    row_owner = jnp.sum(jnp.where(segment_match, request_owner[None, :], 0), axis=1)
-    row_first = jnp.sum(jnp.where(segment_match, first_row[None, :], 0), axis=1)
-    slot_pos = jnp.arange(local_rows, dtype=jnp.int32) - row_first
-    usable = (segment_ids >= 0) & (slot_pos >= 0) & (slot_pos < capacity)
-    flat_index = row_owner * capacity + jnp.clip(slot_pos, 0, capacity - 1)
     flattened = returned.reshape(-1, returned.shape[2])
-    local_attention = jnp.where(usable[:, None], flattened[flat_index], jnp.zeros((), returned.dtype))
-    partial_sum = jnp.dot(local_attention, output_weight, preferred_element_type=jnp.float32)
-    attended = lax.psum_scatter(
-        partial_sum.astype(jnp.bfloat16), "tensor", scatter_dimension=1, tiled=True
-    )
+    local_attention = lax.dot_general(
+        select, flattened, (((0,), (0,)), ((), ())), preferred_element_type=jnp.float32
+    ).astype(jnp.bfloat16)
+    attended = ring_output(local_attention, output_weight, "tensor")
     all_cached = jnp.concatenate(cached_chunks, axis=0)
     slot_ids = jnp.arange(SLOTS_DEV, dtype=jnp.int32)
     cache_table = jnp.where(

time: 166 us -> 148 us (0.89)
  waiting for transfers between devices: 79.4 us -> 59.8 us
  between operations: 16.6 us -> 3.25 us
  starting transfers between devices: 33.1 us -> 44.6 us
  matrix products: 7.85 us -> 15.4 us
  local copies, waits for them, and re-layouts: 10.9 us -> 6.4 us
    ppermute x0 -> x6, waiting for transfers between devices: none -> 27.3 us  [the longest x3 16.5 us: ring_blocks(): blocks.append(lax.ppermute(narrow, axis_name, perm))]
    all_gather x1 -> x0, waiting for transfers between devices: 27.1 us -> none  [body(): full_rows = lax.all_gather(narrow_rows, 'tensor', axis=1, tiled=True)]
    ppermute x0 -> x6, starting transfers between devices: none -> 20.3 us  [the longest x3 10.7 us: ring_blocks(): blocks.append(lax.ppermute(narrow, axis_name, perm))]
    reduce_scatter x1 -> x0, waiting for transfers between devices: 13.9 us -> none  [body(): lax.psum_scatter(partial_sum.astype(jnp.bfloat16), 'tensor', scatter_dime...]
    all_to_all x1, starting transfers between devices: 14.3 us -> 5.84 us  [body(): lax.all_to_all(outgoing, 'seq', split_axis=0, concat_axis=0, tiled=True)]
    dot_general x3 -> x14, matrix products: 6.35 us -> 13.9 us  [the longest x4 4.06 us: ring_output(): jnp.dot(local_attention, lax.dynamic_slice_in_dim(output_weight, first, w...]
    gather x5 -> x0, local copies, waits for them, and re-layouts: 6.87 us -> none  [the longest x2 3.62 us: body(): segment_ids[safe_index] == owned_by[:, None]]
    all_to_all x1, waiting for transfers between devices: 20.2 us -> 15.4 us  [body(): lax.all_to_all(outgoing, 'seq', split_axis=0, concat_axis=0, tiled=True)]
  transfers between devices with their start and end apart: 4 -> 8, of which waited for: 4 -> 6; matrix products, arithmetic and copies ran while one was open for 4% -> 7% of each run, Pallas kernels for 0% -> 0%
where the time goes in v3:
time: 148 us; the launch traced here: 147 us
  waiting for transfers between devices  59.8 us (40%)
  starting transfers between devices  44.6 us (30%)
  other arithmetic  17.3 us (12%)
  matrix products  15.4 us (10%)
  local copies, waits for them, and re-layouts  6.4 us (4%)
  between operations  3.25 us (2%)
    all_to_all x1, starting transfers between devices, body(): lax.all_to_all(picked[:, chunk * chunk_slots:(chunk + 1) * chunk_slots],...  18.4 us
    all_to_all x1, waiting for transfers between devices, body(): lax.all_to_all(picked[:, chunk * chunk_slots:(chunk + 1) * chunk_slots],...  17.1 us
    ppermute x3, waiting for transfers between devices, ring_blocks(): blocks.append(lax.ppermute(narrow, axis_name, perm))  16.5 us
    all_to_all x1, waiting for transfers between devices, body(): lax.all_to_all(outgoing, 'seq', split_axis=0, concat_axis=0, tiled=True)  15.4 us
    ppermute x3, waiting for transfers between devices, ring_output(): total = total + lax.ppermute(part, axis_name, perm).astype(jnp.float32)  10.8 us
    ppermute x3, starting transfers between devices, ring_blocks(): blocks.append(lax.ppermute(narrow, axis_name, perm))  10.7 us
    ppermute x3, starting transfers between devices, ring_output(): total = total + lax.ppermute(part, axis_name, perm).astype(jnp.float32)  9.62 us
    all_to_all x1, starting transfers between devices, body(): lax.all_to_all(outgoing, 'seq', split_axis=0, concat_axis=0, tiled=True)  5.84 us
  transfers between devices with their start and end apart: 8, of which 6 were waited for; matrix products, arithmetic and copies ran while one was open for 7% of the time, Pallas kernels for 0%

profile of v3, /device:TPU:1, one launch (start us, length us, event | category | flops | bytes accessed | tf_op | source)
XLA Modules:
  0.0 146.7 jit_solution(1696610583896422378)
XLA Ops:
  3.1 2.0 %fusion.74 = (s32[128]{0:T(128)S(1)}, s32[128]{0:T(128)S(1)}, s32[]{:T(128)}) fusion(s32[]{:T(128)S(6)} %axis_index.27, s32[128]{0:T(128)S(1)} %reduce.1, s32[128]{0:T(128)} %param.16, s32[]{:T(128)} %fusion.73), kind=kLoop, calls=%fused_computation.137 | loop fusion | flops 2815 | bytes 2060 | tf_op jit(solution)/shard_map/max | solution.py:146
  6.6 1.3 convolution_convert_fusion
  8.8 18.4 %all-to-all-start = ((bf16[128,4,512]{2,1,0:T(4,128)(2,1)}), bf16[128,4,512]{2,1,0:T(4,128)(2,1)S(1)}, u32[]{:S(2)}, u32[]{:S(2)}) async-start(bf16[128,4,512]{2,1,0:T(4,128)(2,1)} %reshape.252), calls=%async_computation | async-start | bytes 1048576 | tf_op jit(solution)/shard_map/all_to_all | solution.py:182
  27.3 1.4 select_reduce_fusion.4
  30.7 17.1 %all-to-all-done = bf16[128,4,512]{2,1,0:T(4,128)(2,1)S(1)} async-done(((bf16[128,4,512]{2,1,0:T(4,128)(2,1)}), bf16[128,4,512]{2,1,0:T(4,128)(2,1)S(1)}, u32[]{:S(2)}, u32[]{:S(2)}) %all-to-all-start) | async-done | bytes 524320 | tf_op jit(solution)/shard_map/all_to_all | solution.py:182
  48.4 3.1 %collective-permute-start.2 = (bf16[512,512]{1,0:T(8,128)(2,1)S(1)}, bf16[512,512]{1,0:T(8,128)(2,1)S(1)}, u32[]{:S(2)}, u32[]{:S(2)}) collective-permute-start(bf16[512,512]{1,0:T(8,128)(2,1)S(1)} %bitcast.38), channel_id=1, source_target_pairs={{0,1},{1,2},{2,3},{3,0},{4,5},{5,6},{6,7},{7,4},{8,9},{9,10},{10,1... | collective-permute-start | bytes 1572872 | tf_op jit(solution)/shard_map/ppermute | solution.py:75
  51.6 4.4 %collective-permute-start.1 = (bf16[512,512]{1,0:T(8,128)(2,1)S(1)}, bf16[512,512]{1,0:T(8,128)(2,1)}, u32[]{:S(2)}, u32[]{:S(2)}) collective-permute-start(bf16[512,512]{1,0:T(8,128)(2,1)S(1)} %bitcast.39), channel_id=1, source_target_pairs={{0,2},{1,3},{2,0},{3,1},{4,6},{5,7},{6,4},{7,5},{8,10},{9,11},{10,... | collective-permute-start | bytes 1572872 | tf_op jit(solution)/shard_map/ppermute | solution.py:75
  56.8 3.2 %collective-permute-start = (bf16[512,512]{1,0:T(8,128)(2,1)S(1)}, bf16[512,512]{1,0:T(8,128)(2,1)S(1)}, u32[]{:S(2)}, u32[]{:S(2)}) collective-permute-start(bf16[512,512]{1,0:T(8,128)(2,1)S(1)} %bitcast.40), channel_id=1, source_target_pairs={{0,3},{1,0},{2,1},{3,2},{4,7},{5,4},{6,5},{7,6},{8,11},{9,8},{10,9... | collective-permute-start | bytes 1572872 | tf_op jit(solution)/shard_map/ppermute | solution.py:75
  61.1 4.4 %collective-permute-done.2 = bf16[512,512]{1,0:T(8,128)(2,1)S(1)} collective-permute-done((bf16[512,512]{1,0:T(8,128)(2,1)S(1)}, bf16[512,512]{1,0:T(8,128)(2,1)S(1)}, u32[]{:S(2)}, u32[]{:S(2)}) %collective-permute-start.2) | collective-permute-done | bytes 524320 | tf_op jit(solution)/shard_map/ppermute | solution.py:75
  65.6 12.1 %collective-permute-done.1 = bf16[512,512]{1,0:T(8,128)(2,1)} collective-permute-done((bf16[512,512]{1,0:T(8,128)(2,1)S(1)}, bf16[512,512]{1,0:T(8,128)(2,1)}, u32[]{:S(2)}, u32[]{:S(2)}) %collective-permute-start.1) | collective-permute-done | bytes 524320 | tf_op jit(solution)/shard_map/ppermute | solution.py:75
  80.4 1.6 %convolution_add_fusion.1 = f32[512,512]{0,1:T(8,128)S(1)} fusion(f32[512,512]{0,1:T(8,128)S(1)} %convolution_add_fusion.2, bf16[2048,512]{1,0:T(8,128)(2,1)S(1)} %copy-done, s32[]{:T(128)S(6)} %select_n.116, bf16[512,512]{1,0:T(8,128)(2,1)} %collective-permute-done.1, f32[512]{0:T(512)S(1)} %get-tuple-element.17, f32[512]{0:T(512)S(1)} %fusion.72), kind=kOutput, calls=%fused_computation.1 | convolution fusion | flops 269746176 | bytes 3149828 | tf_op jit(solution)/shard_map/dot_general | solution.py:97
  85.1 1.6 %convolution_add_fusion.4 = f32[512,512]{0,1:T(8,128)S(1)} fusion(f32[512,512]{0,1:T(8,128)S(1)} %convolution_add_fusion.5, bf16[2048,512]{1,0:T(8,128)(2,1)S(1)} %copy-done.2, s32[]{:T(128)S(6)} %select_n.116, bf16[512,512]{1,0:T(8,128)(2,1)} %collective-permute-done.1, f32[512]{0:T(512)S(1)} %get-tuple-element.17, f32[512]{0:T(512)S(1)} %fusion.72), kind=kOutput, calls=%fused_computation.4 | convolution fusion | flops 269746176 | bytes 3149828 | tf_op jit(solution)/shard_map/dot_general | solution.py:92
  90.2 1.7 %fusion.15 = bf16[128,4,512]{2,1,0:T(4,128)(2,1)} fusion(s32[]{:T(128)S(6)} %select_n.128, bf16[128,4,512]{2,1,0:T(4,128)(2,1)S(1)} %bitcast.44), kind=kLoop, calls=%fused_computation.49 | loop fusion | flops 262144 | bytes 1048580 | tf_op jit(solution)/shard_map/jit(_roll_dynamic)/concatenate | solution.py:67
  91.9 5.8 %all-to-all-start.1 = ((bf16[128,4,512]{2,1,0:T(4,128)(2,1)}), bf16[128,4,512]{2,1,0:T(4,128)(2,1)S(1)}, u32[]{:S(2)}, u32[]{:S(2)}) async-start(bf16[128,4,512]{2,1,0:T(4,128)(2,1)} %fusion.15), calls=%async_computation.1 | async-start | bytes 1048576 | tf_op jit(solution)/shard_map/all_to_all | solution.py:221
  97.8 1.4 select_reduce_fusion.3
  103.0 15.4 %all-to-all-done.1 = bf16[128,4,512]{2,1,0:T(4,128)(2,1)S(1)} async-done(((bf16[128,4,512]{2,1,0:T(4,128)(2,1)}), bf16[128,4,512]{2,1,0:T(4,128)(2,1)S(1)}, u32[]{:S(2)}, u32[]{:S(2)}) %all-to-all-start.1) | async-done | bytes 524320 | tf_op jit(solution)/shard_map/all_to_all | solution.py:221
  119.4 1.7 %convolution_convert_fusion.7 = bf16[256,512]{1,0:T(8,128)(2,1)S(1)} fusion(bf16[512,512]{1,0:T(8,128)(2,1)} %reshape.257, s32[512]{0:T(512)S(1)} %add.181, pred[512]{0:T(512)(128)(4,1)S(1)} %compare_and_fusion), kind=kOutput, calls=%fused_computation.24 | convolution fusion | flops 134610944 | bytes 788992 | tf_op jit(solution)/shard_map/dot_general | solution.py:225
  121.1 1.3 convolution_convert_fusion.3
  122.4 1.3 convolution_convert_fusion.4
  124.1 4.2 %collective-permute-start.5 = (bf16[256,512]{1,0:T(8,128)(2,1)S(1)}, bf16[256,512]{1,0:T(8,128)(2,1)S(1)}, u32[]{:S(2)}, u32[]{:S(2)}) collective-permute-start(bf16[256,512]{1,0:T(8,128)(2,1)S(1)} %convolution_convert_fusion.3), channel_id=1, source_target_pairs={{0,3},{1,0},{2,1},{3,2},{4,7},{5,4},{6,5},{7,6},{8,11},{9,8},{10,9... | collective-permute-start | bytes 786440 | tf_op jit(solution)/shard_map/ppermute | solution.py:123
  128.3 3.5 %collective-permute-start.4 = (bf16[256,512]{1,0:T(8,128)(2,1)S(1)}, bf16[256,512]{1,0:T(8,128)(2,1)S(1)}, u32[]{:S(2)}, u32[]{:S(2)}) collective-permute-start(bf16[256,512]{1,0:T(8,128)(2,1)S(1)} %convolution_convert_fusion.4), channel_id=1, source_target_pairs={{0,2},{1,3},{2,0},{3,1},{4,6},{5,7},{6,4},{7,5},{8,10},{9,11},{10,... | collective-permute-start | bytes 786440 | tf_op jit(solution)/shard_map/ppermute | solution.py:123
  131.8 1.9 %collective-permute-start.3 = (bf16[256,512]{1,0:T(8,128)(2,1)S(1)}, bf16[256,512]{1,0:T(8,128)(2,1)S(1)}, u32[]{:S(2)}, u32[]{:S(2)}) collective-permute-start(bf16[256,512]{1,0:T(8,128)(2,1)S(1)} %convolution_convert_fusion.5), channel_id=1, source_target_pairs={{0,1},{1,2},{2,3},{3,0},{4,5},{5,6},{6,7},{7,4},{8,9},{9,10},{10,1... | collective-permute-start | bytes 786440 | tf_op jit(solution)/shard_map/ppermute | solution.py:123
  134.9 5.0 %collective-permute-done.5 = bf16[256,512]{1,0:T(8,128)(2,1)S(1)} collective-permute-done((bf16[256,512]{1,0:T(8,128)(2,1)S(1)}, bf16[256,512]{1,0:T(8,128)(2,1)S(1)}, u32[]{:S(2)}, u32[]{:S(2)}) %collective-permute-start.5) | collective-permute-done | bytes 262176 | tf_op jit(solution)/shard_map/ppermute | solution.py:123
  139.9 5.8 %collective-permute-done.3 = bf16[256,512]{1,0:T(8,128)(2,1)S(1)} collective-permute-done((bf16[256,512]{1,0:T(8,128)(2,1)S(1)}, bf16[256,512]{1,0:T(8,128)(2,1)S(1)}, u32[]{:S(2)}, u32[]{:S(2)}) %collective-permute-start.3) | collective-permute-done | bytes 262176 | tf_op jit(solution)/shard_map/ppermute | solution.py:123
  (67 shorter events, 23.7 us)
Async XLA Ops:
  0.6 78.5 %copy-start = (bf16[2048,512]{1,0:T(8,128)(2,1)S(1)}, bf16[2048,512]{1,0:T(8,128)(2,1)}, u32[]{:S(2)}) copy-start(bf16[2048,512]{1,0:T(8,128)(2,1)} %param.14) | copy-start | bytes 6291460
  7.9 48.8 %copy-start.4 = (bf16[2048]{0:T(1024)(128)(2,1)S(1)}, bf16[2048]{0:T(1024)(128)(2,1)}, u32[]{:S(2)}) copy-start(bf16[2048]{0:T(1024)(128)(2,1)} %param.12) | copy-start | bytes 12292
  8.8 39.0 %all-to-all-start = ((bf16[128,4,512]{2,1,0:T(4,128)(2,1)}), bf16[128,4,512]{2,1,0:T(4,128)(2,1)S(1)}, u32[]{:S(2)}, u32[]{:S(2)}) async-start(bf16[128,4,512]{2,1,0:T(4,128)(2,1)} %reshape.252), calls=%async_computation | async-start | bytes 1048576 | tf_op jit(solution)/shard_map/all_to_all | solution.py:182
  48.4 17.0 %collective-permute-start.2 = (bf16[512,512]{1,0:T(8,128)(2,1)S(1)}, bf16[512,512]{1,0:T(8,128)(2,1)S(1)}, u32[]{:S(2)}, u32[]{:S(2)}) collective-permute-start(bf16[512,512]{1,0:T(8,128)(2,1)S(1)} %bitcast.38), channel_id=1, source_target_pairs={{0,1},{1,2},{2,3},{3,0},{4,5},{5,6},{6,7},{7,4},{8,9},{9,10},{10,1... | collective-permute-start | bytes 1572872 | tf_op jit(solution)/shard_map/ppermute | solution.py:75
  51.6 26.2 %collective-permute-start.1 = (bf16[512,512]{1,0:T(8,128)(2,1)S(1)}, bf16[512,512]{1,0:T(8,128)(2,1)}, u32[]{:S(2)}, u32[]{:S(2)}) collective-permute-start(bf16[512,512]{1,0:T(8,128)(2,1)S(1)} %bitcast.39), channel_id=1, source_target_pairs={{0,2},{1,3},{2,0},{3,1},{4,6},{5,7},{6,4},{7,5},{8,10},{9,11},{10,... | collective-permute-start | bytes 1572872 | tf_op jit(solution)/shard_map/ppermute | solution.py:75
  56.8 22.1 %collective-permute-start = (bf16[512,512]{1,0:T(8,128)(2,1)S(1)}, bf16[512,512]{1,0:T(8,128)(2,1)S(1)}, u32[]{:S(2)}, u32[]{:S(2)}) collective-permute-start(bf16[512,512]{1,0:T(8,128)(2,1)S(1)} %bitcast.40), channel_id=1, source_target_pairs={{0,3},{1,0},{2,1},{3,2},{4,7},{5,4},{6,5},{7,6},{8,11},{9,8},{10,9... | collective-permute-start | bytes 1572872 | tf_op jit(solution)/shard_map/ppermute | solution.py:75
  82.0 1.8 %copy-start.2 = (bf16[2048,512]{1,0:T(8,128)(2,1)S(1)}, bf16[2048,512]{1,0:T(8,128)(2,1)}, u32[]{:S(2)}) copy-start(bf16[2048,512]{1,0:T(8,128)(2,1)} %param.13) | copy-start | bytes 6291460
  82.6 6.5 %copy-start.1 = (f32[512,512]{0,1:T(8,128)}, f32[512,512]{0,1:T(8,128)S(1)}, u32[]{:S(2)}) copy-start(f32[512,512]{0,1:T(8,128)S(1)} %convolution_add_fusion) | copy-start | bytes 3145732
  89.5 8.2 %copy-start.5 = (s32[128]{0:T(128)S(1)}, s32[128]{0:T(128)}, u32[]{:S(2)}) copy-start(s32[128]{0:T(128)} %param.18) | copy-start | bytes 1540
  91.9 26.5 %all-to-all-start.1 = ((bf16[128,4,512]{2,1,0:T(4,128)(2,1)}), bf16[128,4,512]{2,1,0:T(4,128)(2,1)S(1)}, u32[]{:S(2)}, u32[]{:S(2)}) async-start(bf16[128,4,512]{2,1,0:T(4,128)(2,1)} %fusion.15), calls=%async_computation.1 | async-start | bytes 1048576 | tf_op jit(solution)/shard_map/all_to_all | solution.py:221
  119.4 4.4 %copy-start.3 = (bf16[512,2048]{1,0:T(8,128)(2,1)S(1)}, bf16[512,2048]{1,0:T(8,128)(2,1)}, u32[]{:S(2)}) copy-start(bf16[512,2048]{1,0:T(8,128)(2,1)} %param.15) | copy-start | bytes 6291460
  124.1 15.8 %collective-permute-start.5 = (bf16[256,512]{1,0:T(8,128)(2,1)S(1)}, bf16[256,512]{1,0:T(8,128)(2,1)S(1)}, u32[]{:S(2)}, u32[]{:S(2)}) collective-permute-start(bf16[256,512]{1,0:T(8,128)(2,1)S(1)} %convolution_convert_fusion.3), channel_id=1, source_target_pairs={{0,3},{1,0},{2,1},{3,2},{4,7},{5,4},{6,5},{7,6},{8,11},{9,8},{10,9... | collective-permute-start | bytes 786440 | tf_op jit(solution)/shard_map/ppermute | solution.py:123
  128.3 11.5 %collective-permute-start.4 = (bf16[256,512]{1,0:T(8,128)(2,1)S(1)}, bf16[256,512]{1,0:T(8,128)(2,1)S(1)}, u32[]{:S(2)}, u32[]{:S(2)}) collective-permute-start(bf16[256,512]{1,0:T(8,128)(2,1)S(1)} %convolution_convert_fusion.4), channel_id=1, source_target_pairs={{0,2},{1,3},{2,0},{3,1},{4,6},{5,7},{6,4},{7,5},{8,10},{9,11},{10,... | collective-permute-start | bytes 786440 | tf_op jit(solution)/shard_map/ppermute | solution.py:123
  131.8 13.8 %collective-permute-start.3 = (bf16[256,512]{1,0:T(8,128)(2,1)S(1)}, bf16[256,512]{1,0:T(8,128)(2,1)S(1)}, u32[]{:S(2)}, u32[]{:S(2)}) collective-permute-start(bf16[256,512]{1,0:T(8,128)(2,1)S(1)} %convolution_convert_fusion.5), channel_id=1, source_target_pairs={{0,1},{1,2},{2,3},{3,0},{4,5},{5,6},{6,7},{7,4},{8,9},{9,10},{10,1... | collective-permute-start | bytes 786440 | tf_op jit(solution)/shard_map/ppermute | solution.py:123

commit v4 on v3

--- a/solution.py
+++ b/solution.py
@@ -15,12 +15,12 @@
 CHUNKS = 1
 
 
-def rotate_rows(values, head_size, first_pos):
+def rotate_rows(values, head_size, row_pos):
     row_count = values.shape[0]
     shaped = values.reshape(row_count, -1, head_size)
     half_size = head_size // 2
     frequency = ROPE_BASE ** (jnp.arange(half_size, dtype=jnp.float32) * (-2.0 / head_size))
-    positions = (first_pos + jnp.arange(row_count, dtype=jnp.int32)).astype(jnp.float32)
+    positions = row_pos.astype(jnp.float32)
     angles = positions[:, None] * frequency[None, :]
     cosine_table = jnp.cos(angles)[:, None, :]
     sine_table = jnp.sin(angles)[:, None, :]
@@ -42,14 +42,11 @@
     return (widened * inverse_rms * gain.astype(jnp.float32)).astype(jnp.bfloat16)
 
 
-def attend(query_block, start_row, key_rows, value_rows, length):
-    row_count = query_block.shape[0]
+def attend(query_block, query_pos, key_rows, key_pos, value_rows, length):
     scores = jnp.dot(query_block, key_rows.T, preferred_element_type=jnp.float32) * key_rows.shape[
         1
     ] ** (-0.5)
-    query_pos = start_row + jnp.arange(row_count, dtype=jnp.int32)[:, None]
-    key_pos = jnp.arange(key_rows.shape[0], dtype=jnp.int32)[None, :]
-    allowed = (key_pos <= query_pos) & (key_pos < length)
+    allowed = (key_pos[None, :] <= query_pos[:, None]) & (key_pos[None, :] < length)
     scores = jnp.where(allowed, scores, -jnp.inf)
     row_top = jnp.max(scores, axis=-1, keepdims=True)
     powered = jnp.exp(scores - row_top)
@@ -157,7 +154,7 @@
     )
     local_ids = jnp.arange(local_rows, dtype=jnp.int32)
     select = (
-        (row_index.reshape(-1)[:, None] == local_ids[None, :]) & live_send.reshape(-1)[:, None]
+        (row_index.T.reshape(-1)[:, None] == local_ids[None, :]) & live_send.T.reshape(-1)[:, None]
     ).astype(jnp.bfloat16)
     owned_request = jnp.sum(jnp.where(request_owner == source_pos, request_ids, 0))
     own_match = request_ids == owned_request
@@ -168,8 +165,13 @@
     picked = (
         jnp.dot(select, hidden_in, preferred_element_type=jnp.float32)
         .astype(jnp.bfloat16)
-        .reshape(source_count, capacity, hidden_in.shape[1])
-    )
+        .reshape(capacity, source_count, hidden_in.shape[1])
+    )
+    source_ids = jnp.arange(source_count, dtype=jnp.int32)
+    slot_ids_all = jnp.arange(capacity, dtype=jnp.int32)
+    row_pos = (
+        slot_ids_all[:, None] * source_count + (source_ids[None, :] - shift_by) % source_count
+    ).reshape(-1)
     head_count = query_weight.shape[1] // HD
     per_group = HEADS // KV_HEADS
     block_count = keyval_weight.shape[1] // HD
@@ -180,22 +182,23 @@
     for chunk in range(CHUNKS):
         chunk_first = chunk * chunk_rows
         arrived = lax.all_to_all(
-            picked[:, chunk * chunk_slots : (chunk + 1) * chunk_slots],
+            picked[chunk * chunk_slots : (chunk + 1) * chunk_slots],
             "seq",
-            split_axis=0,
-            concat_axis=0,
+            split_axis=1,
+            concat_axis=1,
             tiled=True,
         )
-        narrow_rows = to_request(arrived, shift_by)
+        narrow_rows = arrived.reshape(-1, arrived.shape[2])
+        chunk_pos = row_pos[chunk * chunk_rows : (chunk + 1) * chunk_rows]
         queries, keyvals = project_blocks(
             ring_blocks(narrow_rows, "tensor"), norm_gain, query_weight, keyval_weight, "tensor"
         )
-        rotated_query = rotate_rows(queries, HD, chunk_first).astype(jnp.bfloat16)
+        rotated_query = rotate_rows(queries, HD, chunk_pos).astype(jnp.bfloat16)
         own_blocks = []
         for block_index in range(block_count):
             plain_block = keyvals[:, block_index * HD : (block_index + 1) * HD]
             if block_index % 2 == 0:
-                own_blocks.append(rotate_rows(plain_block, HD, chunk_first).astype(jnp.bfloat16))
+                own_blocks.append(rotate_rows(plain_block, HD, chunk_pos).astype(jnp.bfloat16))
             else:
                 own_blocks.append(plain_block.astype(jnp.bfloat16))
         own_cached = jnp.concatenate(own_blocks, axis=1)
@@ -209,24 +212,28 @@
             head_outputs.append(
                 attend(
                     rotated_query[:, head_index * HD : (head_index + 1) * HD],
-                    chunk_first,
+                    chunk_pos,
                     key_rows,
+                    row_pos[: (chunk + 1) * chunk_rows],
                     value_rows,
                     own_length,
                 )
             )
         attention_rows = jnp.concatenate(head_outputs, axis=1)
-        outgoing = from_request(attention_rows, shift_by, source_count)
+        outgoing = attention_rows.reshape(chunk_slots, source_count, attention_rows.shape[1])
         returned_chunks.append(
-            lax.all_to_all(outgoing, "seq", split_axis=0, concat_axis=0, tiled=True)
-        )
-    returned = jnp.concatenate(returned_chunks, axis=1)
+            lax.all_to_all(outgoing, "seq", split_axis=1, concat_axis=1, tiled=True)
+        )
+    returned = jnp.concatenate(returned_chunks, axis=0)
     flattened = returned.reshape(-1, returned.shape[2])
     local_attention = lax.dot_general(
         select, flattened, (((0,), (0,)), ((), ())), preferred_element_type=jnp.float32
     ).astype(jnp.bfloat16)
     attended = ring_output(local_attention, output_weight, "tensor")
-    all_cached = jnp.concatenate(cached_chunks, axis=0)
+    all_cached = to_request(
+        jnp.swapaxes(jnp.concatenate(cached_chunks, axis=0).reshape(capacity, source_count, -1), 0, 1),
+        shift_by,
+    )
     slot_ids = jnp.arange(SLOTS_DEV, dtype=jnp.int32)
     cache_table = jnp.where(
         (slot_ids == own_slot)[:, None, None], all_cached[None], jnp.zeros((), jnp.bfloat16)

time: 148 us -> 153 us (1.034)
  other arithmetic: 17.3 us -> 20.3 us
  matrix products: 15.4 us -> 17.7 us
  local copies, waits for them, and re-layouts: 6.4 us -> 7.99 us
    transpose x0 -> x1, other arithmetic: none -> 3.08 us  [to_request(): return jnp.swapaxes(rolled, 0, 1).reshape(-1, received.shape[2])]
    dot_general x4, matrix products: 3.42 us -> 5.64 us  [project_blocks(): jnp.dot(normed, lax.dynamic_slice_in_dim(keyval_weight, first, width, 0),...]
    dot_general x4, matrix products: 3.42 us -> 5.53 us  [project_blocks(): jnp.dot(normed, lax.dynamic_slice_in_dim(query_weight, first, width, 0),...]
    max x1 -> x0, other arithmetic: 2.02 us -> none  [body(): jnp.maximum((starts - source_pos + source_count - 1) // source_count, 0)]
    reduce_sum x4, other arithmetic: 2.07 us -> 3.99 us  [project_blocks(): jnp.sum(block * block, axis=-1, keepdims=True)]
    concatenate x1 -> x0, other arithmetic: 1.66 us -> none  [from_request(): return jnp.roll(jnp.swapaxes(shaped, 0, 1), shift_by, axis=0)]
  transfers between devices with their start and end apart: 8 -> 8, of which waited for: 6 -> 7; matrix products, arithmetic and copies ran while one was open for 7% -> 11% of each run, Pallas kernels for 0% -> 0%
where the time goes in v4:
time: 153 us; the launch traced here: 152 us
  waiting for transfers between devices  58.5 us (38%)
  starting transfers between devices  44.6 us (29%)
  other arithmetic  20.3 us (13%)
  matrix products  17.7 us (12%)
  local copies, waits for them, and re-layouts  7.99 us (5%)
  between operations  3.18 us (2%)
    all_to_all x1, waiting for transfers between devices, body(): lax.all_to_all(picked[chunk * chunk_slots:(chunk + 1) * chunk_slots], 'se...  19.9 us
    all_to_all x1, starting transfers between devices, body(): lax.all_to_all(picked[chunk * chunk_slots:(chunk + 1) * chunk_slots], 'se...  18.4 us
    ppermute x3, waiting for transfers between devices, ring_blocks(): blocks.append(lax.ppermute(narrow, axis_name, perm))  15.6 us
    all_to_all x1, waiting for transfers between devices, body(): lax.all_to_all(outgoing, 'seq', split_axis=1, concat_axis=1, tiled=True)  12.2 us
    ppermute x3, waiting for transfers between devices, ring_output(): total = total + lax.ppermute(part, axis_name, perm).astype(jnp.float32)  10.8 us
    ppermute x3, starting transfers between devices, ring_blocks(): blocks.append(lax.ppermute(narrow, axis_name, perm))  10.7 us
    ppermute x3, starting transfers between devices, ring_output(): total = total + lax.ppermute(part, axis_name, perm).astype(jnp.float32)  9.62 us
    all_to_all x1, starting transfers between devices, body(): lax.all_to_all(outgoing, 'seq', split_axis=1, concat_axis=1, tiled=True)  5.91 us
  transfers between devices with their start and end apart: 8, of which 7 were waited for; matrix products, arithmetic and copies ran while one was open for 11% of the time, Pallas kernels for 0%

profile of v4, /device:TPU:1, one launch (start us, length us, event | category | flops | bytes accessed | tf_op | source)
XLA Modules:
  0.0 152.3 jit_solution(544327384236241828)
XLA Ops:
  3.2 2.0 %select_reduce_fusion.5 = (s32[]{:T(128)}, s32[128]{0:T(128)S(1)}, s32[]{:T(128)}) fusion(s32[]{:T(128)} %fusion.76, s32[128]{0:T(128)S(1)} %reduce.1, s32[128]{0:T(128)} %param.14), kind=kLoop, calls=%fused_computation.140 | loop fusion | flops 766 | bytes 1548 | tf_op jit(solution)/shard_map/reduce_sum | solution.py:161
  11.1 18.4 %all-to-all-start = ((bf16[4,128,512]{2,0,1:T(4,128)(2,1)}), bf16[4,128,512]{2,0,1:T(4,128)(2,1)S(1)}, u32[]{:S(2)}, u32[]{:S(2)}) async-start(bf16[4,128,512]{2,0,1:T(4,128)(2,1)} %copy.38), calls=%async_computation | async-start | bytes 1048576 | tf_op jit(solution)/shard_map/all_to_all | solution.py:184
  30.2 19.9 %all-to-all-done = bf16[4,128,512]{2,0,1:T(4,128)(2,1)S(1)} async-done(((bf16[4,128,512]{2,0,1:T(4,128)(2,1)}), bf16[4,128,512]{2,0,1:T(4,128)(2,1)S(1)}, u32[]{:S(2)}, u32[]{:S(2)}) %all-to-all-start) | async-done | bytes 524320 | tf_op jit(solution)/shard_map/all_to_all | solution.py:184
  50.2 3.1 %collective-permute-start.2 = (bf16[512,512]{1,0:T(8,128)(2,1)S(1)}, bf16[512,512]{1,0:T(8,128)(2,1)}, u32[]{:S(2)}, u32[]{:S(2)}) collective-permute-start(bf16[512,512]{1,0:T(8,128)(2,1)S(1)} %bitcast.62), channel_id=1, source_target_pairs={{0,1},{1,2},{2,3},{3,0},{4,5},{5,6},{6,7},{7,4},{8,9},{9,10},{10,1... | collective-permute-start | bytes 1572872 | tf_op jit(solution)/shard_map/ppermute | solution.py:72
  53.3 1.8 %multiply_cosine_fusion.1 = (f32[512,128]{0,1:T(8,128)S(1)}, f32[512,128]{0,1:T(8,128)}) fusion(f32[128]{0:T(128)S(1)} %multiply_power_fusion, f32[512]{0:T(512)S(1)} %get-tuple-element.17), kind=kLoop, calls=%fused_computation.75 | loop fusion | flops 65536 | bytes 526848 | tf_op jit(solution)/shard_map/cos | solution.py:25
  55.1 4.3 %collective-permute-start.1 = (bf16[512,512]{1,0:T(8,128)(2,1)S(1)}, bf16[512,512]{1,0:T(8,128)(2,1)}, u32[]{:S(2)}, u32[]{:S(2)}) collective-permute-start(bf16[512,512]{1,0:T(8,128)(2,1)S(1)} %bitcast.63), channel_id=1, source_target_pairs={{0,2},{1,3},{2,0},{3,1},{4,6},{5,7},{6,4},{7,5},{8,10},{9,11},{10,... | collective-permute-start | bytes 1572872 | tf_op jit(solution)/shard_map/ppermute | solution.py:72
  60.7 3.2 %collective-permute-start = (bf16[512,512]{1,0:T(8,128)(2,1)S(1)}, bf16[512,512]{1,0:T(8,128)(2,1)}, u32[]{:S(2)}, u32[]{:S(2)}) collective-permute-start(bf16[512,512]{1,0:T(8,128)(2,1)S(1)} %bitcast.64), channel_id=1, source_target_pairs={{0,3},{1,0},{2,1},{3,2},{4,7},{5,4},{6,5},{7,6},{8,11},{9,8},{10,9... | collective-permute-start | bytes 1572872 | tf_op jit(solution)/shard_map/ppermute | solution.py:72
  64.5 2.8 %collective-permute-done.2 = bf16[512,512]{1,0:T(8,128)(2,1)} collective-permute-done((bf16[512,512]{1,0:T(8,128)(2,1)S(1)}, bf16[512,512]{1,0:T(8,128)(2,1)}, u32[]{:S(2)}, u32[]{:S(2)}) %collective-permute-start.2) | collective-permute-done | bytes 524320 | tf_op jit(solution)/shard_map/ppermute | solution.py:72
  68.5 11.0 %collective-permute-done.1 = bf16[512,512]{1,0:T(8,128)(2,1)} collective-permute-done((bf16[512,512]{1,0:T(8,128)(2,1)S(1)}, bf16[512,512]{1,0:T(8,128)(2,1)}, u32[]{:S(2)}, u32[]{:S(2)}) %collective-permute-start.1) | collective-permute-done | bytes 524320 | tf_op jit(solution)/shard_map/ppermute | solution.py:72
  80.7 1.8 %collective-permute-done = bf16[512,512]{1,0:T(8,128)(2,1)} collective-permute-done((bf16[512,512]{1,0:T(8,128)(2,1)S(1)}, bf16[512,512]{1,0:T(8,128)(2,1)}, u32[]{:S(2)}, u32[]{:S(2)}) %collective-permute-start) | collective-permute-done | bytes 524320 | tf_op jit(solution)/shard_map/ppermute | solution.py:72
  84.4 1.6 %convolution_add_fusion.2 = f32[512,512]{0,1:T(8,128)S(1)} fusion(f32[512,512]{0,1:T(8,128)S(1)} %fusion.25, bf16[2048,512]{1,0:T(8,128)(2,1)S(1)} %copy-done, s32[]{:T(128)S(6)} %select_n.129, bf16[512,512]{1,0:T(8,128)(2,1)} %collective-permute-done, f32[512]{0:T(512)S(1)} %get-tuple-element.12, f32[512]{0:T(512)S(1)} %fusion.71), kind=kOutput, calls=%fused_computation.2 | convolution fusion | flops 269746176 | bytes 3149828 | tf_op jit(solution)/shard_map/dot_general | solution.py:94
  86.0 1.6 %convolution_add_fusion.1 = f32[512,512]{0,1:T(8,128)S(1)} fusion(f32[512,512]{0,1:T(8,128)S(1)} %convolution_add_fusion.2, bf16[2048,512]{1,0:T(8,128)(2,1)S(1)} %copy-done, s32[]{:T(128)S(6)} %select_n.131, bf16[512,512]{1,0:T(8,128)(2,1)} %collective-permute-done.1, f32[512]{0:T(512)S(1)} %get-tuple-element.14, f32[512]{0:T(512)S(1)} %fusion.71), kind=kOutput, calls=%fused_computation.1 | convolution fusion | flops 269746176 | bytes 3149828 | tf_op jit(solution)/shard_map/dot_general | solution.py:94
  87.7 1.8 %convolution_add_fusion = f32[512,512]{0,1:T(8,128)S(1)} fusion(f32[512,512]{0,1:T(8,128)S(1)} %convolution_add_fusion.1, bf16[2048,512]{1,0:T(8,128)(2,1)S(1)} %copy-done, s32[]{:T(128)S(6)} %select_n.133, bf16[512,512]{1,0:T(8,128)(2,1)} %collective-permute-done.2, f32[512]{0:T(512)S(1)} %get-tuple-element.11, f32[512]{0:T(512)S(1)} %fusion.71), kind=kOutput, calls=%fused_computation | convolution fusion | flops 269746176 | bytes 3149828 | tf_op jit(solution)/shard_map/dot_general | solution.py:94
  91.3 1.6 %convolution_add_fusion.5 = f32[512,512]{0,1:T(8,128)S(1)} fusion(f32[512,512]{0,1:T(8,128)S(1)} %fusion.30, bf16[2048,512]{1,0:T(8,128)(2,1)S(1)} %copy-done.2, s32[]{:T(128)S(6)} %select_n.129, bf16[512,512]{1,0:T(8,128)(2,1)} %collective-permute-done, f32[512]{0:T(512)S(1)} %copy-done.8, f32[512]{0:T(512)S(1)} %fusion.71), kind=kOutput, calls=%fused_computation.5 | convolution fusion | flops 269746176 | bytes 3149828 | tf_op jit(solution)/shard_map/dot_general | solution.py:89
  93.0 1.6 %convolution_add_fusion.4 = f32[512,512]{0,1:T(8,128)S(1)} fusion(f32[512,512]{0,1:T(8,128)S(1)} %convolution_add_fusion.5, bf16[2048,512]{1,0:T(8,128)(2,1)S(1)} %copy-done.2, s32[]{:T(128)S(6)} %select_n.131, bf16[512,512]{1,0:T(8,128)(2,1)} %collective-permute-done.1, f32[512]{0:T(512)S(1)} %get-tuple-element.14, f32[512]{0:T(512)S(1)} %fusion.71), kind=kOutput, calls=%fused_computation.4 | convolution fusion | flops 269746176 | bytes 3149828 | tf_op jit(solution)/shard_map/dot_general | solution.py:89
  94.6 1.7 %convolution_add_fusion.3 = f32[512,512]{0,1:T(8,128)S(1)} fusion(f32[512,512]{0,1:T(8,128)S(1)} %convolution_add_fusion.4, bf16[2048,512]{1,0:T(8,128)(2,1)S(1)} %copy-done.2, s32[]{:T(128)S(6)} %select_n.133, bf16[512,512]{1,0:T(8,128)(2,1)} %collective-permute-done.2, f32[512]{0:T(512)S(1)} %get-tuple-element.11, f32[512]{0:T(512)S(1)} %fusion.71), kind=kOutput, calls=%fused_computation.3 | convolution fusion | flops 269746176 | bytes 3149828 | tf_op jit(solution)/shard_map/dot_general | solution.py:89
  100.5 5.9 %all-to-all-start.1 = ((bf16[4,128,512]{2,0,1:T(4,128)(2,1)}), bf16[4,128,512]{2,0,1:T(4,128)(2,1)S(1)}, u32[]{:S(2)}, u32[]{:S(2)}) async-start(bf16[4,128,512]{2,0,1:T(4,128)(2,1)} %copy.41), calls=%async_computation.1 | async-start | bytes 1048576 | tf_op jit(solution)/shard_map/all_to_all | solution.py:225
  110.4 3.1 %fusion.15 = bf16[4,128,512]{1,0,2:T(4,128)(2,1)} fusion(s32[]{:T(128)S(6)} %select_n.138, bf16[128,4,512]{0,1,2:T(4,128)(2,1)} %bitcast.69), kind=kLoop, calls=%fused_computation.47 | loop fusion | flops 1048576 | bytes 1048580 | tf_op jit(solution)/shard_map/transpose | solution.py:59
  114.8 12.2 %all-to-all-done.1 = bf16[4,128,512]{2,0,1:T(4,128)(2,1)S(1)} async-done(((bf16[4,128,512]{2,0,1:T(4,128)(2,1)}), bf16[4,128,512]{2,0,1:T(4,128)(2,1)S(1)}, u32[]{:S(2)}, u32[]{:S(2)}) %all-to-all-start.1) | async-done | bytes 524320 | tf_op jit(solution)/shard_map/all_to_all | solution.py:225
  129.7 4.2 %collective-permute-start.5 = (bf16[256,512]{1,0:T(8,128)(2,1)S(1)}, bf16[256,512]{1,0:T(8,128)(2,1)S(1)}, u32[]{:S(2)}, u32[]{:S(2)}) collective-permute-start(bf16[256,512]{1,0:T(8,128)(2,1)S(1)} %convolution_convert_fusion.3), channel_id=1, source_target_pairs={{0,3},{1,0},{2,1},{3,2},{4,7},{5,4},{6,5},{7,6},{8,11},{9,8},{10,9... | collective-permute-start | bytes 786440 | tf_op jit(solution)/shard_map/ppermute | solution.py:120
  133.9 3.5 %collective-permute-start.4 = (bf16[256,512]{1,0:T(8,128)(2,1)S(1)}, bf16[256,512]{1,0:T(8,128)(2,1)S(1)}, u32[]{:S(2)}, u32[]{:S(2)}) collective-permute-start(bf16[256,512]{1,0:T(8,128)(2,1)S(1)} %convolution_convert_fusion.4), channel_id=1, source_target_pairs={{0,2},{1,3},{2,0},{3,1},{4,6},{5,7},{6,4},{7,5},{8,10},{9,11},{10,... | collective-permute-start | bytes 786440 | tf_op jit(solution)/shard_map/ppermute | solution.py:120
  137.4 1.9 %collective-permute-start.3 = (bf16[256,512]{1,0:T(8,128)(2,1)S(1)}, bf16[256,512]{1,0:T(8,128)(2,1)S(1)}, u32[]{:S(2)}, u32[]{:S(2)}) collective-permute-start(bf16[256,512]{1,0:T(8,128)(2,1)S(1)} %convolution_convert_fusion.5), channel_id=1, source_target_pairs={{0,1},{1,2},{2,3},{3,0},{4,5},{5,6},{6,7},{7,4},{8,9},{9,10},{10,1... | collective-permute-start | bytes 786440 | tf_op jit(solution)/shard_map/ppermute | solution.py:120
  140.4 5.0 %collective-permute-done.5 = bf16[256,512]{1,0:T(8,128)(2,1)S(1)} collective-permute-done((bf16[256,512]{1,0:T(8,128)(2,1)S(1)}, bf16[256,512]{1,0:T(8,128)(2,1)S(1)}, u32[]{:S(2)}, u32[]{:S(2)}) %collective-permute-start.5) | collective-permute-done | bytes 262176 | tf_op jit(solution)/shard_map/ppermute | solution.py:120
  145.5 5.8 %collective-permute-done.3 = bf16[256,512]{1,0:T(8,128)(2,1)S(1)} collective-permute-done((bf16[256,512]{1,0:T(8,128)(2,1)S(1)}, bf16[256,512]{1,0:T(8,128)(2,1)S(1)}, u32[]{:S(2)}, u32[]{:S(2)}) %collective-permute-start.3) | collective-permute-done | bytes 262176 | tf_op jit(solution)/shard_map/ppermute | solution.py:120
  (91 shorter events, 29.1 us)
Async XLA Ops:
  0.6 83.1 %copy-start = (bf16[2048,512]{1,0:T(8,128)(2,1)S(1)}, bf16[2048,512]{1,0:T(8,128)(2,1)}, u32[]{:S(2)}) copy-start(bf16[2048,512]{1,0:T(8,128)(2,1)} %param.12) | copy-start | bytes 6291460
  8.5 21.6 %copy-start.15 = (pred[512]{0:T(512)(128)(4,1)}, pred[512]{0:T(512)(128)(4,1)S(1)}, u32[]{:S(2)}) copy-start(pred[512]{0:T(512)(128)(4,1)S(1)} %fusion.73) | copy-start | bytes 1540
  9.9 54.1 %copy-start.11 = (bf16[2048]{0:T(1024)(128)(2,1)S(1)}, bf16[2048]{0:T(1024)(128)(2,1)}, u32[]{:S(2)}) copy-start(bf16[2048]{0:T(1024)(128)(2,1)} %param.10) | copy-start | bytes 12292
  11.1 39.0 %all-to-all-start = ((bf16[4,128,512]{2,0,1:T(4,128)(2,1)}), bf16[4,128,512]{2,0,1:T(4,128)(2,1)S(1)}, u32[]{:S(2)}, u32[]{:S(2)}) async-start(bf16[4,128,512]{2,0,1:T(4,128)(2,1)} %copy.38), calls=%async_computation | async-start | bytes 1048576 | tf_op jit(solution)/shard_map/all_to_all | solution.py:184
  29.5 34.4 %copy-start.13 = (f32[128]{0:T(128)}, f32[128]{0:T(128)S(1)}, u32[]{:S(2)}) copy-start(f32[128]{0:T(128)S(1)} %multiply_power_fusion) | copy-start | bytes 1540
  50.2 17.1 %collective-permute-start.2 = (bf16[512,512]{1,0:T(8,128)(2,1)S(1)}, bf16[512,512]{1,0:T(8,128)(2,1)}, u32[]{:S(2)}, u32[]{:S(2)}) collective-permute-start(bf16[512,512]{1,0:T(8,128)(2,1)S(1)} %bitcast.62), channel_id=1, source_target_pairs={{0,1},{1,2},{2,3},{3,0},{4,5},{5,6},{6,7},{7,4},{8,9},{9,10},{10,1... | collective-permute-start | bytes 1572872 | tf_op jit(solution)/shard_map/ppermute | solution.py:72
  55.1 24.4 %collective-permute-start.1 = (bf16[512,512]{1,0:T(8,128)(2,1)S(1)}, bf16[512,512]{1,0:T(8,128)(2,1)}, u32[]{:S(2)}, u32[]{:S(2)}) collective-permute-start(bf16[512,512]{1,0:T(8,128)(2,1)S(1)} %bitcast.63), channel_id=1, source_target_pairs={{0,2},{1,3},{2,0},{3,1},{4,6},{5,7},{6,4},{7,5},{8,10},{9,11},{10,... | collective-permute-start | bytes 1572872 | tf_op jit(solution)/shard_map/ppermute | solution.py:72
  60.7 21.8 %collective-permute-start = (bf16[512,512]{1,0:T(8,128)(2,1)S(1)}, bf16[512,512]{1,0:T(8,128)(2,1)}, u32[]{:S(2)}, u32[]{:S(2)}) collective-permute-start(bf16[512,512]{1,0:T(8,128)(2,1)S(1)} %bitcast.64), channel_id=1, source_target_pairs={{0,3},{1,0},{2,1},{3,2},{4,7},{5,4},{6,5},{7,6},{8,11},{9,8},{10,9... | collective-permute-start | bytes 1572872 | tf_op jit(solution)/shard_map/ppermute | solution.py:72
  64.1 20.3 %copy-start.7 = (f32[512]{0:T(512)}, f32[512]{0:T(512)S(1)}, u32[]{:S(2)}) copy-start(f32[512]{0:T(512)S(1)} %get-tuple-element.12) | copy-start | bytes 6148
  87.7 1.9 %copy-start.14 = (f32[128]{0:T(128)S(1)}, f32[128]{0:T(128)}, u32[]{:S(2)}) copy-start(f32[128]{0:T(128)} %copy-done.13) | copy-start | bytes 1540
  87.7 3.1 %copy-start.2 = (bf16[2048,512]{1,0:T(8,128)(2,1)S(1)}, bf16[2048,512]{1,0:T(8,128)(2,1)}, u32[]{:S(2)}) copy-start(bf16[2048,512]{1,0:T(8,128)(2,1)} %param.11) | copy-start | bytes 6291460
  89.5 9.2 %copy-start.1 = (f32[512,512]{0,1:T(8,128)}, f32[512,512]{0,1:T(8,128)S(1)}, u32[]{:S(2)}) copy-start(f32[512,512]{0,1:T(8,128)S(1)} %convolution_add_fusion) | copy-start | bytes 3145732
  89.5 1.9 %copy-start.8 = (f32[512]{0:T(512)S(1)}, f32[512]{0:T(512)}, u32[]{:S(2)}) copy-start(f32[512]{0:T(512)} %copy-done.7) | copy-start | bytes 6148
  90.7 6.7 %copy-start.5 = (bf16[512,1,128]{0,2,1:T(8,128)(2,1)}, bf16[512,1,128]{0,2,1:T(8,128)(2,1)S(1)}, u32[]{:S(2)}) copy-start(bf16[512,1,128]{0,2,1:T(8,128)(2,1)S(1)} %get-tuple-element.10) | copy-start | bytes 393220
  94.6 1.7 %copy-start.4 = (f32[512,128]{0,1:T(8,128)S(1)}, f32[512,128]{0,1:T(8,128)}, u32[]{:S(2)}) copy-start(f32[512,128]{0,1:T(8,128)} %get-tuple-element.16) | copy-start | bytes 786436
  99.1 7.3 %copy-start.18 = (s32[128]{0:T(128)S(1)}, s32[128]{0:T(128)}, u32[]{:S(2)}) copy-start(s32[128]{0:T(128)} %param.16) | copy-start | bytes 1540
  99.1 10.3 %copy-start.6 = (bf16[512,1,128]{0,2,1:T(8,128)(2,1)S(1)}, bf16[512,1,128]{0,2,1:T(8,128)(2,1)}, u32[]{:S(2)}) copy-start(bf16[512,1,128]{0,2,1:T(8,128)(2,1)} %copy-done.5) | copy-start | bytes 393220
  100.5 26.6 %all-to-all-start.1 = ((bf16[4,128,512]{2,0,1:T(4,128)(2,1)}), bf16[4,128,512]{2,0,1:T(4,128)(2,1)S(1)}, u32[]{:S(2)}, u32[]{:S(2)}) async-start(bf16[4,128,512]{2,0,1:T(4,128)(2,1)} %copy.41), calls=%async_computation.1 | async-start | bytes 1048576 | tf_op jit(solution)/shard_map/all_to_all | solution.py:225
  109.5 17.7 %copy-start.10 = (s32[512]{0:T(512)S(1)}, s32[512]{0:T(512)}, u32[]{:S(2)}) copy-start(s32[512]{0:T(512)} %copy-done.9) | copy-start | bytes 6148
  109.5 17.7 %copy-start.16 = (pred[512]{0:T(512)(128)(4,1)S(1)}, pred[512]{0:T(512)(128)(4,1)}, u32[]{:S(2)}) copy-start(pred[512]{0:T(512)(128)(4,1)} %copy-done.15) | copy-start | bytes 1540
  127.1 2.0 %copy-start.3 = (bf16[512,2048]{1,0:T(8,128)(2,1)S(1)}, bf16[512,2048]{1,0:T(8,128)(2,1)}, u32[]{:S(2)}) copy-start(bf16[512,2048]{1,0:T(8,128)(2,1)} %param.13) | copy-start | bytes 6291460
  129.7 15.8 %collective-permute-start.5 = (bf16[256,512]{1,0:T(8,128)(2,1)S(1)}, bf16[256,512]{1,0:T(8,128)(2,1)S(1)}, u32[]{:S(2)}, u32[]{:S(2)}) collective-permute-start(bf16[256,512]{1,0:T(8,128)(2,1)S(1)} %convolution_convert_fusion.3), channel_id=1, source_target_pairs={{0,3},{1,0},{2,1},{3,2},{4,7},{5,4},{6,5},{7,6},{8,11},{9,8},{10,9... | collective-permute-start | bytes 786440 | tf_op jit(solution)/shard_map/ppermute | solution.py:120
  133.9 11.5 %collective-permute-start.4 = (bf16[256,512]{1,0:T(8,128)(2,1)S(1)}, bf16[256,512]{1,0:T(8,128)(2,1)S(1)}, u32[]{:S(2)}, u32[]{:S(2)}) collective-permute-start(bf16[256,512]{1,0:T(8,128)(2,1)S(1)} %convolution_convert_fusion.4), channel_id=1, source_target_pairs={{0,2},{1,3},{2,0},{3,1},{4,6},{5,7},{6,4},{7,5},{8,10},{9,11},{10,... | collective-permute-start | bytes 786440 | tf_op jit(solution)/shard_map/ppermute | solution.py:120
  137.4 13.8 %collective-permute-start.3 = (bf16[256,512]{1,0:T(8,128)(2,1)S(1)}, bf16[256,512]{1,0:T(8,128)(2,1)S(1)}, u32[]{:S(2)}, u32[]{:S(2)}) collective-permute-start(bf16[256,512]{1,0:T(8,128)(2,1)S(1)} %convolution_convert_fusion.5), channel_id=1, source_target_pairs={{0,1},{1,2},{2,3},{3,0},{4,5},{5,6},{6,7},{7,4},{8,9},{9,10},{10,1... | collective-permute-start | bytes 786440 | tf_op jit(solution)/shard_map/ppermute | solution.py:120
  (3 other events, 1.9 us)

commit v5 on v3

--- a/solution.py
+++ b/solution.py
@@ -69,11 +69,25 @@
 
 def ring_blocks(narrow, axis_name):
     count = lax.axis_size(axis_name)
-    blocks = [narrow]
-    for shift in range(1, count):
-        perm = [(index, (index - shift) % count) for index in range(count)]
-        blocks.append(lax.ppermute(narrow, axis_name, perm))
-    return blocks
+    to_left = [(index, (index - 1) % count) for index in range(count)]
+    to_right = [(index, (index + 1) % count) for index in range(count)]
+    from_right = lax.ppermute(narrow, axis_name, to_left)
+    from_left = lax.ppermute(narrow, axis_name, to_right)
+    if count != 4:
+        blocks = [narrow]
+        for shift in range(1, count):
+            perm = [(index, (index - shift) % count) for index in range(count)]
+            blocks.append(lax.ppermute(narrow, axis_name, perm))
+        return blocks
+    half = narrow.shape[1] // 2
+    across = jnp.concatenate(
+        [
+            lax.ppermute(from_right[:, :half], axis_name, to_left),
+            lax.ppermute(from_left[:, half:], axis_name, to_right),
+        ],
+        axis=1,
+    )
+    return [narrow, from_right, across, from_left]
 
 
 def project_blocks(blocks, gain, query_weight, keyval_weight, axis_name):

time: 148 us -> 150 us (1.014)
  starting transfers between devices: 44.6 us -> 49.1 us
  matrix products: 15.4 us -> 12.2 us
  local copies, waits for them, and re-layouts: 6.4 us -> 8.04 us
    ppermute x3 -> x4, waiting for transfers between devices: 16.5 us -> 13 us  [the longest x1 8.68 us: ring_blocks(): from_left = lax.ppermute(narrow, axis_name, to_right)]
    reshape x2, local copies, waits for them, and re-layouts: 0.67 us -> 4.12 us  [from_request(): shaped = request_rows.reshape(-1, source_count, request_rows.shape[1])]
    all_to_all x1, waiting for transfers between devices: 15.4 us -> 18.1 us  [body(): lax.all_to_all(outgoing, 'seq', split_axis=0, concat_axis=0, tiled=True)]
    ppermute x3 -> x4, starting transfers between devices: 10.7 us -> 13.2 us  [the longest x1 4.75 us: ring_blocks(): lax.ppermute(from_right[:, :half], axis_name, to_left)]
    all_to_all x1, starting transfers between devices: 5.84 us -> 7.79 us  [body(): lax.all_to_all(outgoing, 'seq', split_axis=0, concat_axis=0, tiled=True)]
  transfers between devices with their start and end apart: 8 -> 9, of which waited for: 6 -> 7; matrix products, arithmetic and copies ran while one was open for 7% -> 5% of each run, Pallas kernels for 0% -> 0%
where the time goes in v5:
time: 150 us
  waiting for transfers between devices  60.4 us (40%)
  starting transfers between devices  49.1 us (33%)
  other arithmetic  17 us (11%)
  matrix products  12.2 us (8%)
  local copies, waits for them, and re-layouts  8.04 us (5%)
  between operations  2.86 us (2%)
    all_to_all x1, starting transfers between devices, body(): lax.all_to_all(picked[:, chunk * chunk_slots:(chunk + 1) * chunk_slots],...  18.4 us
    all_to_all x1, waiting for transfers between devices, body(): lax.all_to_all(outgoing, 'seq', split_axis=0, concat_axis=0, tiled=True)  18.1 us
    all_to_all x1, waiting for transfers between devices, body(): lax.all_to_all(picked[:, chunk * chunk_slots:(chunk + 1) * chunk_slots],...  17.5 us
    ppermute x3, waiting for transfers between devices, ring_output(): total = total + lax.ppermute(part, axis_name, perm).astype(jnp.float32)  11.8 us
    ppermute x3, starting transfers between devices, ring_output(): total = total + lax.ppermute(part, axis_name, perm).astype(jnp.float32)  9.74 us
    ppermute x1, waiting for transfers between devices, ring_blocks(): from_left = lax.ppermute(narrow, axis_name, to_right)  8.68 us
    all_to_all x1, starting transfers between devices, body(): lax.all_to_all(outgoing, 'seq', split_axis=0, concat_axis=0, tiled=True)  7.79 us
    ppermute x1, starting transfers between devices, ring_blocks(): lax.ppermute(from_right[:, :half], axis_name, to_left)  4.75 us
  transfers between devices with their start and end apart: 9, of which 7 were waited for; matrix products, arithmetic and copies ran while one was open for 5% of the time, Pallas kernels for 0%

profile of v5, /device:TPU:1, one launch (start us, length us, event | category | flops | bytes accessed | tf_op | source)
XLA Modules:
  0.0 149.5 jit_solution(8618435747102199527)
XLA Ops:
  1.8 1.3 fusion.71
  3.1 2.0 %fusion.72 = (s32[128]{0:T(128)S(1)}, s32[128]{0:T(128)S(1)}, s32[]{:T(128)}) fusion(s32[]{:T(128)S(6)} %axis_index.27, s32[128]{0:T(128)S(1)} %reduce.1, s32[128]{0:T(128)} %param.16, s32[]{:T(128)} %fusion.71), kind=kLoop, calls=%fused_computation.138 | loop fusion | flops 2815 | bytes 2060 | tf_op jit(solution)/shard_map/max | solution.py:160
  6.6 1.3 convolution_convert_fusion
  8.8 18.4 %all-to-all-start = ((bf16[128,4,512]{2,1,0:T(4,128)(2,1)}), bf16[128,4,512]{2,1,0:T(4,128)(2,1)S(1)}, u32[]{:S(2)}, u32[]{:S(2)}) async-start(bf16[128,4,512]{2,1,0:T(4,128)(2,1)} %reshape.252), calls=%async_computation | async-start | bytes 1048576 | tf_op jit(solution)/shard_map/all_to_all | solution.py:196
  30.3 17.5 %all-to-all-done = bf16[128,4,512]{2,1,0:T(4,128)(2,1)S(1)} async-done(((bf16[128,4,512]{2,1,0:T(4,128)(2,1)}), bf16[128,4,512]{2,1,0:T(4,128)(2,1)S(1)}, u32[]{:S(2)}, u32[]{:S(2)}) %all-to-all-start) | async-done | bytes 524320 | tf_op jit(solution)/shard_map/all_to_all | solution.py:196
  48.4 3.1 %collective-permute-start.2 = (bf16[512,512]{1,0:T(8,128)(2,1)S(1)}, bf16[512,512]{1,0:T(8,128)(2,1)S(1)}, u32[]{:S(2)}, u32[]{:S(2)}) collective-permute-start(bf16[512,512]{1,0:T(8,128)(2,1)S(1)} %bitcast.38), channel_id=1, source_target_pairs={{0,1},{1,2},{2,3},{3,0},{4,5},{5,6},{6,7},{7,4},{8,9},{9,10},{10,1... | collective-permute-start | bytes 1572872 | tf_op jit(solution)/shard_map/ppermute | solution.py:75
  51.6 3.4 %collective-permute-start = (bf16[512,512]{1,0:T(8,128)(2,1)S(1)}, bf16[512,512]{1,0:T(8,128)(2,1)S(1)}, u32[]{:S(2)}, u32[]{:S(2)}) collective-permute-start(bf16[512,512]{1,0:T(8,128)(2,1)S(1)} %bitcast.39), channel_id=1, source_target_pairs={{0,3},{1,0},{2,1},{3,2},{4,7},{5,4},{6,5},{7,6},{8,11},{9,8},{10,9... | collective-permute-start | bytes 1572872 | tf_op jit(solution)/shard_map/ppermute | solution.py:74
  56.7 8.7 %collective-permute-done.2 = bf16[512,512]{1,0:T(8,128)(2,1)S(1)} collective-permute-done((bf16[512,512]{1,0:T(8,128)(2,1)S(1)}, bf16[512,512]{1,0:T(8,128)(2,1)S(1)}, u32[]{:S(2)}, u32[]{:S(2)}) %collective-permute-start.2) | collective-permute-done | bytes 524320 | tf_op jit(solution)/shard_map/ppermute | solution.py:75
  65.4 1.9 %collective-permute-start.3 = (bf16[512,256]{1,0:T(8,128)(2,1)S(1)}, bf16[512,256]{1,0:T(8,128)(2,1)S(1)}, u32[]{:S(2)}, u32[]{:S(2)}) collective-permute-start(bf16[512,256]{1,0:T(8,128)(2,1)S(1)} %slice.42), channel_id=1, source_target_pairs={{0,1},{1,2},{2,3},{3,0},{4,5},{5,6},{6,7},{7,4},{8,9},{9,10},{10,1... | collective-permute-start | bytes 786440 | tf_op jit(solution)/shard_map/ppermute | solution.py:86
  67.4 4.8 %collective-permute-start.1 = (bf16[512,256]{1,0:T(8,128)(2,1)S(1)}, bf16[512,256]{1,0:T(8,128)(2,1)S(1)}, u32[]{:S(2)}, u32[]{:S(2)}) collective-permute-start(bf16[512,256]{1,0:T(8,128)(2,1)S(1)} %slice.41), channel_id=1, source_target_pairs={{0,3},{1,0},{2,1},{3,2},{4,7},{5,4},{6,5},{7,6},{8,11},{9,8},{10,9... | collective-permute-start | bytes 786440 | tf_op jit(solution)/shard_map/ppermute | solution.py:85
  72.5 3.5 %collective-permute-done.3 = bf16[512,256]{1,0:T(8,128)(2,1)S(1)} collective-permute-done((bf16[512,256]{1,0:T(8,128)(2,1)S(1)}, bf16[512,256]{1,0:T(8,128)(2,1)S(1)}, u32[]{:S(2)}, u32[]{:S(2)}) %collective-permute-start.3) | collective-permute-done | bytes 262176 | tf_op jit(solution)/shard_map/ppermute | solution.py:86
  86.1 2.0 %reshape.256 = bf16[4,128,512]{1,0,2:T(4,128)(2,1)} reshape(bf16[512,512]{0,1:T(8,128)(2,1)} %pad_maximum_fusion.2) | data formatting | bytes 1048576 | tf_op jit(solution)/shard_map/reshape | solution.py:66
  88.1 2.2 %copy.24 = bf16[4,128,512]{2,0,1:T(4,128)(2,1)} copy(bf16[4,128,512]{1,0,2:T(4,128)(2,1)} %reshape.256) | data formatting | bytes 1048576 | tf_op jit(solution)/shard_map/reshape | solution.py:66
  90.3 2.6 %fusion.15 = bf16[128,4,512]{2,1,0:T(4,128)(2,1)} fusion(s32[]{:T(128)S(6)} %select_n.128, bf16[128,4,512]{2,1,0:T(4,128)(2,1)} %bitcast.43), kind=kLoop, calls=%fused_computation.49 | loop fusion | flops 262144 | bytes 1048580 | tf_op jit(solution)/shard_map/jit(_roll_dynamic)/concatenate | solution.py:67
  92.9 7.8 %all-to-all-start.1 = ((bf16[128,4,512]{2,1,0:T(4,128)(2,1)}), bf16[128,4,512]{2,1,0:T(4,128)(2,1)}, u32[]{:S(2)}, u32[]{:S(2)}) async-start(bf16[128,4,512]{2,1,0:T(4,128)(2,1)} %fusion.15), calls=%async_computation.1 | async-start | bytes 1048576 | tf_op jit(solution)/shard_map/all_to_all | solution.py:235
  100.7 1.3 select_reduce_fusion.3
  102.9 18.1 %all-to-all-done.1 = bf16[128,4,512]{2,1,0:T(4,128)(2,1)} async-done(((bf16[128,4,512]{2,1,0:T(4,128)(2,1)}), bf16[128,4,512]{2,1,0:T(4,128)(2,1)}, u32[]{:S(2)}, u32[]{:S(2)}) %all-to-all-start.1) | async-done | bytes 524320 | tf_op jit(solution)/shard_map/all_to_all | solution.py:235
  122.7 1.4 convolution_convert_fusion.3
  124.1 1.3 convolution_convert_fusion.4
  125.8 5.3 %collective-permute-start.6 = (bf16[256,512]{1,0:T(8,128)(2,1)S(1)}, bf16[256,512]{1,0:T(8,128)(2,1)S(1)}, u32[]{:S(2)}, u32[]{:S(2)}) collective-permute-start(bf16[256,512]{1,0:T(8,128)(2,1)S(1)} %convolution_convert_fusion.3), channel_id=1, source_target_pairs={{0,3},{1,0},{2,1},{3,2},{4,7},{5,4},{6,5},{7,6},{8,11},{9,8},{10,9... | collective-permute-start | bytes 786440 | tf_op jit(solution)/shard_map/ppermute | solution.py:137
  131.2 1.9 %collective-permute-start.5 = (bf16[256,512]{1,0:T(8,128)(2,1)S(1)}, bf16[256,512]{1,0:T(8,128)(2,1)S(1)}, u32[]{:S(2)}, u32[]{:S(2)}) collective-permute-start(bf16[256,512]{1,0:T(8,128)(2,1)S(1)} %convolution_convert_fusion.4), channel_id=1, source_target_pairs={{0,2},{1,3},{2,0},{3,1},{4,6},{5,7},{6,4},{7,5},{8,10},{9,11},{10,... | collective-permute-start | bytes 786440 | tf_op jit(solution)/shard_map/ppermute | solution.py:137
  133.1 2.5 %collective-permute-start.4 = (bf16[256,512]{1,0:T(8,128)(2,1)S(1)}, bf16[256,512]{1,0:T(8,128)(2,1)S(1)}, u32[]{:S(2)}, u32[]{:S(2)}) collective-permute-start(bf16[256,512]{1,0:T(8,128)(2,1)S(1)} %convolution_convert_fusion.5), channel_id=1, source_target_pairs={{0,1},{1,2},{2,3},{3,0},{4,5},{5,6},{6,7},{7,4},{8,9},{9,10},{10,1... | collective-permute-start | bytes 786440 | tf_op jit(solution)/shard_map/ppermute | solution.py:137
  136.7 6.1 %collective-permute-done.6 = bf16[256,512]{1,0:T(8,128)(2,1)S(1)} collective-permute-done((bf16[256,512]{1,0:T(8,128)(2,1)S(1)}, bf16[256,512]{1,0:T(8,128)(2,1)S(1)}, u32[]{:S(2)}, u32[]{:S(2)}) %collective-permute-start.6) | collective-permute-done | bytes 262176 | tf_op jit(solution)/shard_map/ppermute | solution.py:137
  142.8 5.6 %collective-permute-done.4 = bf16[256,512]{1,0:T(8,128)(2,1)S(1)} collective-permute-done((bf16[256,512]{1,0:T(8,128)(2,1)S(1)}, bf16[256,512]{1,0:T(8,128)(2,1)S(1)}, u32[]{:S(2)}, u32[]{:S(2)}) %collective-permute-start.4) | collective-permute-done | bytes 262176 | tf_op jit(solution)/shard_map/ppermute | solution.py:137
  (69 shorter events, 22.7 us)
Async XLA Ops:
  0.6 76.5 %copy-start = (bf16[2048,512]{1,0:T(8,128)(2,1)S(1)}, bf16[2048,512]{1,0:T(8,128)(2,1)}, u32[]{:S(2)}) copy-start(bf16[2048,512]{1,0:T(8,128)(2,1)} %param.14) | copy-start | bytes 6291460
  7.9 47.8 %copy-start.3 = (bf16[2048]{0:T(1024)(128)(2,1)S(1)}, bf16[2048]{0:T(1024)(128)(2,1)}, u32[]{:S(2)}) copy-start(bf16[2048]{0:T(1024)(128)(2,1)} %param.12) | copy-start | bytes 12292
  8.8 39.0 %all-to-all-start = ((bf16[128,4,512]{2,1,0:T(4,128)(2,1)}), bf16[128,4,512]{2,1,0:T(4,128)(2,1)S(1)}, u32[]{:S(2)}, u32[]{:S(2)}) async-start(bf16[128,4,512]{2,1,0:T(4,128)(2,1)} %reshape.252), calls=%async_computation | async-start | bytes 1048576 | tf_op jit(solution)/shard_map/all_to_all | solution.py:196
  48.4 17.0 %collective-permute-start.2 = (bf16[512,512]{1,0:T(8,128)(2,1)S(1)}, bf16[512,512]{1,0:T(8,128)(2,1)S(1)}, u32[]{:S(2)}, u32[]{:S(2)}) collective-permute-start(bf16[512,512]{1,0:T(8,128)(2,1)S(1)} %bitcast.38), channel_id=1, source_target_pairs={{0,1},{1,2},{2,3},{3,0},{4,5},{5,6},{6,7},{7,4},{8,9},{9,10},{10,1... | collective-permute-start | bytes 1572872 | tf_op jit(solution)/shard_map/ppermute | solution.py:75
  51.6 15.8 %collective-permute-start = (bf16[512,512]{1,0:T(8,128)(2,1)S(1)}, bf16[512,512]{1,0:T(8,128)(2,1)S(1)}, u32[]{:S(2)}, u32[]{:S(2)}) collective-permute-start(bf16[512,512]{1,0:T(8,128)(2,1)S(1)} %bitcast.39), channel_id=1, source_target_pairs={{0,3},{1,0},{2,1},{3,2},{4,7},{5,4},{6,5},{7,6},{8,11},{9,8},{10,9... | collective-permute-start | bytes 1572872 | tf_op jit(solution)/shard_map/ppermute | solution.py:74
  65.4 10.5 %collective-permute-start.3 = (bf16[512,256]{1,0:T(8,128)(2,1)S(1)}, bf16[512,256]{1,0:T(8,128)(2,1)S(1)}, u32[]{:S(2)}, u32[]{:S(2)}) collective-permute-start(bf16[512,256]{1,0:T(8,128)(2,1)S(1)} %slice.42), channel_id=1, source_target_pairs={{0,1},{1,2},{2,3},{3,0},{4,5},{5,6},{6,7},{7,4},{8,9},{9,10},{10,1... | collective-permute-start | bytes 786440 | tf_op jit(solution)/shard_map/ppermute | solution.py:86
  67.4 9.5 %collective-permute-start.1 = (bf16[512,256]{1,0:T(8,128)(2,1)S(1)}, bf16[512,256]{1,0:T(8,128)(2,1)S(1)}, u32[]{:S(2)}, u32[]{:S(2)}) collective-permute-start(bf16[512,256]{1,0:T(8,128)(2,1)S(1)} %slice.41), channel_id=1, source_target_pairs={{0,3},{1,0},{2,1},{3,2},{4,7},{5,4},{6,5},{7,6},{8,11},{9,8},{10,9... | collective-permute-start | bytes 786440 | tf_op jit(solution)/shard_map/ppermute | solution.py:85
  78.9 1.8 %copy-start.1 = (bf16[2048,512]{1,0:T(8,128)(2,1)S(1)}, bf16[2048,512]{1,0:T(8,128)(2,1)}, u32[]{:S(2)}) copy-start(bf16[2048,512]{1,0:T(8,128)(2,1)} %param.13) | copy-start | bytes 6291460
  86.1 14.5 %copy-start.4 = (s32[128]{0:T(128)S(1)}, s32[128]{0:T(128)}, u32[]{:S(2)}) copy-start(s32[128]{0:T(128)} %param.18) | copy-start | bytes 1540
  92.9 28.1 %all-to-all-start.1 = ((bf16[128,4,512]{2,1,0:T(4,128)(2,1)}), bf16[128,4,512]{2,1,0:T(4,128)(2,1)}, u32[]{:S(2)}, u32[]{:S(2)}) async-start(bf16[128,4,512]{2,1,0:T(4,128)(2,1)} %fusion.15), calls=%async_computation.1 | async-start | bytes 1048576 | tf_op jit(solution)/shard_map/all_to_all | solution.py:235
  122.2 3.3 %copy-start.2 = (bf16[512,2048]{1,0:T(8,128)(2,1)S(1)}, bf16[512,2048]{1,0:T(8,128)(2,1)}, u32[]{:S(2)}) copy-start(bf16[512,2048]{1,0:T(8,128)(2,1)} %param.15) | copy-start | bytes 6291460
  125.8 17.0 %collective-permute-start.6 = (bf16[256,512]{1,0:T(8,128)(2,1)S(1)}, bf16[256,512]{1,0:T(8,128)(2,1)S(1)}, u32[]{:S(2)}, u32[]{:S(2)}) collective-permute-start(bf16[256,512]{1,0:T(8,128)(2,1)S(1)} %convolution_convert_fusion.3), channel_id=1, source_target_pairs={{0,3},{1,0},{2,1},{3,2},{4,7},{5,4},{6,5},{7,6},{8,11},{9,8},{10,9... | collective-permute-start | bytes 786440 | tf_op jit(solution)/shard_map/ppermute | solution.py:137
  131.2 11.7 %collective-permute-start.5 = (bf16[256,512]{1,0:T(8,128)(2,1)S(1)}, bf16[256,512]{1,0:T(8,128)(2,1)S(1)}, u32[]{:S(2)}, u32[]{:S(2)}) collective-permute-start(bf16[256,512]{1,0:T(8,128)(2,1)S(1)} %convolution_convert_fusion.4), channel_id=1, source_target_pairs={{0,2},{1,3},{2,0},{3,1},{4,6},{5,7},{6,4},{7,5},{8,10},{9,11},{10,... | collective-permute-start | bytes 786440 | tf_op jit(solution)/shard_map/ppermute | solution.py:137
  133.1 15.4 %collective-permute-start.4 = (bf16[256,512]{1,0:T(8,128)(2,1)S(1)}, bf16[256,512]{1,0:T(8,128)(2,1)S(1)}, u32[]{:S(2)}, u32[]{:S(2)}) collective-permute-start(bf16[256,512]{1,0:T(8,128)(2,1)S(1)} %convolution_convert_fusion.5), channel_id=1, source_target_pairs={{0,1},{1,2},{2,3},{3,0},{4,5},{5,6},{6,7},{7,4},{8,9},{9,10},{10,1... | collective-permute-start | bytes 786440 | tf_op jit(solution)/shard_map/ppermute | solution.py:137

commit v6 on v3

--- a/solution.py
+++ b/solution.py
@@ -159,11 +159,10 @@
     select = (
         (row_index.reshape(-1)[:, None] == local_ids[None, :]) & live_send.reshape(-1)[:, None]
     ).astype(jnp.bfloat16)
-    owned_request = jnp.sum(jnp.where(request_owner == source_pos, request_ids, 0))
-    own_match = request_ids == owned_request
-    own_start = jnp.sum(jnp.where(own_match, starts, 0))
-    own_length = jnp.sum(jnp.where(own_match, request_lengths, 0))
-    own_slot = jnp.sum(jnp.where(own_match, cache_slots, 0))
+    send_slot = jnp.sum(jnp.where(owner_match, cache_slots[None, :], 0), axis=1)
+    own_start = lax.dynamic_index_in_dim(send_start, source_pos, 0, keepdims=False)
+    own_length = lax.dynamic_index_in_dim(send_length, source_pos, 0, keepdims=False)
+    own_slot = lax.dynamic_index_in_dim(send_slot, source_pos, 0, keepdims=False)
     shift_by = own_start % source_count
     picked = (
         jnp.dot(select, hidden_in, preferred_element_type=jnp.float32)

time: 148 us -> 145 us (0.980)
  other arithmetic: 17.3 us -> 11.8 us
  local copies, waits for them, and re-layouts: 6.4 us -> 8.16 us
    reduce_sum x4 -> x1, other arithmetic: 4.83 us -> 0.83 us  [body(): send_slot = jnp.sum(jnp.where(owner_match, cache_slots[None, :], 0), axis=1)]
    dynamic_slice x0 -> x3, local copies, waits for them, and re-layouts: none -> 1.77 us  [the longest x1 0.59 us: body(): lax.dynamic_index_in_dim(send_start, source_pos, 0, keepdims=False)]
where the time goes in v6:
time: 145 us; the launch traced here: 144 us
  waiting for transfers between devices  61 us (42%)
  starting transfers between devices  44.6 us (31%)
  matrix products  15.4 us (11%)
  other arithmetic  11.8 us (8%)
  local copies, waits for them, and re-layouts  8.16 us (6%)
  between operations  3.09 us (2%)
    all_to_all x1, starting transfers between devices, body(): lax.all_to_all(picked[:, chunk * chunk_slots:(chunk + 1) * chunk_slots],...  18.4 us
    all_to_all x1, waiting for transfers between devices, body(): lax.all_to_all(picked[:, chunk * chunk_slots:(chunk + 1) * chunk_slots],...  17.4 us
    ppermute x3, waiting for transfers between devices, ring_blocks(): blocks.append(lax.ppermute(narrow, axis_name, perm))  16.6 us
    all_to_all x1, waiting for transfers between devices, body(): lax.all_to_all(outgoing, 'seq', split_axis=0, concat_axis=0, tiled=True)  16.3 us
    ppermute x3, waiting for transfers between devices, ring_output(): total = total + lax.ppermute(part, axis_name, perm).astype(jnp.float32)  10.8 us
    ppermute x3, starting transfers between devices, ring_blocks(): blocks.append(lax.ppermute(narrow, axis_name, perm))  10.7 us
    ppermute x3, starting transfers between devices, ring_output(): total = total + lax.ppermute(part, axis_name, perm).astype(jnp.float32)  9.61 us
    all_to_all x1, starting transfers between devices, body(): lax.all_to_all(outgoing, 'seq', split_axis=0, concat_axis=0, tiled=True)  5.86 us
  transfers between devices with their start and end apart: 8, of which 6 were waited for; matrix products, arithmetic and copies ran while one was open for 7% of the time, Pallas kernels for 0%

profile of v6, /device:TPU:1, one launch (start us, length us, event | category | flops | bytes accessed | tf_op | source)
XLA Modules:
  0.0 144.1 jit_solution(10486199955881899191)
XLA Ops:
  4.0 1.3 convolution_convert_fusion
  6.2 18.4 %all-to-all-start = ((bf16[128,4,512]{2,1,0:T(4,128)(2,1)}), bf16[128,4,512]{2,1,0:T(4,128)(2,1)S(1)}, u32[]{:S(2)}, u32[]{:S(2)}) async-start(bf16[128,4,512]{2,1,0:T(4,128)(2,1)} %reshape.253), calls=%async_computation | async-start | bytes 1048576 | tf_op jit(solution)/shard_map/all_to_all | solution.py:181
  27.8 17.4 %all-to-all-done = bf16[128,4,512]{2,1,0:T(4,128)(2,1)S(1)} async-done(((bf16[128,4,512]{2,1,0:T(4,128)(2,1)}), bf16[128,4,512]{2,1,0:T(4,128)(2,1)S(1)}, u32[]{:S(2)}, u32[]{:S(2)}) %all-to-all-start) | async-done | bytes 524320 | tf_op jit(solution)/shard_map/all_to_all | solution.py:181
  45.8 3.1 %collective-permute-start.2 = (bf16[512,512]{1,0:T(8,128)(2,1)S(1)}, bf16[512,512]{1,0:T(8,128)(2,1)S(1)}, u32[]{:S(2)}, u32[]{:S(2)}) collective-permute-start(bf16[512,512]{1,0:T(8,128)(2,1)S(1)} %bitcast.41), channel_id=1, source_target_pairs={{0,1},{1,2},{2,3},{3,0},{4,5},{5,6},{6,7},{7,4},{8,9},{9,10},{10,1... | collective-permute-start | bytes 1572872 | tf_op jit(solution)/shard_map/ppermute | solution.py:75
  48.9 4.4 %collective-permute-start.1 = (bf16[512,512]{1,0:T(8,128)(2,1)S(1)}, bf16[512,512]{1,0:T(8,128)(2,1)}, u32[]{:S(2)}, u32[]{:S(2)}) collective-permute-start(bf16[512,512]{1,0:T(8,128)(2,1)S(1)} %bitcast.42), channel_id=1, source_target_pairs={{0,2},{1,3},{2,0},{3,1},{4,6},{5,7},{6,4},{7,5},{8,10},{9,11},{10,... | collective-permute-start | bytes 1572872 | tf_op jit(solution)/shard_map/ppermute | solution.py:75
  54.2 3.2 %collective-permute-start = (bf16[512,512]{1,0:T(8,128)(2,1)S(1)}, bf16[512,512]{1,0:T(8,128)(2,1)S(1)}, u32[]{:S(2)}, u32[]{:S(2)}) collective-permute-start(bf16[512,512]{1,0:T(8,128)(2,1)S(1)} %bitcast.43), channel_id=1, source_target_pairs={{0,3},{1,0},{2,1},{3,2},{4,7},{5,4},{6,5},{7,6},{8,11},{9,8},{10,9... | collective-permute-start | bytes 1572872 | tf_op jit(solution)/shard_map/ppermute | solution.py:75
  58.4 4.4 %collective-permute-done.2 = bf16[512,512]{1,0:T(8,128)(2,1)S(1)} collective-permute-done((bf16[512,512]{1,0:T(8,128)(2,1)S(1)}, bf16[512,512]{1,0:T(8,128)(2,1)S(1)}, u32[]{:S(2)}, u32[]{:S(2)}) %collective-permute-start.2) | collective-permute-done | bytes 524320 | tf_op jit(solution)/shard_map/ppermute | solution.py:75
  63.0 12.1 %collective-permute-done.1 = bf16[512,512]{1,0:T(8,128)(2,1)} collective-permute-done((bf16[512,512]{1,0:T(8,128)(2,1)S(1)}, bf16[512,512]{1,0:T(8,128)(2,1)}, u32[]{:S(2)}, u32[]{:S(2)}) %collective-permute-start.1) | collective-permute-done | bytes 524320 | tf_op jit(solution)/shard_map/ppermute | solution.py:75
  75.1 1.2 fusion.6
  77.8 1.6 %convolution_add_fusion.1 = f32[512,512]{0,1:T(8,128)S(1)} fusion(f32[512,512]{0,1:T(8,128)S(1)} %convolution_add_fusion.2, bf16[2048,512]{1,0:T(8,128)(2,1)S(1)} %copy-done, s32[]{:T(128)S(6)} %select_n.110, bf16[512,512]{1,0:T(8,128)(2,1)} %collective-permute-done.1, f32[512]{0:T(512)S(1)} %get-tuple-element.18, f32[512]{0:T(512)S(1)} %fusion.72), kind=kOutput, calls=%fused_computation.1 | convolution fusion | flops 269746176 | bytes 3149828 | tf_op jit(solution)/shard_map/dot_general | solution.py:97
  80.1 1.2 fusion.41
  82.5 1.6 %convolution_add_fusion.4 = f32[512,512]{0,1:T(8,128)S(1)} fusion(f32[512,512]{0,1:T(8,128)S(1)} %convolution_add_fusion.5, bf16[2048,512]{1,0:T(8,128)(2,1)S(1)} %copy-done.2, s32[]{:T(128)S(6)} %select_n.110, bf16[512,512]{1,0:T(8,128)(2,1)} %collective-permute-done.1, f32[512]{0:T(512)S(1)} %get-tuple-element.18, f32[512]{0:T(512)S(1)} %fusion.72), kind=kOutput, calls=%fused_computation.4 | convolution fusion | flops 269746176 | bytes 3149828 | tf_op jit(solution)/shard_map/dot_general | solution.py:92
  87.6 1.7 %fusion.15 = bf16[128,4,512]{2,1,0:T(4,128)(2,1)} fusion(s32[]{:T(128)S(6)} %select_n.122, bf16[128,4,512]{2,1,0:T(4,128)(2,1)S(1)} %bitcast.47), kind=kLoop, calls=%fused_computation.49 | loop fusion | flops 262144 | bytes 1048580 | tf_op jit(solution)/shard_map/jit(_roll_dynamic)/concatenate | solution.py:67
  89.2 5.9 %all-to-all-start.1 = ((bf16[128,4,512]{2,1,0:T(4,128)(2,1)}), bf16[128,4,512]{2,1,0:T(4,128)(2,1)S(1)}, u32[]{:S(2)}, u32[]{:S(2)}) async-start(bf16[128,4,512]{2,1,0:T(4,128)(2,1)} %fusion.15), calls=%async_computation.1 | async-start | bytes 1048576 | tf_op jit(solution)/shard_map/all_to_all | solution.py:220
  98.3 1.3 copy.25
  99.6 16.3 %all-to-all-done.1 = bf16[128,4,512]{2,1,0:T(4,128)(2,1)S(1)} async-done(((bf16[128,4,512]{2,1,0:T(4,128)(2,1)}), bf16[128,4,512]{2,1,0:T(4,128)(2,1)S(1)}, u32[]{:S(2)}, u32[]{:S(2)}) %all-to-all-start.1) | async-done | bytes 524320 | tf_op jit(solution)/shard_map/all_to_all | solution.py:220
  116.7 1.7 %convolution_convert_fusion.7 = bf16[256,512]{1,0:T(8,128)(2,1)S(1)} fusion(bf16[512,512]{1,0:T(8,128)(2,1)} %reshape.258, s32[512]{0:T(512)S(1)} %add.187, pred[512]{0:T(512)(128)(4,1)S(1)} %compare_and_fusion), kind=kOutput, calls=%fused_computation.24 | convolution fusion | flops 134610944 | bytes 788992 | tf_op jit(solution)/shard_map/dot_general | solution.py:224
  118.4 1.3 convolution_convert_fusion.3
  119.8 1.3 convolution_convert_fusion.4
  121.5 4.3 %collective-permute-start.5 = (bf16[256,512]{1,0:T(8,128)(2,1)S(1)}, bf16[256,512]{1,0:T(8,128)(2,1)S(1)}, u32[]{:S(2)}, u32[]{:S(2)}) collective-permute-start(bf16[256,512]{1,0:T(8,128)(2,1)S(1)} %convolution_convert_fusion.3), channel_id=1, source_target_pairs={{0,3},{1,0},{2,1},{3,2},{4,7},{5,4},{6,5},{7,6},{8,11},{9,8},{10,9... | collective-permute-start | bytes 786440 | tf_op jit(solution)/shard_map/ppermute | solution.py:123
  125.7 3.4 %collective-permute-start.4 = (bf16[256,512]{1,0:T(8,128)(2,1)S(1)}, bf16[256,512]{1,0:T(8,128)(2,1)S(1)}, u32[]{:S(2)}, u32[]{:S(2)}) collective-permute-start(bf16[256,512]{1,0:T(8,128)(2,1)S(1)} %convolution_convert_fusion.4), channel_id=1, source_target_pairs={{0,2},{1,3},{2,0},{3,1},{4,6},{5,7},{6,4},{7,5},{8,10},{9,11},{10,... | collective-permute-start | bytes 786440 | tf_op jit(solution)/shard_map/ppermute | solution.py:123
  129.2 1.9 %collective-permute-start.3 = (bf16[256,512]{1,0:T(8,128)(2,1)S(1)}, bf16[256,512]{1,0:T(8,128)(2,1)S(1)}, u32[]{:S(2)}, u32[]{:S(2)}) collective-permute-start(bf16[256,512]{1,0:T(8,128)(2,1)S(1)} %convolution_convert_fusion.5), channel_id=1, source_target_pairs={{0,1},{1,2},{2,3},{3,0},{4,5},{5,6},{6,7},{7,4},{8,9},{9,10},{10,1... | collective-permute-start | bytes 786440 | tf_op jit(solution)/shard_map/ppermute | solution.py:123
  132.2 5.0 %collective-permute-done.5 = bf16[256,512]{1,0:T(8,128)(2,1)S(1)} collective-permute-done((bf16[256,512]{1,0:T(8,128)(2,1)S(1)}, bf16[256,512]{1,0:T(8,128)(2,1)S(1)}, u32[]{:S(2)}, u32[]{:S(2)}) %collective-permute-start.5) | collective-permute-done | bytes 262176 | tf_op jit(solution)/shard_map/ppermute | solution.py:123
  137.3 5.8 %collective-permute-done.3 = bf16[256,512]{1,0:T(8,128)(2,1)S(1)} collective-permute-done((bf16[256,512]{1,0:T(8,128)(2,1)S(1)}, bf16[256,512]{1,0:T(8,128)(2,1)S(1)}, u32[]{:S(2)}, u32[]{:S(2)}) %collective-permute-start.3) | collective-permute-done | bytes 262176 | tf_op jit(solution)/shard_map/ppermute | solution.py:123
  (65 shorter events, 21.1 us)
Async XLA Ops:
  0.6 75.9 %copy-start = (bf16[2048,512]{1,0:T(8,128)(2,1)S(1)}, bf16[2048,512]{1,0:T(8,128)(2,1)}, u32[]{:S(2)}) copy-start(bf16[2048,512]{1,0:T(8,128)(2,1)} %param.14) | copy-start | bytes 6291460
  5.3 48.8 %copy-start.4 = (bf16[2048]{0:T(1024)(128)(2,1)S(1)}, bf16[2048]{0:T(1024)(128)(2,1)}, u32[]{:S(2)}) copy-start(bf16[2048]{0:T(1024)(128)(2,1)} %param.12) | copy-start | bytes 12292
  6.2 39.0 %all-to-all-start = ((bf16[128,4,512]{2,1,0:T(4,128)(2,1)}), bf16[128,4,512]{2,1,0:T(4,128)(2,1)S(1)}, u32[]{:S(2)}, u32[]{:S(2)}) async-start(bf16[128,4,512]{2,1,0:T(4,128)(2,1)} %reshape.253), calls=%async_computation | async-start | bytes 1048576 | tf_op jit(solution)/shard_map/all_to_all | solution.py:181
  45.8 17.0 %collective-permute-start.2 = (bf16[512,512]{1,0:T(8,128)(2,1)S(1)}, bf16[512,512]{1,0:T(8,128)(2,1)S(1)}, u32[]{:S(2)}, u32[]{:S(2)}) collective-permute-start(bf16[512,512]{1,0:T(8,128)(2,1)S(1)} %bitcast.41), channel_id=1, source_target_pairs={{0,1},{1,2},{2,3},{3,0},{4,5},{5,6},{6,7},{7,4},{8,9},{9,10},{10,1... | collective-permute-start | bytes 1572872 | tf_op jit(solution)/shard_map/ppermute | solution.py:75
  48.9 26.2 %collective-permute-start.1 = (bf16[512,512]{1,0:T(8,128)(2,1)S(1)}, bf16[512,512]{1,0:T(8,128)(2,1)}, u32[]{:S(2)}, u32[]{:S(2)}) collective-permute-start(bf16[512,512]{1,0:T(8,128)(2,1)S(1)} %bitcast.42), channel_id=1, source_target_pairs={{0,2},{1,3},{2,0},{3,1},{4,6},{5,7},{6,4},{7,5},{8,10},{9,11},{10,... | collective-permute-start | bytes 1572872 | tf_op jit(solution)/shard_map/ppermute | solution.py:75
  54.2 22.2 %collective-permute-start = (bf16[512,512]{1,0:T(8,128)(2,1)S(1)}, bf16[512,512]{1,0:T(8,128)(2,1)S(1)}, u32[]{:S(2)}, u32[]{:S(2)}) collective-permute-start(bf16[512,512]{1,0:T(8,128)(2,1)S(1)} %bitcast.43), channel_id=1, source_target_pairs={{0,3},{1,0},{2,1},{3,2},{4,7},{5,4},{6,5},{7,6},{8,11},{9,8},{10,9... | collective-permute-start | bytes 1572872 | tf_op jit(solution)/shard_map/ppermute | solution.py:75
  79.4 1.8 %copy-start.2 = (bf16[2048,512]{1,0:T(8,128)(2,1)S(1)}, bf16[2048,512]{1,0:T(8,128)(2,1)}, u32[]{:S(2)}) copy-start(bf16[2048,512]{1,0:T(8,128)(2,1)} %param.13) | copy-start | bytes 6291460
  80.0 6.5 %copy-start.1 = (f32[512,512]{0,1:T(8,128)}, f32[512,512]{0,1:T(8,128)S(1)}, u32[]{:S(2)}) copy-start(f32[512,512]{0,1:T(8,128)S(1)} %convolution_add_fusion) | copy-start | bytes 3145732
  89.2 26.6 %all-to-all-start.1 = ((bf16[128,4,512]{2,1,0:T(4,128)(2,1)}), bf16[128,4,512]{2,1,0:T(4,128)(2,1)S(1)}, u32[]{:S(2)}, u32[]{:S(2)}) async-start(bf16[128,4,512]{2,1,0:T(4,128)(2,1)} %fusion.15), calls=%async_computation.1 | async-start | bytes 1048576 | tf_op jit(solution)/shard_map/all_to_all | solution.py:220
  116.7 4.4 %copy-start.3 = (bf16[512,2048]{1,0:T(8,128)(2,1)S(1)}, bf16[512,2048]{1,0:T(8,128)(2,1)}, u32[]{:S(2)}) copy-start(bf16[512,2048]{1,0:T(8,128)(2,1)} %param.15) | copy-start | bytes 6291460
  121.5 15.8 %collective-permute-start.5 = (bf16[256,512]{1,0:T(8,128)(2,1)S(1)}, bf16[256,512]{1,0:T(8,128)(2,1)S(1)}, u32[]{:S(2)}, u32[]{:S(2)}) collective-permute-start(bf16[256,512]{1,0:T(8,128)(2,1)S(1)} %convolution_convert_fusion.3), channel_id=1, source_target_pairs={{0,3},{1,0},{2,1},{3,2},{4,7},{5,4},{6,5},{7,6},{8,11},{9,8},{10,9... | collective-permute-start | bytes 786440 | tf_op jit(solution)/shard_map/ppermute | solution.py:123
  125.7 11.5 %collective-permute-start.4 = (bf16[256,512]{1,0:T(8,128)(2,1)S(1)}, bf16[256,512]{1,0:T(8,128)(2,1)S(1)}, u32[]{:S(2)}, u32[]{:S(2)}) collective-permute-start(bf16[256,512]{1,0:T(8,128)(2,1)S(1)} %convolution_convert_fusion.4), channel_id=1, source_target_pairs={{0,2},{1,3},{2,0},{3,1},{4,6},{5,7},{6,4},{7,5},{8,10},{9,11},{10,... | collective-permute-start | bytes 786440 | tf_op jit(solution)/shard_map/ppermute | solution.py:123
  129.2 13.9 %collective-permute-start.3 = (bf16[256,512]{1,0:T(8,128)(2,1)S(1)}, bf16[256,512]{1,0:T(8,128)(2,1)S(1)}, u32[]{:S(2)}, u32[]{:S(2)}) collective-permute-start(bf16[256,512]{1,0:T(8,128)(2,1)S(1)} %convolution_convert_fusion.5), channel_id=1, source_target_pairs={{0,1},{1,2},{2,3},{3,0},{4,5},{5,6},{6,7},{7,4},{8,9},{9,10},{10,1... | collective-permute-start | bytes 786440 | tf_op jit(solution)/shard_map/ppermute | solution.py:123

commit v7 on v6

--- a/solution.py
+++ b/solution.py
@@ -8,6 +8,7 @@
 HD = 256
 SLOTS_DEV = 2
 MAXLEN = 512
+FILLED = 28672
 
 
 EPSILON = 1e-06
@@ -224,7 +225,13 @@
     local_attention = lax.dot_general(
         select, flattened, (((0,), (0,)), ((), ())), preferred_element_type=jnp.float32
     ).astype(jnp.bfloat16)
-    attended = ring_output(local_attention, output_weight, "tensor")
+    filled_rows = min(-(-FILLED // source_count), local_rows)
+    attended = ring_output(local_attention[:filled_rows], output_weight, "tensor")
+    if filled_rows < local_rows:
+        attended = jnp.concatenate(
+            [attended, jnp.zeros((local_rows - filled_rows, attended.shape[1]), attended.dtype)],
+            axis=0,
+        )
     all_cached = jnp.concatenate(cached_chunks, axis=0)
     slot_ids = jnp.arange(SLOTS_DEV, dtype=jnp.int32)
     cache_table = jnp.where(

time: 145 us -> 143 us (0.986)
  transfers between devices with their start and end apart: 8 -> 8, of which waited for: 6 -> 7; matrix products, arithmetic and copies ran while one was open for 7% -> 7% of each run, Pallas kernels for 0% -> 0%
where the time goes in v7:
time: 143 us
  waiting for transfers between devices  59.6 us (42%)
  starting transfers between devices  44.6 us (31%)
  matrix products  14.6 us (10%)
  other arithmetic  11.8 us (8%)
  local copies, waits for them, and re-layouts  8.88 us (6%)
  between operations  3.1 us (2%)
    all_to_all x1, starting transfers between devices, body(): lax.all_to_all(picked[:, chunk * chunk_slots:(chunk + 1) * chunk_slots],...  18.4 us
    all_to_all x1, waiting for transfers between devices, body(): lax.all_to_all(picked[:, chunk * chunk_slots:(chunk + 1) * chunk_slots],...  17.4 us
    ppermute x3, waiting for transfers between devices, ring_blocks(): blocks.append(lax.ppermute(narrow, axis_name, perm))  16.6 us
    all_to_all x1, waiting for transfers between devices, body(): lax.all_to_all(outgoing, 'seq', split_axis=0, concat_axis=0, tiled=True)  16.3 us
    ppermute x3, starting transfers between devices, ring_blocks(): blocks.append(lax.ppermute(narrow, axis_name, perm))  10.7 us
    ppermute x3, starting transfers between devices, ring_output(): total = total + lax.ppermute(part, axis_name, perm).astype(jnp.float32)  9.61 us
    ppermute x3, waiting for transfers between devices, ring_output(): total = total + lax.ppermute(part, axis_name, perm).astype(jnp.float32)  9.39 us
    all_to_all x1, starting transfers between devices, body(): lax.all_to_all(outgoing, 'seq', split_axis=0, concat_axis=0, tiled=True)  5.86 us
  transfers between devices with their start and end apart: 8, of which 7 were waited for; matrix products, arithmetic and copies ran while one was open for 7% of the time, Pallas kernels for 0%

profile of v7, /device:TPU:1, one launch (start us, length us, event | category | flops | bytes accessed | tf_op | source)
XLA Modules:
  0.0 142.6 jit_solution(8221420421316989624)
XLA Ops:
  4.0 1.3 convolution_convert_fusion
  6.2 18.4 %all-to-all-start = ((bf16[128,4,512]{2,1,0:T(4,128)(2,1)}), bf16[128,4,512]{2,1,0:T(4,128)(2,1)S(1)}, u32[]{:S(2)}, u32[]{:S(2)}) async-start(bf16[128,4,512]{2,1,0:T(4,128)(2,1)} %reshape.253), calls=%async_computation | async-start | bytes 1048576 | tf_op jit(solution)/shard_map/all_to_all | solution.py:182
  27.8 17.4 %all-to-all-done = bf16[128,4,512]{2,1,0:T(4,128)(2,1)S(1)} async-done(((bf16[128,4,512]{2,1,0:T(4,128)(2,1)}), bf16[128,4,512]{2,1,0:T(4,128)(2,1)S(1)}, u32[]{:S(2)}, u32[]{:S(2)}) %all-to-all-start) | async-done | bytes 524320 | tf_op jit(solution)/shard_map/all_to_all | solution.py:182
  45.8 3.1 %collective-permute-start.2 = (bf16[512,512]{1,0:T(8,128)(2,1)S(1)}, bf16[512,512]{1,0:T(8,128)(2,1)S(1)}, u32[]{:S(2)}, u32[]{:S(2)}) collective-permute-start(bf16[512,512]{1,0:T(8,128)(2,1)S(1)} %bitcast.37), channel_id=1, source_target_pairs={{0,1},{1,2},{2,3},{3,0},{4,5},{5,6},{6,7},{7,4},{8,9},{9,10},{10,1... | collective-permute-start | bytes 1572872 | tf_op jit(solution)/shard_map/ppermute | solution.py:76
  48.9 4.4 %collective-permute-start.1 = (bf16[512,512]{1,0:T(8,128)(2,1)S(1)}, bf16[512,512]{1,0:T(8,128)(2,1)}, u32[]{:S(2)}, u32[]{:S(2)}) collective-permute-start(bf16[512,512]{1,0:T(8,128)(2,1)S(1)} %bitcast.38), channel_id=1, source_target_pairs={{0,2},{1,3},{2,0},{3,1},{4,6},{5,7},{6,4},{7,5},{8,10},{9,11},{10,... | collective-permute-start | bytes 1572872 | tf_op jit(solution)/shard_map/ppermute | solution.py:76
  54.2 3.2 %collective-permute-start = (bf16[512,512]{1,0:T(8,128)(2,1)S(1)}, bf16[512,512]{1,0:T(8,128)(2,1)S(1)}, u32[]{:S(2)}, u32[]{:S(2)}) collective-permute-start(bf16[512,512]{1,0:T(8,128)(2,1)S(1)} %bitcast.39), channel_id=1, source_target_pairs={{0,3},{1,0},{2,1},{3,2},{4,7},{5,4},{6,5},{7,6},{8,11},{9,8},{10,9... | collective-permute-start | bytes 1572872 | tf_op jit(solution)/shard_map/ppermute | solution.py:76
  58.4 4.4 %collective-permute-done.2 = bf16[512,512]{1,0:T(8,128)(2,1)S(1)} collective-permute-done((bf16[512,512]{1,0:T(8,128)(2,1)S(1)}, bf16[512,512]{1,0:T(8,128)(2,1)S(1)}, u32[]{:S(2)}, u32[]{:S(2)}) %collective-permute-start.2) | collective-permute-done | bytes 524320 | tf_op jit(solution)/shard_map/ppermute | solution.py:76
  63.0 12.1 %collective-permute-done.1 = bf16[512,512]{1,0:T(8,128)(2,1)} collective-permute-done((bf16[512,512]{1,0:T(8,128)(2,1)S(1)}, bf16[512,512]{1,0:T(8,128)(2,1)}, u32[]{:S(2)}, u32[]{:S(2)}) %collective-permute-start.1) | collective-permute-done | bytes 524320 | tf_op jit(solution)/shard_map/ppermute | solution.py:76
  75.1 1.2 fusion.6
  77.8 1.6 %convolution_add_fusion.1 = f32[512,512]{0,1:T(8,128)S(1)} fusion(f32[512,512]{0,1:T(8,128)S(1)} %convolution_add_fusion.2, bf16[2048,512]{1,0:T(8,128)(2,1)S(1)} %copy-done, s32[]{:T(128)S(6)} %select_n.110, bf16[512,512]{1,0:T(8,128)(2,1)} %collective-permute-done.1, f32[512]{0:T(512)S(1)} %get-tuple-element.18, f32[512]{0:T(512)S(1)} %fusion.73), kind=kOutput, calls=%fused_computation.1 | convolution fusion | flops 269746176 | bytes 3149828 | tf_op jit(solution)/shard_map/dot_general | solution.py:98
  80.1 1.2 fusion.40
  82.5 1.6 %convolution_add_fusion.4 = f32[512,512]{0,1:T(8,128)S(1)} fusion(f32[512,512]{0,1:T(8,128)S(1)} %convolution_add_fusion.5, bf16[2048,512]{1,0:T(8,128)(2,1)S(1)} %copy-done.3, s32[]{:T(128)S(6)} %select_n.110, bf16[512,512]{1,0:T(8,128)(2,1)} %collective-permute-done.1, f32[512]{0:T(512)S(1)} %get-tuple-element.18, f32[512]{0:T(512)S(1)} %fusion.73), kind=kOutput, calls=%fused_computation.4 | convolution fusion | flops 269746176 | bytes 3149828 | tf_op jit(solution)/shard_map/dot_general | solution.py:93
  87.6 1.7 %fusion.15 = bf16[128,4,512]{2,1,0:T(4,128)(2,1)} fusion(s32[]{:T(128)S(6)} %select_n.122, bf16[128,4,512]{2,1,0:T(4,128)(2,1)S(1)} %bitcast.43), kind=kLoop, calls=%fused_computation.48 | loop fusion | flops 262144 | bytes 1048580 | tf_op jit(solution)/shard_map/jit(_roll_dynamic)/concatenate | solution.py:68
  89.2 5.9 %all-to-all-start.1 = ((bf16[128,4,512]{2,1,0:T(4,128)(2,1)}), bf16[128,4,512]{2,1,0:T(4,128)(2,1)S(1)}, u32[]{:S(2)}, u32[]{:S(2)}) async-start(bf16[128,4,512]{2,1,0:T(4,128)(2,1)} %fusion.15), calls=%async_computation.1 | async-start | bytes 1048576 | tf_op jit(solution)/shard_map/all_to_all | solution.py:221
  98.3 1.3 copy.25
  99.6 16.3 %all-to-all-done.1 = bf16[128,4,512]{2,1,0:T(4,128)(2,1)S(1)} async-done(((bf16[128,4,512]{2,1,0:T(4,128)(2,1)}), bf16[128,4,512]{2,1,0:T(4,128)(2,1)S(1)}, u32[]{:S(2)}, u32[]{:S(2)}) %all-to-all-start.1) | async-done | bytes 524320 | tf_op jit(solution)/shard_map/all_to_all | solution.py:221
  116.7 1.7 %fusion.32 = bf16[256,512]{1,0:T(8,128)(2,1)S(1)} fusion(bf16[512,512]{1,0:T(8,128)(2,1)} %reshape.258, s32[512]{0:T(512)S(1)} %add.189, pred[512]{0:T(512)(128)(4,1)S(1)} %compare_and_fusion), kind=kOutput, calls=%fused_computation.73 | convolution fusion | flops 134479872 | bytes 788992 | tf_op jit(solution)/shard_map/dot_general | solution.py:225
  118.4 1.3 convolution_convert_fusion.3
  119.8 1.3 convolution_convert_fusion.4
  121.4 4.3 %collective-permute-start.5 = (bf16[224,512]{1,0:T(8,128)(2,1)S(1)}, bf16[224,512]{1,0:T(8,128)(2,1)S(1)}, u32[]{:S(2)}, u32[]{:S(2)}) collective-permute-start(bf16[224,512]{1,0:T(8,128)(2,1)S(1)} %convolution_convert_fusion.3), channel_id=1, source_target_pairs={{0,3},{1,0},{2,1},{3,2},{4,7},{5,4},{6,5},{7,6},{8,11},{9,8},{10,9... | collective-permute-start | bytes 688136 | tf_op jit(solution)/shard_map/ppermute | solution.py:124
  125.7 3.4 %collective-permute-start.4 = (bf16[224,512]{1,0:T(8,128)(2,1)S(1)}, bf16[224,512]{1,0:T(8,128)(2,1)S(1)}, u32[]{:S(2)}, u32[]{:S(2)}) collective-permute-start(bf16[224,512]{1,0:T(8,128)(2,1)S(1)} %convolution_convert_fusion.4), channel_id=1, source_target_pairs={{0,2},{1,3},{2,0},{3,1},{4,6},{5,7},{6,4},{7,5},{8,10},{9,11},{10,... | collective-permute-start | bytes 688136 | tf_op jit(solution)/shard_map/ppermute | solution.py:124
  129.1 1.9 %collective-permute-start.3 = (bf16[224,512]{1,0:T(8,128)(2,1)S(1)}, bf16[224,512]{1,0:T(8,128)(2,1)S(1)}, u32[]{:S(2)}, u32[]{:S(2)}) collective-permute-start(bf16[224,512]{1,0:T(8,128)(2,1)S(1)} %convolution_convert_fusion.5), channel_id=1, source_target_pairs={{0,1},{1,2},{2,3},{3,0},{4,5},{5,6},{6,7},{7,4},{8,9},{9,10},{10,1... | collective-permute-start | bytes 688136 | tf_op jit(solution)/shard_map/ppermute | solution.py:124
  132.2 3.6 %collective-permute-done.5 = bf16[224,512]{1,0:T(8,128)(2,1)S(1)} collective-permute-done((bf16[224,512]{1,0:T(8,128)(2,1)S(1)}, bf16[224,512]{1,0:T(8,128)(2,1)S(1)}, u32[]{:S(2)}, u32[]{:S(2)}) %collective-permute-start.5) | collective-permute-done | bytes 229408 | tf_op jit(solution)/shard_map/ppermute | solution.py:124
  136.4 5.2 %collective-permute-done.3 = bf16[224,512]{1,0:T(8,128)(2,1)S(1)} collective-permute-done((bf16[224,512]{1,0:T(8,128)(2,1)S(1)}, bf16[224,512]{1,0:T(8,128)(2,1)S(1)}, u32[]{:S(2)}, u32[]{:S(2)}) %collective-permute-start.3) | collective-permute-done | bytes 229408 | tf_op jit(solution)/shard_map/ppermute | solution.py:124
  (66 shorter events, 21.6 us)
Async XLA Ops:
  0.6 75.9 %copy-start = (bf16[2048,512]{1,0:T(8,128)(2,1)S(1)}, bf16[2048,512]{1,0:T(8,128)(2,1)}, u32[]{:S(2)}) copy-start(bf16[2048,512]{1,0:T(8,128)(2,1)} %param.14) | copy-start | bytes 6291460
  5.3 48.8 %copy-start.4 = (bf16[2048]{0:T(1024)(128)(2,1)S(1)}, bf16[2048]{0:T(1024)(128)(2,1)}, u32[]{:S(2)}) copy-start(bf16[2048]{0:T(1024)(128)(2,1)} %param.12) | copy-start | bytes 12292
  6.2 39.0 %all-to-all-start = ((bf16[128,4,512]{2,1,0:T(4,128)(2,1)}), bf16[128,4,512]{2,1,0:T(4,128)(2,1)S(1)}, u32[]{:S(2)}, u32[]{:S(2)}) async-start(bf16[128,4,512]{2,1,0:T(4,128)(2,1)} %reshape.253), calls=%async_computation | async-start | bytes 1048576 | tf_op jit(solution)/shard_map/all_to_all | solution.py:182
  45.8 17.0 %collective-permute-start.2 = (bf16[512,512]{1,0:T(8,128)(2,1)S(1)}, bf16[512,512]{1,0:T(8,128)(2,1)S(1)}, u32[]{:S(2)}, u32[]{:S(2)}) collective-permute-start(bf16[512,512]{1,0:T(8,128)(2,1)S(1)} %bitcast.37), channel_id=1, source_target_pairs={{0,1},{1,2},{2,3},{3,0},{4,5},{5,6},{6,7},{7,4},{8,9},{9,10},{10,1... | collective-permute-start | bytes 1572872 | tf_op jit(solution)/shard_map/ppermute | solution.py:76
  48.9 26.2 %collective-permute-start.1 = (bf16[512,512]{1,0:T(8,128)(2,1)S(1)}, bf16[512,512]{1,0:T(8,128)(2,1)}, u32[]{:S(2)}, u32[]{:S(2)}) collective-permute-start(bf16[512,512]{1,0:T(8,128)(2,1)S(1)} %bitcast.38), channel_id=1, source_target_pairs={{0,2},{1,3},{2,0},{3,1},{4,6},{5,7},{6,4},{7,5},{8,10},{9,11},{10,... | collective-permute-start | bytes 1572872 | tf_op jit(solution)/shard_map/ppermute | solution.py:76
  54.2 22.2 %collective-permute-start = (bf16[512,512]{1,0:T(8,128)(2,1)S(1)}, bf16[512,512]{1,0:T(8,128)(2,1)S(1)}, u32[]{:S(2)}, u32[]{:S(2)}) collective-permute-start(bf16[512,512]{1,0:T(8,128)(2,1)S(1)} %bitcast.39), channel_id=1, source_target_pairs={{0,3},{1,0},{2,1},{3,2},{4,7},{5,4},{6,5},{7,6},{8,11},{9,8},{10,9... | collective-permute-start | bytes 1572872 | tf_op jit(solution)/shard_map/ppermute | solution.py:76
  79.4 1.8 %copy-start.3 = (bf16[2048,512]{1,0:T(8,128)(2,1)S(1)}, bf16[2048,512]{1,0:T(8,128)(2,1)}, u32[]{:S(2)}) copy-start(bf16[2048,512]{1,0:T(8,128)(2,1)} %param.13) | copy-start | bytes 6291460
  80.0 6.5 %copy-start.1 = (f32[512,512]{0,1:T(8,128)}, f32[512,512]{0,1:T(8,128)S(1)}, u32[]{:S(2)}) copy-start(f32[512,512]{0,1:T(8,128)S(1)} %convolution_add_fusion) | copy-start | bytes 3145732
  89.2 26.6 %all-to-all-start.1 = ((bf16[128,4,512]{2,1,0:T(4,128)(2,1)}), bf16[128,4,512]{2,1,0:T(4,128)(2,1)S(1)}, u32[]{:S(2)}, u32[]{:S(2)}) async-start(bf16[128,4,512]{2,1,0:T(4,128)(2,1)} %fusion.15), calls=%async_computation.1 | async-start | bytes 1048576 | tf_op jit(solution)/shard_map/all_to_all | solution.py:221
  116.7 4.4 %copy-start.2 = (bf16[512,2048]{1,0:T(8,128)(2,1)S(1)}, bf16[512,2048]{1,0:T(8,128)(2,1)}, u32[]{:S(2)}) copy-start(bf16[512,2048]{1,0:T(8,128)(2,1)} %param.15) | copy-start | bytes 6291460
  121.4 14.4 %collective-permute-start.5 = (bf16[224,512]{1,0:T(8,128)(2,1)S(1)}, bf16[224,512]{1,0:T(8,128)(2,1)S(1)}, u32[]{:S(2)}, u32[]{:S(2)}) collective-permute-start(bf16[224,512]{1,0:T(8,128)(2,1)S(1)} %convolution_convert_fusion.3), channel_id=1, source_target_pairs={{0,3},{1,0},{2,1},{3,2},{4,7},{5,4},{6,5},{7,6},{8,11},{9,8},{10,9... | collective-permute-start | bytes 688136 | tf_op jit(solution)/shard_map/ppermute | solution.py:124
  125.7 10.7 %collective-permute-start.4 = (bf16[224,512]{1,0:T(8,128)(2,1)S(1)}, bf16[224,512]{1,0:T(8,128)(2,1)S(1)}, u32[]{:S(2)}, u32[]{:S(2)}) collective-permute-start(bf16[224,512]{1,0:T(8,128)(2,1)S(1)} %convolution_convert_fusion.4), channel_id=1, source_target_pairs={{0,2},{1,3},{2,0},{3,1},{4,6},{5,7},{6,4},{7,5},{8,10},{9,11},{10,... | collective-permute-start | bytes 688136 | tf_op jit(solution)/shard_map/ppermute | solution.py:124
  129.1 12.5 %collective-permute-start.3 = (bf16[224,512]{1,0:T(8,128)(2,1)S(1)}, bf16[224,512]{1,0:T(8,128)(2,1)S(1)}, u32[]{:S(2)}, u32[]{:S(2)}) collective-permute-start(bf16[224,512]{1,0:T(8,128)(2,1)S(1)} %convolution_convert_fusion.5), channel_id=1, source_target_pairs={{0,1},{1,2},{2,3},{3,0},{4,5},{5,6},{6,7},{7,4},{8,9},{9,10},{10,1... | collective-permute-start | bytes 688136 | tf_op jit(solution)/shard_map/ppermute | solution.py:124

commit v8 on v7

--- a/solution.py
+++ b/solution.py
@@ -16,12 +16,12 @@
 CHUNKS = 1
 
 
-def rotate_rows(values, head_size, first_pos):
+def rotate_rows(values, head_size, row_pos):
     row_count = values.shape[0]
     shaped = values.reshape(row_count, -1, head_size)
     half_size = head_size // 2
     frequency = ROPE_BASE ** (jnp.arange(half_size, dtype=jnp.float32) * (-2.0 / head_size))
-    positions = (first_pos + jnp.arange(row_count, dtype=jnp.int32)).astype(jnp.float32)
+    positions = row_pos.astype(jnp.float32)
     angles = positions[:, None] * frequency[None, :]
     cosine_table = jnp.cos(angles)[:, None, :]
     sine_table = jnp.sin(angles)[:, None, :]
@@ -43,14 +43,11 @@
     return (widened * inverse_rms * gain.astype(jnp.float32)).astype(jnp.bfloat16)
 
 
-def attend(query_block, start_row, key_rows, value_rows, length):
-    row_count = query_block.shape[0]
+def attend(query_block, query_pos, key_rows, key_pos, value_rows, length):
     scores = jnp.dot(query_block, key_rows.T, preferred_element_type=jnp.float32) * key_rows.shape[
         1
     ] ** (-0.5)
-    query_pos = start_row + jnp.arange(row_count, dtype=jnp.int32)[:, None]
-    key_pos = jnp.arange(key_rows.shape[0], dtype=jnp.int32)[None, :]
-    allowed = (key_pos <= query_pos) & (key_pos < length)
+    allowed = (key_pos[None, :] <= query_pos[:, None]) & (key_pos[None, :] < length)
     scores = jnp.where(allowed, scores, -jnp.inf)
     row_top = jnp.max(scores, axis=-1, keepdims=True)
     powered = jnp.exp(scores - row_top)
@@ -177,6 +174,7 @@
     value_chunks = []
     cached_chunks = []
     returned_chunks = []
+    pos_chunks = []
     for chunk in range(CHUNKS):
         chunk_first = chunk * chunk_rows
         arrived = lax.all_to_all(
@@ -186,16 +184,22 @@
             concat_axis=0,
             tiled=True,
         )
-        narrow_rows = to_request(arrived, shift_by)
+        narrow_rows = arrived.reshape(-1, arrived.shape[2])
+        source_ids = jnp.arange(source_count, dtype=jnp.int32)
+        chunk_pos = (
+            (source_ids[:, None] - shift_by) % source_count
+            + (chunk * chunk_slots + jnp.arange(chunk_slots, dtype=jnp.int32))[None, :] * source_count
+        ).reshape(-1)
+        pos_chunks.append(chunk_pos)
         queries, keyvals = project_blocks(
             ring_blocks(narrow_rows, "tensor"), norm_gain, query_weight, keyval_weight, "tensor"
         )
-        rotated_query = rotate_rows(queries, HD, chunk_first).astype(jnp.bfloat16)
+        rotated_query = rotate_rows(queries, HD, chunk_pos).astype(jnp.bfloat16)
         own_blocks = []
         for block_index in range(block_count):
             plain_block = keyvals[:, block_index * HD : (block_index + 1) * HD]
             if block_index % 2 == 0:
-                own_blocks.append(rotate_rows(plain_block, HD, chunk_first).astype(jnp.bfloat16))
+                own_blocks.append(rotate_rows(plain_block, HD, chunk_pos).astype(jnp.bfloat16))
             else:
                 own_blocks.append(plain_block.astype(jnp.bfloat16))
         own_cached = jnp.concatenate(own_blocks, axis=1)
@@ -209,14 +213,15 @@
             head_outputs.append(
                 attend(
                     rotated_query[:, head_index * HD : (head_index + 1) * HD],
-                    chunk_first,
+                    chunk_pos,
                     key_rows,
+                    jnp.concatenate(pos_chunks, axis=0),
                     value_rows,
                     own_length,
                 )
             )
         attention_rows = jnp.concatenate(head_outputs, axis=1)
-        outgoing = from_request(attention_rows, shift_by, source_count)
+        outgoing = attention_rows.reshape(source_count, chunk_slots, attention_rows.shape[1])
         returned_chunks.append(
             lax.all_to_all(outgoing, "seq", split_axis=0, concat_axis=0, tiled=True)
         )
@@ -232,7 +237,12 @@
             [attended, jnp.zeros((local_rows - filled_rows, attended.shape[1]), attended.dtype)],
             axis=0,
         )
-    all_cached = jnp.concatenate(cached_chunks, axis=0)
+    all_cached = to_request(
+        jnp.concatenate(
+            [block.reshape(source_count, chunk_slots, -1) for block in cached_chunks], axis=1
+        ),
+        shift_by,
+    )
     slot_ids = jnp.arange(SLOTS_DEV, dtype=jnp.int32)
     cache_table = jnp.where(
         (slot_ids == own_slot)[:, None, None], all_cached[None], jnp.zeros((), jnp.bfloat16)

time: 143 us -> 151 us (1.056)
  matrix products: 14.6 us -> 19.1 us
  other arithmetic: 11.8 us -> 14.1 us
  local copies, waits for them, and re-layouts: 8.88 us -> 11 us
  waiting for transfers between devices: 59.6 us -> 57.9 us
    dot_general x4, matrix products: 3.41 us -> 5.65 us  [project_blocks(): jnp.dot(normed, lax.dynamic_slice_in_dim(keyval_weight, first, width, 0),...]
    dot_general x4, matrix products: 3.42 us -> 5.52 us  [project_blocks(): jnp.dot(normed, lax.dynamic_slice_in_dim(query_weight, first, width, 0),...]
    reduce_sum x4, other arithmetic: 2.07 us -> 3.99 us  [project_blocks(): jnp.sum(block * block, axis=-1, keepdims=True)]
    concatenate x1 -> x0, other arithmetic: 1.66 us -> none  [from_request(): return jnp.roll(jnp.swapaxes(shaped, 0, 1), shift_by, axis=0)]
    reshape x2 -> x3, local copies, waits for them, and re-layouts: 0.67 us -> 2.2 us  [the longest x1 1.17 us: body(): block.reshape(source_count, chunk_slots, -1)]
  transfers between devices with their start and end apart: 8 -> 8, of which waited for: 7 -> 8; matrix products, arithmetic and copies ran while one was open for 7% -> 9% of each run, Pallas kernels for 0% -> 0%
where the time goes in v8:
time: 151 us; the launch traced here: 150 us
  waiting for transfers between devices  57.9 us (38%)
  starting transfers between devices  44.6 us (30%)
  matrix products  19.1 us (13%)
  other arithmetic  14.1 us (9%)
  local copies, waits for them, and re-layouts  11 us (7%)
  between operations  3.23 us (2%)
    all_to_all x1, starting transfers between devices, body(): lax.all_to_all(picked[:, chunk * chunk_slots:(chunk + 1) * chunk_slots],...  18.4 us
    all_to_all x1, waiting for transfers between devices, body(): lax.all_to_all(picked[:, chunk * chunk_slots:(chunk + 1) * chunk_slots],...  17.8 us
    ppermute x3, waiting for transfers between devices, ring_blocks(): blocks.append(lax.ppermute(narrow, axis_name, perm))  15.7 us
    all_to_all x1, waiting for transfers between devices, body(): lax.all_to_all(outgoing, 'seq', split_axis=0, concat_axis=0, tiled=True)  15.1 us
    ppermute x3, starting transfers between devices, ring_blocks(): blocks.append(lax.ppermute(narrow, axis_name, perm))  10.7 us
    ppermute x3, starting transfers between devices, ring_output(): total = total + lax.ppermute(part, axis_name, perm).astype(jnp.float32)  9.65 us
    ppermute x3, waiting for transfers between devices, ring_output(): total = total + lax.ppermute(part, axis_name, perm).astype(jnp.float32)  9.35 us
    all_to_all x1, starting transfers between devices, body(): lax.all_to_all(outgoing, 'seq', split_axis=0, concat_axis=0, tiled=True)  5.88 us
  transfers between devices with their start and end apart: 8, of which 8 were waited for; matrix products, arithmetic and copies ran while one was open for 9% of the time, Pallas kernels for 0%

profile of v8, /device:TPU:1, one launch (start us, length us, event | category | flops | bytes accessed | tf_op | source)
XLA Modules:
  0.0 150.0 jit_solution(918130300683976202)
XLA Ops:
  2.5 1.4 select_reduce_fusion
  6.7 18.4 %all-to-all-start = ((bf16[128,4,512]{2,1,0:T(4,128)(2,1)}), bf16[128,4,512]{2,1,0:T(4,128)(2,1)S(1)}, u32[]{:S(2)}, u32[]{:S(2)}) async-start(bf16[128,4,512]{2,1,0:T(4,128)(2,1)} %reshape.322), calls=%async_computation | async-start | bytes 1048576 | tf_op jit(solution)/shard_map/all_to_all | solution.py:180
  28.0 17.8 %all-to-all-done = bf16[128,4,512]{2,1,0:T(4,128)(2,1)S(1)} async-done(((bf16[128,4,512]{2,1,0:T(4,128)(2,1)}), bf16[128,4,512]{2,1,0:T(4,128)(2,1)S(1)}, u32[]{:S(2)}, u32[]{:S(2)}) %all-to-all-start) | async-done | bytes 524320 | tf_op jit(solution)/shard_map/all_to_all | solution.py:180
  45.9 3.1 %collective-permute-start.2 = (bf16[512,512]{1,0:T(8,128)(2,1)S(1)}, bf16[512,512]{1,0:T(8,128)(2,1)}, u32[]{:S(2)}, u32[]{:S(2)}) collective-permute-start(bf16[512,512]{1,0:T(8,128)(2,1)S(1)} %reshape.323), channel_id=1, source_target_pairs={{0,1},{1,2},{2,3},{3,0},{4,5},{5,6},{6,7},{7,4},{8,9},{9,10},{10,1... | collective-permute-start | bytes 1572872 | tf_op jit(solution)/shard_map/ppermute | solution.py:73
  49.0 1.8 %multiply_cosine_fusion.1 = (f32[512,128]{0,1:T(8,128)S(1)}, f32[512,128]{0,1:T(8,128)}) fusion(f32[128]{0:T(128)S(1)} %multiply_power_fusion, f32[512]{0:T(512)S(1)} %convert_element_type.116), kind=kLoop, calls=%fused_computation.76 | loop fusion | flops 65536 | bytes 526848 | tf_op jit(solution)/shard_map/cos | solution.py:26
  51.4 4.3 %collective-permute-start.1 = (bf16[512,512]{1,0:T(8,128)(2,1)S(1)}, bf16[512,512]{1,0:T(8,128)(2,1)}, u32[]{:S(2)}, u32[]{:S(2)}) collective-permute-start(bf16[512,512]{1,0:T(8,128)(2,1)S(1)} %reshape.323), channel_id=1, source_target_pairs={{0,2},{1,3},{2,0},{3,1},{4,6},{5,7},{6,4},{7,5},{8,10},{9,11},{10,... | collective-permute-start | bytes 1572872 | tf_op jit(solution)/shard_map/ppermute | solution.py:73
  56.9 3.2 %collective-permute-start = (bf16[512,512]{1,0:T(8,128)(2,1)S(1)}, bf16[512,512]{1,0:T(8,128)(2,1)}, u32[]{:S(2)}, u32[]{:S(2)}) collective-permute-start(bf16[512,512]{1,0:T(8,128)(2,1)S(1)} %reshape.323), channel_id=1, source_target_pairs={{0,3},{1,0},{2,1},{3,2},{4,7},{5,4},{6,5},{7,6},{8,11},{9,8},{10,9... | collective-permute-start | bytes 1572872 | tf_op jit(solution)/shard_map/ppermute | solution.py:73
  60.7 2.3 %collective-permute-done.2 = bf16[512,512]{1,0:T(8,128)(2,1)} collective-permute-done((bf16[512,512]{1,0:T(8,128)(2,1)S(1)}, bf16[512,512]{1,0:T(8,128)(2,1)}, u32[]{:S(2)}, u32[]{:S(2)}) %collective-permute-start.2) | collective-permute-done | bytes 524320 | tf_op jit(solution)/shard_map/ppermute | solution.py:73
  64.2 11.0 %collective-permute-done.1 = bf16[512,512]{1,0:T(8,128)(2,1)} collective-permute-done((bf16[512,512]{1,0:T(8,128)(2,1)S(1)}, bf16[512,512]{1,0:T(8,128)(2,1)}, u32[]{:S(2)}, u32[]{:S(2)}) %collective-permute-start.1) | collective-permute-done | bytes 524320 | tf_op jit(solution)/shard_map/ppermute | solution.py:73
  76.4 2.4 %collective-permute-done = bf16[512,512]{1,0:T(8,128)(2,1)} collective-permute-done((bf16[512,512]{1,0:T(8,128)(2,1)S(1)}, bf16[512,512]{1,0:T(8,128)(2,1)}, u32[]{:S(2)}, u32[]{:S(2)}) %collective-permute-start) | collective-permute-done | bytes 524320 | tf_op jit(solution)/shard_map/ppermute | solution.py:73
  80.7 1.6 %convolution_add_fusion.2 = f32[512,512]{0,1:T(8,128)S(1)} fusion(f32[512,512]{0,1:T(8,128)S(1)} %fusion.23, bf16[2048,512]{1,0:T(8,128)(2,1)S(1)} %copy-done, s32[]{:T(128)S(6)} %select_n.123, bf16[512,512]{1,0:T(8,128)(2,1)} %collective-permute-done, f32[512]{0:T(512)S(1)} %get-tuple-element.13, f32[512]{0:T(512)S(1)} %add_rsqrt_fusion), kind=kOutput, calls=%fused_computation.2 | convolution fusion | flops 269746176 | bytes 3149828 | tf_op jit(solution)/shard_map/dot_general | solution.py:95
  82.3 1.6 %convolution_add_fusion.1 = f32[512,512]{0,1:T(8,128)S(1)} fusion(f32[512,512]{0,1:T(8,128)S(1)} %convolution_add_fusion.2, bf16[2048,512]{1,0:T(8,128)(2,1)S(1)} %copy-done, s32[]{:T(128)S(6)} %select_n.125, bf16[512,512]{1,0:T(8,128)(2,1)} %collective-permute-done.1, f32[512]{0:T(512)S(1)} %get-tuple-element.15, f32[512]{0:T(512)S(1)} %add_rsqrt_fusion), kind=kOutput, calls=%fused_computation.1 | convolution fusion | flops 269746176 | bytes 3149828 | tf_op jit(solution)/shard_map/dot_general | solution.py:95
  84.0 1.8 %convolution_add_fusion = f32[512,512]{0,1:T(8,128)S(1)} fusion(f32[512,512]{0,1:T(8,128)S(1)} %convolution_add_fusion.1, bf16[2048,512]{1,0:T(8,128)(2,1)S(1)} %copy-done, s32[]{:T(128)S(6)} %select_n.127, bf16[512,512]{1,0:T(8,128)(2,1)} %collective-permute-done.2, f32[512]{0:T(512)S(1)} %get-tuple-element.12, f32[512]{0:T(512)S(1)} %add_rsqrt_fusion), kind=kOutput, calls=%fused_computation | convolution fusion | flops 269746176 | bytes 3149828 | tf_op jit(solution)/shard_map/dot_general | solution.py:95
  87.7 1.6 %convolution_add_fusion.5 = f32[512,512]{0,1:T(8,128)S(1)} fusion(f32[512,512]{0,1:T(8,128)S(1)} %fusion.28, bf16[2048,512]{1,0:T(8,128)(2,1)S(1)} %copy-done.3, s32[]{:T(128)S(6)} %select_n.123, bf16[512,512]{1,0:T(8,128)(2,1)} %collective-permute-done, f32[512]{0:T(512)S(1)} %copy-done.12, f32[512]{0:T(512)S(1)} %add_rsqrt_fusion), kind=kOutput, calls=%fused_computation.5 | convolution fusion | flops 269746176 | bytes 3149828 | tf_op jit(solution)/shard_map/dot_general | solution.py:90
  89.3 1.6 %convolution_add_fusion.4 = f32[512,512]{0,1:T(8,128)S(1)} fusion(f32[512,512]{0,1:T(8,128)S(1)} %convolution_add_fusion.5, bf16[2048,512]{1,0:T(8,128)(2,1)S(1)} %copy-done.3, s32[]{:T(128)S(6)} %select_n.125, bf16[512,512]{1,0:T(8,128)(2,1)} %collective-permute-done.1, f32[512]{0:T(512)S(1)} %copy-done.10, f32[512]{0:T(512)S(1)} %add_rsqrt_fusion), kind=kOutput, calls=%fused_computation.4 | convolution fusion | flops 269746176 | bytes 3149828 | tf_op jit(solution)/shard_map/dot_general | solution.py:90
  91.0 1.7 %convolution_add_fusion.3 = f32[512,512]{0,1:T(8,128)S(1)} fusion(f32[512,512]{0,1:T(8,128)S(1)} %convolution_add_fusion.4, bf16[2048,512]{1,0:T(8,128)(2,1)S(1)} %copy-done.3, s32[]{:T(128)S(6)} %select_n.127, bf16[512,512]{1,0:T(8,128)(2,1)} %collective-permute-done.2, f32[512]{0:T(512)S(1)} %copy-done.8, f32[512]{0:T(512)S(1)} %add_rsqrt_fusion), kind=kOutput, calls=%fused_computation.3 | convolution fusion | flops 269746176 | bytes 3149828 | tf_op jit(solution)/shard_map/dot_general | solution.py:90
  96.6 5.9 %all-to-all-start.1 = ((bf16[128,4,512]{2,1,0:T(4,128)(2,1)}), bf16[128,4,512]{2,1,0:T(4,128)(2,1)S(1)}, u32[]{:S(2)}, u32[]{:S(2)}) async-start(bf16[128,4,512]{2,1,0:T(4,128)(2,1)} %reshape.326), calls=%async_computation.1 | async-start | bytes 1048576 | tf_op jit(solution)/shard_map/all_to_all | solution.py:226
  108.1 15.1 %all-to-all-done.1 = bf16[128,4,512]{2,1,0:T(4,128)(2,1)S(1)} async-done(((bf16[128,4,512]{2,1,0:T(4,128)(2,1)}), bf16[128,4,512]{2,1,0:T(4,128)(2,1)S(1)}, u32[]{:S(2)}, u32[]{:S(2)}) %all-to-all-start.1) | async-done | bytes 524320 | tf_op jit(solution)/shard_map/all_to_all | solution.py:226
  124.1 1.7 %fusion.31 = bf16[256,512]{1,0:T(8,128)(2,1)S(1)} fusion(bf16[512,512]{1,0:T(8,128)(2,1)} %reshape.327, s32[512]{0:T(512)S(1)} %add.234, pred[512]{0:T(512)(128)(4,1)S(1)} %copy-done.17), kind=kOutput, calls=%fused_computation.70 | convolution fusion | flops 134479872 | bytes 788992 | tf_op jit(solution)/shard_map/dot_general | solution.py:230
  128.8 4.3 %collective-permute-start.5 = (bf16[224,512]{1,0:T(8,128)(2,1)S(1)}, bf16[224,512]{1,0:T(8,128)(2,1)S(1)}, u32[]{:S(2)}, u32[]{:S(2)}) collective-permute-start(bf16[224,512]{1,0:T(8,128)(2,1)S(1)} %convolution_convert_fusion.3), channel_id=1, source_target_pairs={{0,3},{1,0},{2,1},{3,2},{4,7},{5,4},{6,5},{7,6},{8,11},{9,8},{10,9... | collective-permute-start | bytes 688136 | tf_op jit(solution)/shard_map/ppermute | solution.py:121
  133.1 3.5 %collective-permute-start.4 = (bf16[224,512]{1,0:T(8,128)(2,1)S(1)}, bf16[224,512]{1,0:T(8,128)(2,1)S(1)}, u32[]{:S(2)}, u32[]{:S(2)}) collective-permute-start(bf16[224,512]{1,0:T(8,128)(2,1)S(1)} %convolution_convert_fusion.4), channel_id=1, source_target_pairs={{0,2},{1,3},{2,0},{3,1},{4,6},{5,7},{6,4},{7,5},{8,10},{9,11},{10,... | collective-permute-start | bytes 688136 | tf_op jit(solution)/shard_map/ppermute | solution.py:121
  136.5 1.9 %collective-permute-start.3 = (bf16[224,512]{1,0:T(8,128)(2,1)S(1)}, bf16[224,512]{1,0:T(8,128)(2,1)S(1)}, u32[]{:S(2)}, u32[]{:S(2)}) collective-permute-start(bf16[224,512]{1,0:T(8,128)(2,1)S(1)} %convolution_convert_fusion.5), channel_id=1, source_target_pairs={{0,1},{1,2},{2,3},{3,0},{4,5},{5,6},{6,7},{7,4},{8,9},{9,10},{10,1... | collective-permute-start | bytes 688136 | tf_op jit(solution)/shard_map/ppermute | solution.py:121
  139.6 3.6 %collective-permute-done.5 = bf16[224,512]{1,0:T(8,128)(2,1)S(1)} collective-permute-done((bf16[224,512]{1,0:T(8,128)(2,1)S(1)}, bf16[224,512]{1,0:T(8,128)(2,1)S(1)}, u32[]{:S(2)}, u32[]{:S(2)}) %collective-permute-start.5) | collective-permute-done | bytes 229408 | tf_op jit(solution)/shard_map/ppermute | solution.py:121
  143.8 5.2 %collective-permute-done.3 = bf16[224,512]{1,0:T(8,128)(2,1)S(1)} collective-permute-done((bf16[224,512]{1,0:T(8,128)(2,1)S(1)}, bf16[224,512]{1,0:T(8,128)(2,1)S(1)}, u32[]{:S(2)}, u32[]{:S(2)}) %collective-permute-start.3) | collective-permute-done | bytes 229408 | tf_op jit(solution)/shard_map/ppermute | solution.py:121
  (103 shorter events, 30.0 us)
Async XLA Ops:
  0.6 79.4 %copy-start = (bf16[2048,512]{1,0:T(8,128)(2,1)S(1)}, bf16[2048,512]{1,0:T(8,128)(2,1)}, u32[]{:S(2)}) copy-start(bf16[2048,512]{1,0:T(8,128)(2,1)} %param.12) | copy-start | bytes 6291460
  4.5 46.3 %copy-start.16 = (pred[512]{0:T(512)(128)(4,1)}, pred[512]{0:T(512)(128)(4,1)S(1)}, u32[]{:S(2)}) copy-start(pred[512]{0:T(512)(128)(4,1)S(1)} %compare_and_fusion.1) | copy-start | bytes 1540
  5.8 54.3 %copy-start.13 = (bf16[2048]{0:T(1024)(128)(2,1)S(1)}, bf16[2048]{0:T(1024)(128)(2,1)}, u32[]{:S(2)}) copy-start(bf16[2048]{0:T(1024)(128)(2,1)} %param.10) | copy-start | bytes 12292
  6.7 39.0 %all-to-all-start = ((bf16[128,4,512]{2,1,0:T(4,128)(2,1)}), bf16[128,4,512]{2,1,0:T(4,128)(2,1)S(1)}, u32[]{:S(2)}, u32[]{:S(2)}) async-start(bf16[128,4,512]{2,1,0:T(4,128)(2,1)} %reshape.322), calls=%async_computation | async-start | bytes 1048576 | tf_op jit(solution)/shard_map/all_to_all | solution.py:180
  28.0 36.2 %copy-start.14 = (f32[128]{0:T(128)}, f32[128]{0:T(128)S(1)}, u32[]{:S(2)}) copy-start(f32[128]{0:T(128)S(1)} %multiply_power_fusion) | copy-start | bytes 1540
  45.9 17.1 %collective-permute-start.2 = (bf16[512,512]{1,0:T(8,128)(2,1)S(1)}, bf16[512,512]{1,0:T(8,128)(2,1)}, u32[]{:S(2)}, u32[]{:S(2)}) collective-permute-start(bf16[512,512]{1,0:T(8,128)(2,1)S(1)} %reshape.323), channel_id=1, source_target_pairs={{0,1},{1,2},{2,3},{3,0},{4,5},{5,6},{6,7},{7,4},{8,9},{9,10},{10,1... | collective-permute-start | bytes 1572872 | tf_op jit(solution)/shard_map/ppermute | solution.py:73
  51.4 23.8 %collective-permute-start.1 = (bf16[512,512]{1,0:T(8,128)(2,1)S(1)}, bf16[512,512]{1,0:T(8,128)(2,1)}, u32[]{:S(2)}, u32[]{:S(2)}) collective-permute-start(bf16[512,512]{1,0:T(8,128)(2,1)S(1)} %reshape.323), channel_id=1, source_target_pairs={{0,2},{1,3},{2,0},{3,1},{4,6},{5,7},{6,4},{7,5},{8,10},{9,11},{10,... | collective-permute-start | bytes 1572872 | tf_op jit(solution)/shard_map/ppermute | solution.py:73
  56.9 21.9 %collective-permute-start = (bf16[512,512]{1,0:T(8,128)(2,1)S(1)}, bf16[512,512]{1,0:T(8,128)(2,1)}, u32[]{:S(2)}, u32[]{:S(2)}) collective-permute-start(bf16[512,512]{1,0:T(8,128)(2,1)S(1)} %reshape.323), channel_id=1, source_target_pairs={{0,3},{1,0},{2,1},{3,2},{4,7},{5,4},{6,5},{7,6},{8,11},{9,8},{10,9... | collective-permute-start | bytes 1572872 | tf_op jit(solution)/shard_map/ppermute | solution.py:73
  60.3 20.4 %copy-start.11 = (f32[512]{0:T(512)}, f32[512]{0:T(512)S(1)}, u32[]{:S(2)}) copy-start(f32[512]{0:T(512)S(1)} %get-tuple-element.13) | copy-start | bytes 6148
  60.3 22.1 %copy-start.9 = (f32[512]{0:T(512)}, f32[512]{0:T(512)S(1)}, u32[]{:S(2)}) copy-start(f32[512]{0:T(512)S(1)} %get-tuple-element.15) | copy-start | bytes 6148
  60.3 23.7 %copy-start.7 = (f32[512]{0:T(512)}, f32[512]{0:T(512)S(1)}, u32[]{:S(2)}) copy-start(f32[512]{0:T(512)S(1)} %get-tuple-element.12) | copy-start | bytes 6148
  84.0 1.9 %copy-start.15 = (f32[128]{0:T(128)S(1)}, f32[128]{0:T(128)}, u32[]{:S(2)}) copy-start(f32[128]{0:T(128)} %copy-done.14) | copy-start | bytes 1540
  84.0 3.1 %copy-start.3 = (bf16[2048,512]{1,0:T(8,128)(2,1)S(1)}, bf16[2048,512]{1,0:T(8,128)(2,1)}, u32[]{:S(2)}) copy-start(bf16[2048,512]{1,0:T(8,128)(2,1)} %param.11) | copy-start | bytes 6291460
  85.8 9.2 %copy-start.1 = (f32[512,512]{0,1:T(8,128)}, f32[512,512]{0,1:T(8,128)S(1)}, u32[]{:S(2)}) copy-start(f32[512,512]{0,1:T(8,128)S(1)} %convolution_add_fusion) | copy-start | bytes 3145732
  85.8 1.9 %copy-start.12 = (f32[512]{0:T(512)S(1)}, f32[512]{0:T(512)}, u32[]{:S(2)}) copy-start(f32[512]{0:T(512)} %copy-done.11) | copy-start | bytes 6148
  87.1 6.7 %copy-start.5 = (bf16[512,1,128]{0,2,1:T(8,128)(2,1)}, bf16[512,1,128]{0,2,1:T(8,128)(2,1)S(1)}, u32[]{:S(2)}) copy-start(bf16[512,1,128]{0,2,1:T(8,128)(2,1)S(1)} %get-tuple-element.11) | copy-start | bytes 393220
  95.4 7.1 %copy-start.18 = (s32[128]{0:T(128)S(1)}, s32[128]{0:T(128)}, u32[]{:S(2)}) copy-start(s32[128]{0:T(128)} %get-tuple-element.2) | copy-start | bytes 1540
  95.5 9.4 %copy-start.6 = (bf16[512,1,128]{0,2,1:T(8,128)(2,1)S(1)}, bf16[512,1,128]{0,2,1:T(8,128)(2,1)}, u32[]{:S(2)}) copy-start(bf16[512,1,128]{0,2,1:T(8,128)(2,1)} %copy-done.5) | copy-start | bytes 393220
  96.6 26.6 %all-to-all-start.1 = ((bf16[128,4,512]{2,1,0:T(4,128)(2,1)}), bf16[128,4,512]{2,1,0:T(4,128)(2,1)S(1)}, u32[]{:S(2)}, u32[]{:S(2)}) async-start(bf16[128,4,512]{2,1,0:T(4,128)(2,1)} %reshape.326), calls=%async_computation.1 | async-start | bytes 1048576 | tf_op jit(solution)/shard_map/all_to_all | solution.py:226
  105.9 18.2 %copy-start.17 = (pred[512]{0:T(512)(128)(4,1)S(1)}, pred[512]{0:T(512)(128)(4,1)}, u32[]{:S(2)}) copy-start(pred[512]{0:T(512)(128)(4,1)} %copy-done.16) | copy-start | bytes 1540
  124.1 4.4 %copy-start.2 = (bf16[512,2048]{1,0:T(8,128)(2,1)S(1)}, bf16[512,2048]{1,0:T(8,128)(2,1)}, u32[]{:S(2)}) copy-start(bf16[512,2048]{1,0:T(8,128)(2,1)} %param.13) | copy-start | bytes 6291460
  128.8 14.4 %collective-permute-start.5 = (bf16[224,512]{1,0:T(8,128)(2,1)S(1)}, bf16[224,512]{1,0:T(8,128)(2,1)S(1)}, u32[]{:S(2)}, u32[]{:S(2)}) collective-permute-start(bf16[224,512]{1,0:T(8,128)(2,1)S(1)} %convolution_convert_fusion.3), channel_id=1, source_target_pairs={{0,3},{1,0},{2,1},{3,2},{4,7},{5,4},{6,5},{7,6},{8,11},{9,8},{10,9... | collective-permute-start | bytes 688136 | tf_op jit(solution)/shard_map/ppermute | solution.py:121
  133.1 10.7 %collective-permute-start.4 = (bf16[224,512]{1,0:T(8,128)(2,1)S(1)}, bf16[224,512]{1,0:T(8,128)(2,1)S(1)}, u32[]{:S(2)}, u32[]{:S(2)}) collective-permute-start(bf16[224,512]{1,0:T(8,128)(2,1)S(1)} %convolution_convert_fusion.4), channel_id=1, source_target_pairs={{0,2},{1,3},{2,0},{3,1},{4,6},{5,7},{6,4},{7,5},{8,10},{9,11},{10,... | collective-permute-start | bytes 688136 | tf_op jit(solution)/shard_map/ppermute | solution.py:121
  136.5 12.4 %collective-permute-start.3 = (bf16[224,512]{1,0:T(8,128)(2,1)S(1)}, bf16[224,512]{1,0:T(8,128)(2,1)S(1)}, u32[]{:S(2)}, u32[]{:S(2)}) collective-permute-start(bf16[224,512]{1,0:T(8,128)(2,1)S(1)} %convolution_convert_fusion.5), channel_id=1, source_target_pairs={{0,1},{1,2},{2,3},{3,0},{4,5},{5,6},{6,7},{7,4},{8,9},{9,10},{10,1... | collective-permute-start | bytes 688136 | tf_op jit(solution)/shard_map/ppermute | solution.py:121
  (4 other events, 5.6 us)

commit v9 on v7

--- a/solution.py
+++ b/solution.py
@@ -143,7 +143,9 @@
     chunk_slots = capacity // CHUNKS
     chunk_rows = chunk_slots * source_count
     request_ids = jnp.arange(source_count, dtype=jnp.int32)
-    starts = jnp.cumsum(request_lengths) - request_lengths
+    starts = jnp.sum(
+        jnp.where(request_ids[None, :] < request_ids[:, None], request_lengths[None, :], 0), axis=1
+    )
     first_row = jnp.maximum((starts - source_pos + source_count - 1) // source_count, 0)
     owner_match = request_owner[None, :] == request_ids[:, None]
     send_first = jnp.sum(jnp.where(owner_match, first_row[None, :], 0), axis=1)

time: 143 us -> 143 us (level)
  no operation moved by 1% of the time
where the time goes in v9:
time: 143 us; the launch traced here: 142 us
  waiting for transfers between devices  59.6 us (42%)
  starting transfers between devices  44.6 us (31%)
  matrix products  14.6 us (10%)
  other arithmetic  11.8 us (8%)
  local copies, waits for them, and re-layouts  7.97 us (6%)
  between operations  3.1 us (2%)
    all_to_all x1, starting transfers between devices, body(): lax.all_to_all(picked[:, chunk * chunk_slots:(chunk + 1) * chunk_slots],...  18.4 us
    all_to_all x1, waiting for transfers between devices, body(): lax.all_to_all(picked[:, chunk * chunk_slots:(chunk + 1) * chunk_slots],...  17.4 us
    ppermute x3, waiting for transfers between devices, ring_blocks(): blocks.append(lax.ppermute(narrow, axis_name, perm))  16.6 us
    all_to_all x1, waiting for transfers between devices, body(): lax.all_to_all(outgoing, 'seq', split_axis=0, concat_axis=0, tiled=True)  16.3 us
    ppermute x3, starting transfers between devices, ring_blocks(): blocks.append(lax.ppermute(narrow, axis_name, perm))  10.7 us
    ppermute x3, starting transfers between devices, ring_output(): total = total + lax.ppermute(part, axis_name, perm).astype(jnp.float32)  9.6 us
    ppermute x3, waiting for transfers between devices, ring_output(): total = total + lax.ppermute(part, axis_name, perm).astype(jnp.float32)  9.4 us
    all_to_all x1, starting transfers between devices, body(): lax.all_to_all(outgoing, 'seq', split_axis=0, concat_axis=0, tiled=True)  5.86 us
  transfers between devices with their start and end apart: 8, of which 7 were waited for; matrix products, arithmetic and copies ran while one was open for 7% of the time, Pallas kernels for 0%

profile of v9, /device:TPU:1, one launch (start us, length us, event | category | flops | bytes accessed | tf_op | source)
XLA Modules:
  0.0 141.7 jit_solution(7425659629009828821)
XLA Ops:
  3.0 1.3 convolution_convert_fusion
  5.3 18.4 %all-to-all-start = ((bf16[128,4,512]{2,1,0:T(4,128)(2,1)}), bf16[128,4,512]{2,1,0:T(4,128)(2,1)S(1)}, u32[]{:S(2)}, u32[]{:S(2)}) async-start(bf16[128,4,512]{2,1,0:T(4,128)(2,1)} %reshape.244), calls=%async_computation | async-start | bytes 1048576 | tf_op jit(solution)/shard_map/all_to_all | solution.py:184
  26.9 17.4 %all-to-all-done = bf16[128,4,512]{2,1,0:T(4,128)(2,1)S(1)} async-done(((bf16[128,4,512]{2,1,0:T(4,128)(2,1)}), bf16[128,4,512]{2,1,0:T(4,128)(2,1)S(1)}, u32[]{:S(2)}, u32[]{:S(2)}) %all-to-all-start) | async-done | bytes 524320 | tf_op jit(solution)/shard_map/all_to_all | solution.py:184
  44.9 3.1 %collective-permute-start.2 = (bf16[512,512]{1,0:T(8,128)(2,1)S(1)}, bf16[512,512]{1,0:T(8,128)(2,1)S(1)}, u32[]{:S(2)}, u32[]{:S(2)}) collective-permute-start(bf16[512,512]{1,0:T(8,128)(2,1)S(1)} %bitcast.36), channel_id=1, source_target_pairs={{0,1},{1,2},{2,3},{3,0},{4,5},{5,6},{6,7},{7,4},{8,9},{9,10},{10,1... | collective-permute-start | bytes 1572872 | tf_op jit(solution)/shard_map/ppermute | solution.py:76
  48.0 4.4 %collective-permute-start.1 = (bf16[512,512]{1,0:T(8,128)(2,1)S(1)}, bf16[512,512]{1,0:T(8,128)(2,1)}, u32[]{:S(2)}, u32[]{:S(2)}) collective-permute-start(bf16[512,512]{1,0:T(8,128)(2,1)S(1)} %bitcast.37), channel_id=1, source_target_pairs={{0,2},{1,3},{2,0},{3,1},{4,6},{5,7},{6,4},{7,5},{8,10},{9,11},{10,... | collective-permute-start | bytes 1572872 | tf_op jit(solution)/shard_map/ppermute | solution.py:76
  53.2 3.2 %collective-permute-start = (bf16[512,512]{1,0:T(8,128)(2,1)S(1)}, bf16[512,512]{1,0:T(8,128)(2,1)S(1)}, u32[]{:S(2)}, u32[]{:S(2)}) collective-permute-start(bf16[512,512]{1,0:T(8,128)(2,1)S(1)} %bitcast.38), channel_id=1, source_target_pairs={{0,3},{1,0},{2,1},{3,2},{4,7},{5,4},{6,5},{7,6},{8,11},{9,8},{10,9... | collective-permute-start | bytes 1572872 | tf_op jit(solution)/shard_map/ppermute | solution.py:76
  57.5 4.4 %collective-permute-done.2 = bf16[512,512]{1,0:T(8,128)(2,1)S(1)} collective-permute-done((bf16[512,512]{1,0:T(8,128)(2,1)S(1)}, bf16[512,512]{1,0:T(8,128)(2,1)S(1)}, u32[]{:S(2)}, u32[]{:S(2)}) %collective-permute-start.2) | collective-permute-done | bytes 524320 | tf_op jit(solution)/shard_map/ppermute | solution.py:76
  62.0 12.1 %collective-permute-done.1 = bf16[512,512]{1,0:T(8,128)(2,1)} collective-permute-done((bf16[512,512]{1,0:T(8,128)(2,1)S(1)}, bf16[512,512]{1,0:T(8,128)(2,1)}, u32[]{:S(2)}, u32[]{:S(2)}) %collective-permute-start.1) | collective-permute-done | bytes 524320 | tf_op jit(solution)/shard_map/ppermute | solution.py:76
  74.2 1.2 fusion.6
  76.8 1.6 %convolution_add_fusion.1 = f32[512,512]{0,1:T(8,128)S(1)} fusion(f32[512,512]{0,1:T(8,128)S(1)} %convolution_add_fusion.2, bf16[2048,512]{1,0:T(8,128)(2,1)S(1)} %copy-done, s32[]{:T(128)S(6)} %select_n.118, bf16[512,512]{1,0:T(8,128)(2,1)} %collective-permute-done.1, f32[512]{0:T(512)S(1)} %get-tuple-element.17, f32[512]{0:T(512)S(1)} %fusion.73), kind=kOutput, calls=%fused_computation.1 | convolution fusion | flops 269746176 | bytes 3149828 | tf_op jit(solution)/shard_map/dot_general | solution.py:98
  79.1 1.2 fusion.40
  81.5 1.6 %convolution_add_fusion.4 = f32[512,512]{0,1:T(8,128)S(1)} fusion(f32[512,512]{0,1:T(8,128)S(1)} %convolution_add_fusion.5, bf16[2048,512]{1,0:T(8,128)(2,1)S(1)} %copy-done.3, s32[]{:T(128)S(6)} %select_n.118, bf16[512,512]{1,0:T(8,128)(2,1)} %collective-permute-done.1, f32[512]{0:T(512)S(1)} %get-tuple-element.17, f32[512]{0:T(512)S(1)} %fusion.73), kind=kOutput, calls=%fused_computation.4 | convolution fusion | flops 269746176 | bytes 3149828 | tf_op jit(solution)/shard_map/dot_general | solution.py:93
  86.7 1.7 %fusion.15 = bf16[128,4,512]{2,1,0:T(4,128)(2,1)} fusion(s32[]{:T(128)S(6)} %select_n.130, bf16[128,4,512]{2,1,0:T(4,128)(2,1)S(1)} %bitcast.42), kind=kLoop, calls=%fused_computation.48 | loop fusion | flops 262144 | bytes 1048580 | tf_op jit(solution)/shard_map/jit(_roll_dynamic)/concatenate | solution.py:68
  88.3 5.9 %all-to-all-start.1 = ((bf16[128,4,512]{2,1,0:T(4,128)(2,1)}), bf16[128,4,512]{2,1,0:T(4,128)(2,1)S(1)}, u32[]{:S(2)}, u32[]{:S(2)}) async-start(bf16[128,4,512]{2,1,0:T(4,128)(2,1)} %fusion.15), calls=%async_computation.1 | async-start | bytes 1048576 | tf_op jit(solution)/shard_map/all_to_all | solution.py:223
  97.4 1.3 copy.21
  98.6 16.3 %all-to-all-done.1 = bf16[128,4,512]{2,1,0:T(4,128)(2,1)S(1)} async-done(((bf16[128,4,512]{2,1,0:T(4,128)(2,1)}), bf16[128,4,512]{2,1,0:T(4,128)(2,1)S(1)}, u32[]{:S(2)}, u32[]{:S(2)}) %all-to-all-start.1) | async-done | bytes 524320 | tf_op jit(solution)/shard_map/all_to_all | solution.py:223
  115.8 1.7 %fusion.32 = bf16[256,512]{1,0:T(8,128)(2,1)S(1)} fusion(bf16[512,512]{1,0:T(8,128)(2,1)} %reshape.249, s32[512]{0:T(512)S(1)} %add.198, pred[512]{0:T(512)(128)(4,1)S(1)} %compare_and_fusion), kind=kOutput, calls=%fused_computation.73 | convolution fusion | flops 134479872 | bytes 788992 | tf_op jit(solution)/shard_map/dot_general | solution.py:227
  117.5 1.3 convolution_convert_fusion.3
  118.8 1.3 convolution_convert_fusion.4
  120.5 4.3 %collective-permute-start.5 = (bf16[224,512]{1,0:T(8,128)(2,1)S(1)}, bf16[224,512]{1,0:T(8,128)(2,1)S(1)}, u32[]{:S(2)}, u32[]{:S(2)}) collective-permute-start(bf16[224,512]{1,0:T(8,128)(2,1)S(1)} %convolution_convert_fusion.3), channel_id=1, source_target_pairs={{0,3},{1,0},{2,1},{3,2},{4,7},{5,4},{6,5},{7,6},{8,11},{9,8},{10,9... | collective-permute-start | bytes 688136 | tf_op jit(solution)/shard_map/ppermute | solution.py:124
  124.8 3.4 %collective-permute-start.4 = (bf16[224,512]{1,0:T(8,128)(2,1)S(1)}, bf16[224,512]{1,0:T(8,128)(2,1)S(1)}, u32[]{:S(2)}, u32[]{:S(2)}) collective-permute-start(bf16[224,512]{1,0:T(8,128)(2,1)S(1)} %convolution_convert_fusion.4), channel_id=1, source_target_pairs={{0,2},{1,3},{2,0},{3,1},{4,6},{5,7},{6,4},{7,5},{8,10},{9,11},{10,... | collective-permute-start | bytes 688136 | tf_op jit(solution)/shard_map/ppermute | solution.py:124
  128.2 1.9 %collective-permute-start.3 = (bf16[224,512]{1,0:T(8,128)(2,1)S(1)}, bf16[224,512]{1,0:T(8,128)(2,1)S(1)}, u32[]{:S(2)}, u32[]{:S(2)}) collective-permute-start(bf16[224,512]{1,0:T(8,128)(2,1)S(1)} %convolution_convert_fusion.5), channel_id=1, source_target_pairs={{0,1},{1,2},{2,3},{3,0},{4,5},{5,6},{6,7},{7,4},{8,9},{9,10},{10,1... | collective-permute-start | bytes 688136 | tf_op jit(solution)/shard_map/ppermute | solution.py:124
  131.2 3.6 %collective-permute-done.5 = bf16[224,512]{1,0:T(8,128)(2,1)S(1)} collective-permute-done((bf16[224,512]{1,0:T(8,128)(2,1)S(1)}, bf16[224,512]{1,0:T(8,128)(2,1)S(1)}, u32[]{:S(2)}, u32[]{:S(2)}) %collective-permute-start.5) | collective-permute-done | bytes 229408 | tf_op jit(solution)/shard_map/ppermute | solution.py:124
  135.4 5.2 %collective-permute-done.3 = bf16[224,512]{1,0:T(8,128)(2,1)S(1)} collective-permute-done((bf16[224,512]{1,0:T(8,128)(2,1)S(1)}, bf16[224,512]{1,0:T(8,128)(2,1)S(1)}, u32[]{:S(2)}, u32[]{:S(2)}) %collective-permute-start.3) | collective-permute-done | bytes 229408 | tf_op jit(solution)/shard_map/ppermute | solution.py:124
  (64 shorter events, 20.7 us)
Async XLA Ops:
  0.6 75.0 %copy-start = (bf16[2048,512]{1,0:T(8,128)(2,1)S(1)}, bf16[2048,512]{1,0:T(8,128)(2,1)}, u32[]{:S(2)}) copy-start(bf16[2048,512]{1,0:T(8,128)(2,1)} %param.14) | copy-start | bytes 6291460
  4.3 48.8 %copy-start.4 = (bf16[2048]{0:T(1024)(128)(2,1)S(1)}, bf16[2048]{0:T(1024)(128)(2,1)}, u32[]{:S(2)}) copy-start(bf16[2048]{0:T(1024)(128)(2,1)} %param.12) | copy-start | bytes 12292
  5.3 39.0 %all-to-all-start = ((bf16[128,4,512]{2,1,0:T(4,128)(2,1)}), bf16[128,4,512]{2,1,0:T(4,128)(2,1)S(1)}, u32[]{:S(2)}, u32[]{:S(2)}) async-start(bf16[128,4,512]{2,1,0:T(4,128)(2,1)} %reshape.244), calls=%async_computation | async-start | bytes 1048576 | tf_op jit(solution)/shard_map/all_to_all | solution.py:184
  44.9 17.0 %collective-permute-start.2 = (bf16[512,512]{1,0:T(8,128)(2,1)S(1)}, bf16[512,512]{1,0:T(8,128)(2,1)S(1)}, u32[]{:S(2)}, u32[]{:S(2)}) collective-permute-start(bf16[512,512]{1,0:T(8,128)(2,1)S(1)} %bitcast.36), channel_id=1, source_target_pairs={{0,1},{1,2},{2,3},{3,0},{4,5},{5,6},{6,7},{7,4},{8,9},{9,10},{10,1... | collective-permute-start | bytes 1572872 | tf_op jit(solution)/shard_map/ppermute | solution.py:76
  48.0 26.2 %collective-permute-start.1 = (bf16[512,512]{1,0:T(8,128)(2,1)S(1)}, bf16[512,512]{1,0:T(8,128)(2,1)}, u32[]{:S(2)}, u32[]{:S(2)}) collective-permute-start(bf16[512,512]{1,0:T(8,128)(2,1)S(1)} %bitcast.37), channel_id=1, source_target_pairs={{0,2},{1,3},{2,0},{3,1},{4,6},{5,7},{6,4},{7,5},{8,10},{9,11},{10,... | collective-permute-start | bytes 1572872 | tf_op jit(solution)/shard_map/ppermute | solution.py:76
  53.2 22.2 %collective-permute-start = (bf16[512,512]{1,0:T(8,128)(2,1)S(1)}, bf16[512,512]{1,0:T(8,128)(2,1)S(1)}, u32[]{:S(2)}, u32[]{:S(2)}) collective-permute-start(bf16[512,512]{1,0:T(8,128)(2,1)S(1)} %bitcast.38), channel_id=1, source_target_pairs={{0,3},{1,0},{2,1},{3,2},{4,7},{5,4},{6,5},{7,6},{8,11},{9,8},{10,9... | collective-permute-start | bytes 1572872 | tf_op jit(solution)/shard_map/ppermute | solution.py:76
  78.5 1.8 %copy-start.3 = (bf16[2048,512]{1,0:T(8,128)(2,1)S(1)}, bf16[2048,512]{1,0:T(8,128)(2,1)}, u32[]{:S(2)}) copy-start(bf16[2048,512]{1,0:T(8,128)(2,1)} %param.13) | copy-start | bytes 6291460
  79.1 6.5 %copy-start.1 = (f32[512,512]{0,1:T(8,128)}, f32[512,512]{0,1:T(8,128)S(1)}, u32[]{:S(2)}) copy-start(f32[512,512]{0,1:T(8,128)S(1)} %convolution_add_fusion) | copy-start | bytes 3145732
  88.3 26.6 %all-to-all-start.1 = ((bf16[128,4,512]{2,1,0:T(4,128)(2,1)}), bf16[128,4,512]{2,1,0:T(4,128)(2,1)S(1)}, u32[]{:S(2)}, u32[]{:S(2)}) async-start(bf16[128,4,512]{2,1,0:T(4,128)(2,1)} %fusion.15), calls=%async_computation.1 | async-start | bytes 1048576 | tf_op jit(solution)/shard_map/all_to_all | solution.py:223
  115.8 4.4 %copy-start.2 = (bf16[512,2048]{1,0:T(8,128)(2,1)S(1)}, bf16[512,2048]{1,0:T(8,128)(2,1)}, u32[]{:S(2)}) copy-start(bf16[512,2048]{1,0:T(8,128)(2,1)} %param.15) | copy-start | bytes 6291460
  120.5 14.4 %collective-permute-start.5 = (bf16[224,512]{1,0:T(8,128)(2,1)S(1)}, bf16[224,512]{1,0:T(8,128)(2,1)S(1)}, u32[]{:S(2)}, u32[]{:S(2)}) collective-permute-start(bf16[224,512]{1,0:T(8,128)(2,1)S(1)} %convolution_convert_fusion.3), channel_id=1, source_target_pairs={{0,3},{1,0},{2,1},{3,2},{4,7},{5,4},{6,5},{7,6},{8,11},{9,8},{10,9... | collective-permute-start | bytes 688136 | tf_op jit(solution)/shard_map/ppermute | solution.py:124
  124.8 10.7 %collective-permute-start.4 = (bf16[224,512]{1,0:T(8,128)(2,1)S(1)}, bf16[224,512]{1,0:T(8,128)(2,1)S(1)}, u32[]{:S(2)}, u32[]{:S(2)}) collective-permute-start(bf16[224,512]{1,0:T(8,128)(2,1)S(1)} %convolution_convert_fusion.4), channel_id=1, source_target_pairs={{0,2},{1,3},{2,0},{3,1},{4,6},{5,7},{6,4},{7,5},{8,10},{9,11},{10,... | collective-permute-start | bytes 688136 | tf_op jit(solution)/shard_map/ppermute | solution.py:124
  128.2 12.5 %collective-permute-start.3 = (bf16[224,512]{1,0:T(8,128)(2,1)S(1)}, bf16[224,512]{1,0:T(8,128)(2,1)S(1)}, u32[]{:S(2)}, u32[]{:S(2)}) collective-permute-start(bf16[224,512]{1,0:T(8,128)(2,1)S(1)} %convolution_convert_fusion.5), channel_id=1, source_target_pairs={{0,1},{1,2},{2,3},{3,0},{4,5},{5,6},{6,7},{7,4},{8,9},{9,10},{10,1... | collective-permute-start | bytes 688136 | tf_op jit(solution)/shard_map/ppermute | solution.py:124

commit v10 on v9

--- a/solution.py
+++ b/solution.py
@@ -78,30 +78,16 @@
 
 
 def project_blocks(blocks, gain, query_weight, keyval_weight, axis_name):
-    count = lax.axis_size(axis_name)
     position = lax.axis_index(axis_name)
-    width = blocks[0].shape[1]
-    widened = [block.astype(jnp.float32) for block in blocks]
-    squares = sum(jnp.sum(block * block, axis=-1, keepdims=True) for block in widened)
-    inverse_rms = lax.rsqrt(squares / (width * count) + EPSILON)
-    queries = None
-    keyvals = None
-    for shift, block in enumerate(widened):
-        first = ((position + shift) % count) * width
-        block_gain = lax.dynamic_slice_in_dim(gain, first, width, 0).astype(jnp.float32)
-        normed = (block * inverse_rms * block_gain).astype(jnp.bfloat16)
-        query_part = jnp.dot(
-            normed,
-            lax.dynamic_slice_in_dim(query_weight, first, width, 0),
-            preferred_element_type=jnp.float32,
-        )
-        keyval_part = jnp.dot(
-            normed,
-            lax.dynamic_slice_in_dim(keyval_weight, first, width, 0),
-            preferred_element_type=jnp.float32,
-        )
-        queries = query_part if queries is None else queries + query_part
-        keyvals = keyval_part if keyvals is None else keyvals + keyval_part
+    offset = position * blocks[0].shape[1]
+    rows = jnp.concatenate(blocks, axis=1)
+    normed = normalize(rows, jnp.roll(gain, -offset))
+    queries = jnp.dot(
+        normed, jnp.roll(query_weight, -offset, axis=0), preferred_element_type=jnp.float32
+    )
+    keyvals = jnp.dot(
+        normed, jnp.roll(keyval_weight, -offset, axis=0), preferred_element_type=jnp.float32
+    )
     return queries, keyvals
 
 

time: 143 us -> 140 us (0.979)
  matrix products: 14.6 us -> 11.7 us
    dot_general x4, matrix products: 3.28 us -> 1.21 us  [ring_output(): jnp.dot(local_attention, lax.dynamic_slice_in_dim(output_weight, first, w...]
    reduce_sum x4 -> x1, other arithmetic: 2.07 us -> 0.48 us  [normalize(): jnp.mean(widened * widened, axis=-1, keepdims=True) + EPSILON]
    dot_general x8 -> x2, matrix products: 6.84 us -> 6.12 us  [the longest x1 3.06 us: project_blocks(): jnp.dot(normed, jnp.roll(query_weight, -offset, axis=0), preferred_elemen...]
  transfers between devices with their start and end apart: 8 -> 8, of which waited for: 7 -> 8; matrix products, arithmetic and copies ran while one was open for 7% -> 7% of each run, Pallas kernels for 0% -> 0%
where the time goes in v10:
time: 140 us; the launch traced here: 139 us
  waiting for transfers between devices  60.6 us (43%)
  starting transfers between devices  45 us (32%)
  matrix products  11.7 us (8%)
  other arithmetic  10.7 us (8%)
  local copies, waits for them, and re-layouts  7.97 us (6%)
  between operations  3.04 us (2%)
    all_to_all x1, starting transfers between devices, body(): lax.all_to_all(picked[:, chunk * chunk_slots:(chunk + 1) * chunk_slots],...  18.4 us
    ppermute x3, waiting for transfers between devices, ring_blocks(): blocks.append(lax.ppermute(narrow, axis_name, perm))  18 us
    all_to_all x1, waiting for transfers between devices, body(): lax.all_to_all(picked[:, chunk * chunk_slots:(chunk + 1) * chunk_slots],...  17.4 us
    all_to_all x1, waiting for transfers between devices, body(): lax.all_to_all(outgoing, 'seq', split_axis=0, concat_axis=0, tiled=True)  16.2 us
    ppermute x3, starting transfers between devices, ring_blocks(): blocks.append(lax.ppermute(narrow, axis_name, perm))  10.9 us
    ppermute x3, starting transfers between devices, ring_output(): total = total + lax.ppermute(part, axis_name, perm).astype(jnp.float32)  9.64 us
    ppermute x3, waiting for transfers between devices, ring_output(): total = total + lax.ppermute(part, axis_name, perm).astype(jnp.float32)  9.04 us
    all_to_all x1, starting transfers between devices, body(): lax.all_to_all(outgoing, 'seq', split_axis=0, concat_axis=0, tiled=True)  6.12 us
  transfers between devices with their start and end apart: 8, of which 8 were waited for; matrix products, arithmetic and copies ran while one was open for 7% of the time, Pallas kernels for 0%

profile of v10, /device:TPU:1, one launch (start us, length us, event | category | flops | bytes accessed | tf_op | source)
XLA Modules:
  0.0 139.0 jit_solution(7587444983025962887)
XLA Ops:
  3.0 1.3 convolution_convert_fusion
  5.3 18.4 %all-to-all-start = ((bf16[128,4,512]{2,1,0:T(4,128)(2,1)}), bf16[128,4,512]{2,1,0:T(4,128)(2,1)S(1)}, u32[]{:S(2)}, u32[]{:S(2)}) async-start(bf16[128,4,512]{2,1,0:T(4,128)(2,1)} %reshape.225), calls=%async_computation | async-start | bytes 1048576 | tf_op jit(solution)/shard_map/all_to_all | solution.py:170
  26.9 17.4 %all-to-all-done = bf16[128,4,512]{2,1,0:T(4,128)(2,1)S(1)} async-done(((bf16[128,4,512]{2,1,0:T(4,128)(2,1)}), bf16[128,4,512]{2,1,0:T(4,128)(2,1)S(1)}, u32[]{:S(2)}, u32[]{:S(2)}) %all-to-all-start) | async-done | bytes 524320 | tf_op jit(solution)/shard_map/all_to_all | solution.py:170
  44.8 3.3 %collective-permute-start.2 = (bf16[512,512]{1,0:T(8,128)(2,1)S(1)}, bf16[512,512]{1,0:T(8,128)(2,1)S(1)}, u32[]{:S(2)}, u32[]{:S(2)}) collective-permute-start(bf16[512,512]{1,0:T(8,128)(2,1)S(1)} %bitcast.23), channel_id=1, source_target_pairs={{0,1},{1,2},{2,3},{3,0},{4,5},{5,6},{6,7},{7,4},{8,9},{9,10},{10,1... | collective-permute-start | bytes 1572872 | tf_op jit(solution)/shard_map/ppermute | solution.py:76
  48.1 4.4 %collective-permute-start.1 = (bf16[512,512]{1,0:T(8,128)(2,1)S(1)}, bf16[512,512]{1,0:T(8,128)(2,1)S(1)}, u32[]{:S(2)}, u32[]{:S(2)}) collective-permute-start(bf16[512,512]{1,0:T(8,128)(2,1)S(1)} %bitcast.24), channel_id=1, source_target_pairs={{0,2},{1,3},{2,0},{3,1},{4,6},{5,7},{6,4},{7,5},{8,10},{9,11},{10,... | collective-permute-start | bytes 1572872 | tf_op jit(solution)/shard_map/ppermute | solution.py:76
  52.4 3.2 %collective-permute-start = (bf16[512,512]{1,0:T(8,128)(2,1)S(1)}, bf16[512,512]{1,0:T(8,128)(2,1)S(1)}, u32[]{:S(2)}, u32[]{:S(2)}) collective-permute-start(bf16[512,512]{1,0:T(8,128)(2,1)S(1)} %bitcast.25), channel_id=1, source_target_pairs={{0,3},{1,0},{2,1},{3,2},{4,7},{5,4},{6,5},{7,6},{8,11},{9,8},{10,9... | collective-permute-start | bytes 1572872 | tf_op jit(solution)/shard_map/ppermute | solution.py:76
  57.5 4.5 %collective-permute-done.2 = bf16[512,512]{1,0:T(8,128)(2,1)S(1)} collective-permute-done((bf16[512,512]{1,0:T(8,128)(2,1)S(1)}, bf16[512,512]{1,0:T(8,128)(2,1)S(1)}, u32[]{:S(2)}, u32[]{:S(2)}) %collective-permute-start.2) | collective-permute-done | bytes 524320 | tf_op jit(solution)/shard_map/ppermute | solution.py:76
  61.9 12.2 %collective-permute-done.1 = bf16[512,512]{1,0:T(8,128)(2,1)S(1)} collective-permute-done((bf16[512,512]{1,0:T(8,128)(2,1)S(1)}, bf16[512,512]{1,0:T(8,128)(2,1)S(1)}, u32[]{:S(2)}, u32[]{:S(2)}) %collective-permute-start.1) | collective-permute-done | bytes 524320 | tf_op jit(solution)/shard_map/ppermute | solution.py:76
  74.2 1.3 collective-permute-done
  75.9 3.1 %fusion.7 = f32[512,512]{0,1:T(8,128)S(1)} fusion(s32[]{:T(128)S(6)} %select_n.111, bf16[2048,512]{1,0:T(8,128)(2,1)S(1)} %copy-done.3, f32[2048]{0:T(1024)S(1)} %fusion.42, f32[512]{0:T(512)S(1)} %add_rsqrt_fusion, bf16[512,512]{1,0:T(8,128)(2,1)S(1)} %collective-permute-done.2, bf16[512,512]{1,0:T(8,128)(2,1)S(1)} %collective-permute-done.1, ...), kind=kOutput, calls=%fused_computation.12 | convolution fusion | flops 1089470464 | bytes 5253124 | tf_op jit(solution)/shard_map/dot_general | solution.py:88
  79.1 1.2 fusion.32
  80.2 3.1 %fusion.4 = f32[512,512]{0,1:T(8,128)S(1)} fusion(s32[]{:T(128)S(6)} %select_n.111, bf16[2048,512]{1,0:T(8,128)(2,1)S(1)} %copy-done.4, f32[2048]{0:T(1024)S(1)} %fusion.42, f32[512]{0:T(512)S(1)} %add_rsqrt_fusion, bf16[512,512]{1,0:T(8,128)(2,1)S(1)} %collective-permute-done.2, bf16[512,512]{1,0:T(8,128)(2,1)S(1)} %collective-permute-done.1, ...), kind=kOutput, calls=%fused_computation.10 | convolution fusion | flops 1089470464 | bytes 5253124 | tf_op jit(solution)/shard_map/dot_general | solution.py:85
  86.2 1.7 %fusion.17 = bf16[128,4,512]{2,1,0:T(4,128)(2,1)} fusion(s32[]{:T(128)S(6)} %select_n.135, bf16[128,4,512]{2,1,0:T(4,128)(2,1)S(1)} %bitcast.29), kind=kLoop, calls=%fused_computation.39 | loop fusion | flops 262144 | bytes 1048580 | tf_op jit(solution)/shard_map/jit(_roll_dynamic)/concatenate | solution.py:68
  87.9 6.1 %all-to-all-start.1 = ((bf16[128,4,512]{2,1,0:T(4,128)(2,1)}), bf16[128,4,512]{2,1,0:T(4,128)(2,1)S(1)}, u32[]{:S(2)}, u32[]{:S(2)}) async-start(bf16[128,4,512]{2,1,0:T(4,128)(2,1)} %fusion.17), calls=%async_computation.1 | async-start | bytes 1048576 | tf_op jit(solution)/shard_map/all_to_all | solution.py:209
  95.3 1.1 slice.61
  97.2 1.3 copy.21
  98.5 16.2 %all-to-all-done.1 = bf16[128,4,512]{2,1,0:T(4,128)(2,1)S(1)} async-done(((bf16[128,4,512]{2,1,0:T(4,128)(2,1)}), bf16[128,4,512]{2,1,0:T(4,128)(2,1)S(1)}, u32[]{:S(2)}, u32[]{:S(2)}) %all-to-all-start.1) | async-done | bytes 524320 | tf_op jit(solution)/shard_map/all_to_all | solution.py:209
  115.6 1.5 %fusion.24 = bf16[256,512]{1,0:T(8,128)(2,1)S(1)} fusion(bf16[512,512]{1,0:T(8,128)(2,1)} %reshape.230, s32[512]{0:T(512)S(1)} %add.153, pred[512]{0:T(512)(128)(4,1)S(1)} %compare_and_fusion), kind=kOutput, calls=%fused_computation.54 | convolution fusion | flops 134479872 | bytes 788992 | tf_op jit(solution)/shard_map/dot_general | solution.py:213
  117.5 4.2 %collective-permute-start.5 = (bf16[224,512]{1,0:T(8,128)(2,1)S(1)}, bf16[224,512]{1,0:T(8,128)(2,1)S(1)}, u32[]{:S(2)}, u32[]{:S(2)}) collective-permute-start(bf16[224,512]{1,0:T(8,128)(2,1)S(1)} %convolution_convert_fusion.3), channel_id=1, source_target_pairs={{0,3},{1,0},{2,1},{3,2},{4,7},{5,4},{6,5},{7,6},{8,11},{9,8},{10,9... | collective-permute-start | bytes 688136 | tf_op jit(solution)/shard_map/ppermute | solution.py:110
  122.0 3.5 %collective-permute-start.4 = (bf16[224,512]{1,0:T(8,128)(2,1)S(1)}, bf16[224,512]{1,0:T(8,128)(2,1)S(1)}, u32[]{:S(2)}, u32[]{:S(2)}) collective-permute-start(bf16[224,512]{1,0:T(8,128)(2,1)S(1)} %convolution_convert_fusion.4), channel_id=1, source_target_pairs={{0,2},{1,3},{2,0},{3,1},{4,6},{5,7},{6,4},{7,5},{8,10},{9,11},{10,... | collective-permute-start | bytes 688136 | tf_op jit(solution)/shard_map/ppermute | solution.py:110
  125.8 1.9 %collective-permute-start.3 = (bf16[224,512]{1,0:T(8,128)(2,1)S(1)}, bf16[224,512]{1,0:T(8,128)(2,1)S(1)}, u32[]{:S(2)}, u32[]{:S(2)}) collective-permute-start(bf16[224,512]{1,0:T(8,128)(2,1)S(1)} %convolution_convert_fusion.5), channel_id=1, source_target_pairs={{0,1},{1,2},{2,3},{3,0},{4,5},{5,6},{6,7},{7,4},{8,9},{9,10},{10,1... | collective-permute-start | bytes 688136 | tf_op jit(solution)/shard_map/ppermute | solution.py:110
  127.7 1.1 broadcast_select_fusion
  128.9 3.0 %collective-permute-done.5 = bf16[224,512]{1,0:T(8,128)(2,1)S(1)} collective-permute-done((bf16[224,512]{1,0:T(8,128)(2,1)S(1)}, bf16[224,512]{1,0:T(8,128)(2,1)S(1)}, u32[]{:S(2)}, u32[]{:S(2)}) %collective-permute-start.5) | collective-permute-done | bytes 229408 | tf_op jit(solution)/shard_map/ppermute | solution.py:110
  132.7 5.2 %collective-permute-done.3 = bf16[224,512]{1,0:T(8,128)(2,1)S(1)} collective-permute-done((bf16[224,512]{1,0:T(8,128)(2,1)S(1)}, bf16[224,512]{1,0:T(8,128)(2,1)S(1)}, u32[]{:S(2)}, u32[]{:S(2)}) %collective-permute-start.3) | collective-permute-done | bytes 229408 | tf_op jit(solution)/shard_map/ppermute | solution.py:110
  (56 shorter events, 15.9 us)
Async XLA Ops:
  0.6 116.5 %copy-start = (bf16[512,2048]{1,0:T(8,128)(2,1)S(1)}, bf16[512,2048]{1,0:T(8,128)(2,1)}, u32[]{:S(2)}) copy-start(bf16[512,2048]{1,0:T(8,128)(2,1)} %param.17) | copy-start | bytes 6291460
  4.3 52.0 %copy-start.2 = (bf16[2048]{0:T(1024)(128)(2,1)S(1)}, bf16[2048]{0:T(1024)(128)(2,1)}, u32[]{:S(2)}) copy-start(bf16[2048]{0:T(1024)(128)(2,1)} %param.14) | copy-start | bytes 12292
  5.3 39.0 %all-to-all-start = ((bf16[128,4,512]{2,1,0:T(4,128)(2,1)}), bf16[128,4,512]{2,1,0:T(4,128)(2,1)S(1)}, u32[]{:S(2)}, u32[]{:S(2)}) async-start(bf16[128,4,512]{2,1,0:T(4,128)(2,1)} %reshape.225), calls=%async_computation | async-start | bytes 1048576 | tf_op jit(solution)/shard_map/all_to_all | solution.py:170
  44.4 31.5 %copy-start.3 = (bf16[2048,512]{1,0:T(8,128)(2,1)S(1)}, bf16[2048,512]{1,0:T(8,128)(2,1)}, u32[]{:S(2)}) copy-start(bf16[2048,512]{1,0:T(8,128)(2,1)} %param.16) | copy-start | bytes 6291460
  44.8 17.1 %collective-permute-start.2 = (bf16[512,512]{1,0:T(8,128)(2,1)S(1)}, bf16[512,512]{1,0:T(8,128)(2,1)S(1)}, u32[]{:S(2)}, u32[]{:S(2)}) collective-permute-start(bf16[512,512]{1,0:T(8,128)(2,1)S(1)} %bitcast.23), channel_id=1, source_target_pairs={{0,1},{1,2},{2,3},{3,0},{4,5},{5,6},{6,7},{7,4},{8,9},{9,10},{10,1... | collective-permute-start | bytes 1572872 | tf_op jit(solution)/shard_map/ppermute | solution.py:76
  48.1 26.1 %collective-permute-start.1 = (bf16[512,512]{1,0:T(8,128)(2,1)S(1)}, bf16[512,512]{1,0:T(8,128)(2,1)S(1)}, u32[]{:S(2)}, u32[]{:S(2)}) collective-permute-start(bf16[512,512]{1,0:T(8,128)(2,1)S(1)} %bitcast.24), channel_id=1, source_target_pairs={{0,2},{1,3},{2,0},{3,1},{4,6},{5,7},{6,4},{7,5},{8,10},{9,11},{10,... | collective-permute-start | bytes 1572872 | tf_op jit(solution)/shard_map/ppermute | solution.py:76
  52.4 23.0 %collective-permute-start = (bf16[512,512]{1,0:T(8,128)(2,1)S(1)}, bf16[512,512]{1,0:T(8,128)(2,1)S(1)}, u32[]{:S(2)}, u32[]{:S(2)}) collective-permute-start(bf16[512,512]{1,0:T(8,128)(2,1)S(1)} %bitcast.25), channel_id=1, source_target_pairs={{0,3},{1,0},{2,1},{3,2},{4,7},{5,4},{6,5},{7,6},{8,11},{9,8},{10,9... | collective-permute-start | bytes 1572872 | tf_op jit(solution)/shard_map/ppermute | solution.py:76
  75.9 4.3 %copy-start.4 = (bf16[2048,512]{1,0:T(8,128)(2,1)S(1)}, bf16[2048,512]{1,0:T(8,128)(2,1)}, u32[]{:S(2)}) copy-start(bf16[2048,512]{1,0:T(8,128)(2,1)} %param.15) | copy-start | bytes 6291460
  79.0 6.1 %copy-start.1 = (f32[512,512]{0,1:T(8,128)}, f32[512,512]{0,1:T(8,128)S(1)}, u32[]{:S(2)}) copy-start(f32[512,512]{0,1:T(8,128)S(1)} %fusion.7) | copy-start | bytes 3145732
  87.9 26.8 %all-to-all-start.1 = ((bf16[128,4,512]{2,1,0:T(4,128)(2,1)}), bf16[128,4,512]{2,1,0:T(4,128)(2,1)S(1)}, u32[]{:S(2)}, u32[]{:S(2)}) async-start(bf16[128,4,512]{2,1,0:T(4,128)(2,1)} %fusion.17), calls=%async_computation.1 | async-start | bytes 1048576 | tf_op jit(solution)/shard_map/all_to_all | solution.py:209
  117.5 14.4 %collective-permute-start.5 = (bf16[224,512]{1,0:T(8,128)(2,1)S(1)}, bf16[224,512]{1,0:T(8,128)(2,1)S(1)}, u32[]{:S(2)}, u32[]{:S(2)}) collective-permute-start(bf16[224,512]{1,0:T(8,128)(2,1)S(1)} %convolution_convert_fusion.3), channel_id=1, source_target_pairs={{0,3},{1,0},{2,1},{3,2},{4,7},{5,4},{6,5},{7,6},{8,11},{9,8},{10,9... | collective-permute-start | bytes 688136 | tf_op jit(solution)/shard_map/ppermute | solution.py:110
  122.0 10.7 %collective-permute-start.4 = (bf16[224,512]{1,0:T(8,128)(2,1)S(1)}, bf16[224,512]{1,0:T(8,128)(2,1)S(1)}, u32[]{:S(2)}, u32[]{:S(2)}) collective-permute-start(bf16[224,512]{1,0:T(8,128)(2,1)S(1)} %convolution_convert_fusion.4), channel_id=1, source_target_pairs={{0,2},{1,3},{2,0},{3,1},{4,6},{5,7},{6,4},{7,5},{8,10},{9,11},{10,... | collective-permute-start | bytes 688136 | tf_op jit(solution)/shard_map/ppermute | solution.py:110
  125.8 12.1 %collective-permute-start.3 = (bf16[224,512]{1,0:T(8,128)(2,1)S(1)}, bf16[224,512]{1,0:T(8,128)(2,1)S(1)}, u32[]{:S(2)}, u32[]{:S(2)}) collective-permute-start(bf16[224,512]{1,0:T(8,128)(2,1)S(1)} %convolution_convert_fusion.5), channel_id=1, source_target_pairs={{0,1},{1,2},{2,3},{3,0},{4,5},{5,6},{6,7},{7,4},{8,9},{9,10},{10,1... | collective-permute-start | bytes 688136 | tf_op jit(solution)/shard_map/ppermute | solution.py:110

commit v11 on v10

--- a/solution.py
+++ b/solution.py
@@ -95,19 +95,15 @@
     count = lax.axis_size(axis_name)
     position = lax.axis_index(axis_name)
     width = output_weight.shape[1] // count
-    total = None
-    for shift in range(count):
-        first = ((position + shift) % count) * width
-        part = jnp.dot(
-            local_attention,
-            lax.dynamic_slice_in_dim(output_weight, first, width, 1),
-            preferred_element_type=jnp.float32,
-        ).astype(jnp.bfloat16)
-        if shift == 0:
-            total = part.astype(jnp.float32)
-        else:
-            perm = [(index, (index + shift) % count) for index in range(count)]
-            total = total + lax.ppermute(part, axis_name, perm).astype(jnp.float32)
+    rotated = jnp.roll(output_weight, -position * width, axis=1)
+    stacked = jnp.transpose(rotated.reshape(rotated.shape[0], count, width), (1, 0, 2))
+    parts = jnp.einsum(
+        "id,kdc->kic", local_attention, stacked, preferred_element_type=jnp.float32
+    ).astype(jnp.bfloat16)
+    total = parts[0].astype(jnp.float32)
+    for shift in range(1, count):
+        perm = [(index, (index + shift) % count) for index in range(count)]
+        total = total + lax.ppermute(parts[shift], axis_name, perm).astype(jnp.float32)
     return total.astype(jnp.bfloat16)
 
 

time: 140 us -> 136 us (0.971)
  waiting for transfers between devices: 60.6 us -> 45.8 us
  other arithmetic: 10.7 us -> 16.6 us
  local copies, waits for them, and re-layouts: 7.97 us -> 13.8 us
  matrix products: 11.7 us -> 10.1 us
    all_to_all x1, waiting for transfers between devices: 16.2 us -> 4.7 us  [body(): lax.all_to_all(outgoing, 'seq', split_axis=0, concat_axis=0, tiled=True)]
    concatenate x0 -> x1, other arithmetic: none -> 4.98 us  [ring_output(): rotated = jnp.roll(output_weight, -position * width, axis=1)]
    ppermute x3, waiting for transfers between devices: 9.04 us -> 5.87 us  [ring_output(): lax.ppermute(parts[shift], axis_name, perm).astype(jnp.float32)]
    unnamed x10 -> x13, local copies, waits for them, and re-layouts: 0.03 us -> 2.9 us
    reshape x0 -> x1, local copies, waits for them, and re-layouts: none -> 2.79 us  [ring_output(): rotated.reshape(rotated.shape[0], count, width)]
  transfers between devices with their start and end apart: 8 -> 8, of which waited for: 8 -> 7; matrix products, arithmetic and copies ran while one was open for 7% -> 15% of each run, Pallas kernels for 0% -> 0%
where the time goes in v11:
time: 136 us; the launch traced here: 135 us
  waiting for transfers between devices  45.8 us (34%)
  starting transfers between devices  45.3 us (33%)
  other arithmetic  16.6 us (12%)
  local copies, waits for them, and re-layouts  13.8 us (10%)
  matrix products  10.1 us (7%)
  between operations  3.06 us (2%)
    all_to_all x1, starting transfers between devices, body(): lax.all_to_all(picked[:, chunk * chunk_slots:(chunk + 1) * chunk_slots],...  18.4 us
    ppermute x3, waiting for transfers between devices, ring_blocks(): blocks.append(lax.ppermute(narrow, axis_name, perm))  17.9 us
    all_to_all x1, waiting for transfers between devices, body(): lax.all_to_all(picked[:, chunk * chunk_slots:(chunk + 1) * chunk_slots],...  17.3 us
    ppermute x3, starting transfers between devices, ring_blocks(): blocks.append(lax.ppermute(narrow, axis_name, perm))  10.9 us
    ppermute x3, starting transfers between devices, ring_output(): lax.ppermute(parts[shift], axis_name, perm).astype(jnp.float32)  9.93 us
    all_to_all x1, starting transfers between devices, body(): lax.all_to_all(outgoing, 'seq', split_axis=0, concat_axis=0, tiled=True)  6.11 us
    ppermute x3, waiting for transfers between devices, ring_output(): lax.ppermute(parts[shift], axis_name, perm).astype(jnp.float32)  5.87 us
    concatenate x1, other arithmetic, ring_output(): rotated = jnp.roll(output_weight, -position * width, axis=1)  4.98 us
  transfers between devices with their start and end apart: 8, of which 7 were waited for; matrix products, arithmetic and copies ran while one was open for 15% of the time, Pallas kernels for 0%

profile of v11, /device:TPU:1, one launch (start us, length us, event | category | flops | bytes accessed | tf_op | source)
XLA Modules:
  0.0 134.6 jit_solution(5819373682677983216)
XLA Ops:
  4.2 18.4 %all-to-all-start = ((bf16[128,4,512]{2,1,0:T(4,128)(2,1)}), bf16[128,4,512]{2,1,0:T(4,128)(2,1)S(1)}, u32[]{:S(2)}, u32[]{:S(2)}) async-start(bf16[128,4,512]{2,1,0:T(4,128)(2,1)} %reshape.231), calls=%async_computation | async-start | bytes 1048576 | tf_op jit(solution)/shard_map/all_to_all | solution.py:166
  25.9 17.3 %all-to-all-done = bf16[128,4,512]{2,1,0:T(4,128)(2,1)S(1)} async-done(((bf16[128,4,512]{2,1,0:T(4,128)(2,1)}), bf16[128,4,512]{2,1,0:T(4,128)(2,1)S(1)}, u32[]{:S(2)}, u32[]{:S(2)}) %all-to-all-start) | async-done | bytes 524320 | tf_op jit(solution)/shard_map/all_to_all | solution.py:166
  43.8 3.3 %collective-permute-start.2 = (bf16[512,512]{1,0:T(8,128)(2,1)S(1)}, bf16[512,512]{1,0:T(8,128)(2,1)S(1)}, u32[]{:S(2)}, u32[]{:S(2)}) collective-permute-start(bf16[512,512]{1,0:T(8,128)(2,1)S(1)} %bitcast.48), channel_id=1, source_target_pairs={{0,1},{1,2},{2,3},{3,0},{4,5},{5,6},{6,7},{7,4},{8,9},{9,10},{10,1... | collective-permute-start | bytes 1572872 | tf_op jit(solution)/shard_map/ppermute | solution.py:76
  47.0 4.4 %collective-permute-start.1 = (bf16[512,512]{1,0:T(8,128)(2,1)S(1)}, bf16[512,512]{1,0:T(8,128)(2,1)S(1)}, u32[]{:S(2)}, u32[]{:S(2)}) collective-permute-start(bf16[512,512]{1,0:T(8,128)(2,1)S(1)} %bitcast.49), channel_id=1, source_target_pairs={{0,2},{1,3},{2,0},{3,1},{4,6},{5,7},{6,4},{7,5},{8,10},{9,11},{10,... | collective-permute-start | bytes 1572872 | tf_op jit(solution)/shard_map/ppermute | solution.py:76
  51.4 3.2 %collective-permute-start = (bf16[512,512]{1,0:T(8,128)(2,1)S(1)}, bf16[512,512]{1,0:T(8,128)(2,1)S(1)}, u32[]{:S(2)}, u32[]{:S(2)}) collective-permute-start(bf16[512,512]{1,0:T(8,128)(2,1)S(1)} %bitcast.50), channel_id=1, source_target_pairs={{0,3},{1,0},{2,1},{3,2},{4,7},{5,4},{6,5},{7,6},{8,11},{9,8},{10,9... | collective-permute-start | bytes 1572872 | tf_op jit(solution)/shard_map/ppermute | solution.py:76
  56.4 4.4 %collective-permute-done.2 = bf16[512,512]{1,0:T(8,128)(2,1)S(1)} collective-permute-done((bf16[512,512]{1,0:T(8,128)(2,1)S(1)}, bf16[512,512]{1,0:T(8,128)(2,1)S(1)}, u32[]{:S(2)}, u32[]{:S(2)}) %collective-permute-start.2) | collective-permute-done | bytes 524320 | tf_op jit(solution)/shard_map/ppermute | solution.py:76
  60.9 12.2 %collective-permute-done.1 = bf16[512,512]{1,0:T(8,128)(2,1)S(1)} collective-permute-done((bf16[512,512]{1,0:T(8,128)(2,1)S(1)}, bf16[512,512]{1,0:T(8,128)(2,1)S(1)}, u32[]{:S(2)}, u32[]{:S(2)}) %collective-permute-start.1) | collective-permute-done | bytes 524320 | tf_op jit(solution)/shard_map/ppermute | solution.py:76
  73.1 1.3 collective-permute-done
  74.9 3.0 %fusion.8 = f32[512,512]{0,1:T(8,128)S(1)} fusion(s32[]{:T(128)S(6)} %select_n.95, bf16[2048,512]{1,0:T(8,128)(2,1)S(1)} %copy-done.4, f32[2048]{0:T(1024)S(1)} %fusion.51, f32[512]{0:T(512)S(1)} %add_rsqrt_fusion, bf16[512,512]{1,0:T(8,128)(2,1)S(1)} %collective-permute-done.2, bf16[512,512]{1,0:T(8,128)(2,1)S(1)} %collective-permute-done.1, ...), kind=kOutput, calls=%fused_computation.15 | convolution fusion | flops 1089470464 | bytes 5253124 | tf_op jit(solution)/shard_map/dot_general | solution.py:88
  78.0 1.2 fusion.39
  79.2 3.1 %fusion.5 = f32[512,512]{0,1:T(8,128)S(1)} fusion(s32[]{:T(128)S(6)} %select_n.95, bf16[2048,512]{1,0:T(8,128)(2,1)S(1)} %copy-done.5, f32[2048]{0:T(1024)S(1)} %fusion.51, f32[512]{0:T(512)S(1)} %add_rsqrt_fusion, bf16[512,512]{1,0:T(8,128)(2,1)S(1)} %collective-permute-done.2, bf16[512,512]{1,0:T(8,128)(2,1)S(1)} %collective-permute-done.1, ...), kind=kOutput, calls=%fused_computation.13 | convolution fusion | flops 1089470464 | bytes 5253124 | tf_op jit(solution)/shard_map/dot_general | solution.py:85
  85.2 1.7 %fusion.25 = bf16[128,4,512]{2,1,0:T(4,128)(2,1)} fusion(s32[]{:T(128)S(6)} %select_n.111, bf16[128,4,512]{2,1,0:T(4,128)(2,1)S(1)} %bitcast.54), kind=kLoop, calls=%fused_computation.41 | loop fusion | flops 262144 | bytes 1048580 | tf_op jit(solution)/shard_map/jit(_roll_dynamic)/concatenate | solution.py:68
  86.8 6.1 %all-to-all-start.1 = ((bf16[128,4,512]{2,1,0:T(4,128)(2,1)}), bf16[128,4,512]{2,1,0:T(4,128)(2,1)S(1)}, u32[]{:S(2)}, u32[]{:S(2)}) async-start(bf16[128,4,512]{2,1,0:T(4,128)(2,1)} %fusion.25), calls=%async_computation.1 | async-start | bytes 1048576 | tf_op jit(solution)/shard_map/all_to_all | solution.py:205
  93.6 2.9 %copy.24 = bf16[512,2048]{0,1:T(8,128)(2,1)S(1)} copy(bf16[512,2048]{1,0:T(8,128)(2,1)} %param.17) | data formatting | bytes 4194304 | tf_op args[4]
  96.5 5.0 %fusion.3 = bf16[512,2048]{0,1:T(8,128)(2,1)} fusion(s32[]{:T(128)S(6)} %select_n.86, bf16[512,2048]{0,1:T(8,128)(2,1)S(1)} %copy.24), kind=kLoop, calls=%fused_computation.11 | loop fusion | flops 4194304 | bytes 4194308 | tf_op jit(solution)/shard_map/jit(_roll_dynamic)/concatenate | solution.py:98
  101.4 2.8 %copy.26 = bf16[512,4,512]{2,0,1:T(8,128)(2,1)S(1)} copy(bf16[512,4,512]{0,2,1:T(8,128)(2,1)} %bitcast.47) | data formatting | bytes 4194304 | tf_op jit(solution)/shard_map/reshape | solution.py:99
  107.7 1.3 copy.30
  109.0 4.7 %all-to-all-done.1 = bf16[128,4,512]{2,1,0:T(4,128)(2,1)S(1)} async-done(((bf16[128,4,512]{2,1,0:T(4,128)(2,1)}), bf16[128,4,512]{2,1,0:T(4,128)(2,1)S(1)}, u32[]{:S(2)}, u32[]{:S(2)}) %all-to-all-start.1) | async-done | bytes 524320 | tf_op jit(solution)/shard_map/all_to_all | solution.py:205
  114.6 1.5 %fusion.28 = bf16[256,512]{1,0:T(8,128)(2,1)S(1)} fusion(bf16[512,512]{1,0:T(8,128)(2,1)} %reshape.236, s32[512]{0:T(512)S(1)} %add.131, pred[512]{0:T(512)(128)(4,1)S(1)} %compare_and_fusion), kind=kOutput, calls=%fused_computation.52 | convolution fusion | flops 134479872 | bytes 788992 | tf_op jit(solution)/shard_map/dot_general | solution.py:209
  116.8 4.0 %collective-permute-start.3 = (bf16[224,512]{1,0:T(8,128)(2,1)S(1)}, bf16[224,512]{1,0:T(8,128)(2,1)S(1)}, u32[]{:S(2)}, u32[]{:S(2)}) collective-permute-start(bf16[224,512]{1,0:T(8,128)(2,1)S(1)} %get-tuple-element.11), channel_id=1, source_target_pairs={{0,1},{1,2},{2,3},{3,0},{4,5},{5,6},{6,7},{7,4},{8,9},{9,10},{10,1... | collective-permute-start | bytes 688136 | tf_op jit(solution)/shard_map/ppermute | solution.py:106
  120.8 2.5 %collective-permute-start.5 = (bf16[224,512]{1,0:T(8,128)(2,1)S(1)}, bf16[224,512]{1,0:T(8,128)(2,1)S(1)}, u32[]{:S(2)}, u32[]{:S(2)}) collective-permute-start(bf16[224,512]{1,0:T(8,128)(2,1)S(1)} %get-tuple-element.12), channel_id=1, source_target_pairs={{0,3},{1,0},{2,1},{3,2},{4,7},{5,4},{6,5},{7,6},{8,11},{9,8},{10,9... | collective-permute-start | bytes 688136 | tf_op jit(solution)/shard_map/ppermute | solution.py:106
  123.3 3.4 %collective-permute-start.4 = (bf16[224,512]{1,0:T(8,128)(2,1)S(1)}, bf16[224,512]{1,0:T(8,128)(2,1)S(1)}, u32[]{:S(2)}, u32[]{:S(2)}) collective-permute-start(bf16[224,512]{1,0:T(8,128)(2,1)S(1)} %get-tuple-element.13), channel_id=1, source_target_pairs={{0,2},{1,3},{2,0},{3,1},{4,6},{5,7},{6,4},{7,5},{8,10},{9,11},{10,... | collective-permute-start | bytes 688136 | tf_op jit(solution)/shard_map/ppermute | solution.py:106
  127.9 2.1 %collective-permute-done.5 = bf16[224,512]{1,0:T(8,128)(2,1)S(1)} collective-permute-done((bf16[224,512]{1,0:T(8,128)(2,1)S(1)}, bf16[224,512]{1,0:T(8,128)(2,1)S(1)}, u32[]{:S(2)}, u32[]{:S(2)}) %collective-permute-start.5) | collective-permute-done | bytes 229408 | tf_op jit(solution)/shard_map/ppermute | solution.py:106
  130.0 3.8 %collective-permute-done.4 = bf16[224,512]{1,0:T(8,128)(2,1)S(1)} collective-permute-done((bf16[224,512]{1,0:T(8,128)(2,1)S(1)}, bf16[224,512]{1,0:T(8,128)(2,1)S(1)}, u32[]{:S(2)}, u32[]{:S(2)}) %collective-permute-start.4) | collective-permute-done | bytes 229408 | tf_op jit(solution)/shard_map/ppermute | solution.py:106
  (60 shorter events, 18.1 us)
Async XLA Ops:
  0.6 2.3 %copy-start = (bf16[256,512]{1,0:T(8,128)(2,1)S(1)}, bf16[256,512]{1,0:T(8,128)(2,1)}, u32[]{:S(2)}) copy-start(bf16[256,512]{1,0:T(8,128)(2,1)} %param.13) | copy-start | bytes 786436
  3.3 52.1 %copy-start.3 = (bf16[2048]{0:T(1024)(128)(2,1)S(1)}, bf16[2048]{0:T(1024)(128)(2,1)}, u32[]{:S(2)}) copy-start(bf16[2048]{0:T(1024)(128)(2,1)} %param.14) | copy-start | bytes 12292
  4.2 39.0 %all-to-all-start = ((bf16[128,4,512]{2,1,0:T(4,128)(2,1)}), bf16[128,4,512]{2,1,0:T(4,128)(2,1)S(1)}, u32[]{:S(2)}, u32[]{:S(2)}) async-start(bf16[128,4,512]{2,1,0:T(4,128)(2,1)} %reshape.231), calls=%async_computation | async-start | bytes 1048576 | tf_op jit(solution)/shard_map/all_to_all | solution.py:166
  43.3 31.5 %copy-start.4 = (bf16[2048,512]{1,0:T(8,128)(2,1)S(1)}, bf16[2048,512]{1,0:T(8,128)(2,1)}, u32[]{:S(2)}) copy-start(bf16[2048,512]{1,0:T(8,128)(2,1)} %param.16) | copy-start | bytes 6291460
  43.8 17.1 %collective-permute-start.2 = (bf16[512,512]{1,0:T(8,128)(2,1)S(1)}, bf16[512,512]{1,0:T(8,128)(2,1)S(1)}, u32[]{:S(2)}, u32[]{:S(2)}) collective-permute-start(bf16[512,512]{1,0:T(8,128)(2,1)S(1)} %bitcast.48), channel_id=1, source_target_pairs={{0,1},{1,2},{2,3},{3,0},{4,5},{5,6},{6,7},{7,4},{8,9},{9,10},{10,1... | collective-permute-start | bytes 1572872 | tf_op jit(solution)/shard_map/ppermute | solution.py:76
  47.0 26.1 %collective-permute-start.1 = (bf16[512,512]{1,0:T(8,128)(2,1)S(1)}, bf16[512,512]{1,0:T(8,128)(2,1)S(1)}, u32[]{:S(2)}, u32[]{:S(2)}) collective-permute-start(bf16[512,512]{1,0:T(8,128)(2,1)S(1)} %bitcast.49), channel_id=1, source_target_pairs={{0,2},{1,3},{2,0},{3,1},{4,6},{5,7},{6,4},{7,5},{8,10},{9,11},{10,... | collective-permute-start | bytes 1572872 | tf_op jit(solution)/shard_map/ppermute | solution.py:76
  51.4 23.0 %collective-permute-start = (bf16[512,512]{1,0:T(8,128)(2,1)S(1)}, bf16[512,512]{1,0:T(8,128)(2,1)S(1)}, u32[]{:S(2)}, u32[]{:S(2)}) collective-permute-start(bf16[512,512]{1,0:T(8,128)(2,1)S(1)} %bitcast.50), channel_id=1, source_target_pairs={{0,3},{1,0},{2,1},{3,2},{4,7},{5,4},{6,5},{7,6},{8,11},{9,8},{10,9... | collective-permute-start | bytes 1572872 | tf_op jit(solution)/shard_map/ppermute | solution.py:76
  74.9 4.3 %copy-start.5 = (bf16[2048,512]{1,0:T(8,128)(2,1)S(1)}, bf16[2048,512]{1,0:T(8,128)(2,1)}, u32[]{:S(2)}) copy-start(bf16[2048,512]{1,0:T(8,128)(2,1)} %param.15) | copy-start | bytes 6291460
  77.9 6.1 %copy-start.1 = (f32[512,512]{0,1:T(8,128)}, f32[512,512]{0,1:T(8,128)S(1)}, u32[]{:S(2)}) copy-start(f32[512,512]{0,1:T(8,128)S(1)} %fusion.8) | copy-start | bytes 3145732
  79.2 3.7 %copy-start.2 = (bf16[512,1,128]{0,2,1:T(8,128)(2,1)}, bf16[512,1,128]{0,2,1:T(8,128)(2,1)S(1)}, u32[]{:S(2)}) copy-start(bf16[512,1,128]{0,2,1:T(8,128)(2,1)S(1)} %get-tuple-element.15) | copy-start | bytes 393220
  86.8 26.8 %all-to-all-start.1 = ((bf16[128,4,512]{2,1,0:T(4,128)(2,1)}), bf16[128,4,512]{2,1,0:T(4,128)(2,1)S(1)}, u32[]{:S(2)}, u32[]{:S(2)}) async-start(bf16[128,4,512]{2,1,0:T(4,128)(2,1)} %fusion.25), calls=%async_computation.1 | async-start | bytes 1048576 | tf_op jit(solution)/shard_map/all_to_all | solution.py:205
  116.8 11.1 %collective-permute-start.3 = (bf16[224,512]{1,0:T(8,128)(2,1)S(1)}, bf16[224,512]{1,0:T(8,128)(2,1)S(1)}, u32[]{:S(2)}, u32[]{:S(2)}) collective-permute-start(bf16[224,512]{1,0:T(8,128)(2,1)S(1)} %get-tuple-element.11), channel_id=1, source_target_pairs={{0,1},{1,2},{2,3},{3,0},{4,5},{5,6},{6,7},{7,4},{8,9},{9,10},{10,1... | collective-permute-start | bytes 688136 | tf_op jit(solution)/shard_map/ppermute | solution.py:106
  120.8 9.2 %collective-permute-start.5 = (bf16[224,512]{1,0:T(8,128)(2,1)S(1)}, bf16[224,512]{1,0:T(8,128)(2,1)S(1)}, u32[]{:S(2)}, u32[]{:S(2)}) collective-permute-start(bf16[224,512]{1,0:T(8,128)(2,1)S(1)} %get-tuple-element.12), channel_id=1, source_target_pairs={{0,3},{1,0},{2,1},{3,2},{4,7},{5,4},{6,5},{7,6},{8,11},{9,8},{10,9... | collective-permute-start | bytes 688136 | tf_op jit(solution)/shard_map/ppermute | solution.py:106
  123.3 10.4 %collective-permute-start.4 = (bf16[224,512]{1,0:T(8,128)(2,1)S(1)}, bf16[224,512]{1,0:T(8,128)(2,1)S(1)}, u32[]{:S(2)}, u32[]{:S(2)}) collective-permute-start(bf16[224,512]{1,0:T(8,128)(2,1)S(1)} %get-tuple-element.13), channel_id=1, source_target_pairs={{0,2},{1,3},{2,0},{3,1},{4,6},{5,7},{6,4},{7,5},{8,10},{9,11},{10,... | collective-permute-start | bytes 688136 | tf_op jit(solution)/shard_map/ppermute | solution.py:106

commit v12 on v11

--- a/solution.py
+++ b/solution.py
@@ -77,17 +77,11 @@
     return blocks
 
 
-def project_blocks(blocks, gain, query_weight, keyval_weight, axis_name):
-    position = lax.axis_index(axis_name)
-    offset = position * blocks[0].shape[1]
+def project_blocks(blocks, gain, query_weight, keyval_weight):
     rows = jnp.concatenate(blocks, axis=1)
-    normed = normalize(rows, jnp.roll(gain, -offset))
-    queries = jnp.dot(
-        normed, jnp.roll(query_weight, -offset, axis=0), preferred_element_type=jnp.float32
-    )
-    keyvals = jnp.dot(
-        normed, jnp.roll(keyval_weight, -offset, axis=0), preferred_element_type=jnp.float32
-    )
+    normed = normalize(rows, gain)
+    queries = jnp.dot(normed, query_weight, preferred_element_type=jnp.float32)
+    keyvals = jnp.dot(normed, keyval_weight, preferred_element_type=jnp.float32)
     return queries, keyvals
 
 
@@ -170,9 +164,18 @@
             concat_axis=0,
             tiled=True,
         )
+        tensor_offset = lax.axis_index("tensor") * arrived.shape[2]
+        arrived, gain_rolled, query_rolled, keyval_rolled = lax.optimization_barrier(
+            (
+                arrived,
+                jnp.roll(norm_gain, -tensor_offset),
+                jnp.roll(query_weight, -tensor_offset, axis=0),
+                jnp.roll(keyval_weight, -tensor_offset, axis=0),
+            )
+        )
         narrow_rows = to_request(arrived, shift_by)
         queries, keyvals = project_blocks(
-            ring_blocks(narrow_rows, "tensor"), norm_gain, query_weight, keyval_weight, "tensor"
+            ring_blocks(narrow_rows, "tensor"), gain_rolled, query_rolled, keyval_rolled
         )
         rotated_query = rotate_rows(queries, HD, chunk_first).astype(jnp.bfloat16)
         own_blocks = []

time: 136 us -> 135 us (level)
  other arithmetic: 16.6 us -> 23.2 us
  matrix products: 10.1 us -> 6.79 us
  starting transfers between devices: 45.3 us -> 42.1 us
    concatenate x0 -> x2, other arithmetic: none -> 6.72 us  [the longest x1 6.62 us: body(): jnp.roll(keyval_weight, -tensor_offset, axis=0)]
    all_to_all x1, waiting for transfers between devices: 17.3 us -> 10.7 us  [body(): lax.all_to_all(picked[:, chunk * chunk_slots:(chunk + 1) * chunk_slots],...]
    ppermute x3, waiting for transfers between devices: 17.9 us -> 21.7 us  [ring_blocks(): blocks.append(lax.ppermute(narrow, axis_name, perm))]
    dot_general x2, matrix products: 6.11 us -> 2.77 us  [the longest x1 1.39 us: project_blocks(): queries = jnp.dot(normed, query_weight, preferred_element_type=jnp.float32)]
    ppermute x3, waiting for transfers between devices: 5.87 us -> 8.28 us  [ring_output(): lax.ppermute(parts[shift], axis_name, perm).astype(jnp.float32)]
    ppermute x3, starting transfers between devices: 9.93 us -> 8.41 us  [ring_output(): lax.ppermute(parts[shift], axis_name, perm).astype(jnp.float32)]
    unnamed x13 -> x15, local copies, waits for them, and re-layouts: 2.9 us -> 2.9 us
  transfers between devices with their start and end apart: 8 -> 8, of which waited for: 7 -> 6; matrix products, arithmetic and copies ran while one was open for 15% -> 20% of each run, Pallas kernels for 0% -> 0%
where the time goes in v12:
time: 135 us; the launch traced here: 134 us
  waiting for transfers between devices  45.4 us (34%)
  starting transfers between devices  42.1 us (31%)
  other arithmetic  23.2 us (17%)
  local copies, waits for them, and re-layouts  13.7 us (10%)
  matrix products  6.79 us (5%)
  between operations  3.04 us (2%)
    ppermute x3, waiting for transfers between devices, ring_blocks(): blocks.append(lax.ppermute(narrow, axis_name, perm))  21.7 us
    all_to_all x1, starting transfers between devices, body(): lax.all_to_all(picked[:, chunk * chunk_slots:(chunk + 1) * chunk_slots],...  18.4 us
    all_to_all x1, waiting for transfers between devices, body(): lax.all_to_all(picked[:, chunk * chunk_slots:(chunk + 1) * chunk_slots],...  10.7 us
    ppermute x3, starting transfers between devices, ring_blocks(): blocks.append(lax.ppermute(narrow, axis_name, perm))  9.64 us
    ppermute x3, starting transfers between devices, ring_output(): lax.ppermute(parts[shift], axis_name, perm).astype(jnp.float32)  8.41 us
    ppermute x3, waiting for transfers between devices, ring_output(): lax.ppermute(parts[shift], axis_name, perm).astype(jnp.float32)  8.28 us
    concatenate x1, other arithmetic, body(): jnp.roll(keyval_weight, -tensor_offset, axis=0)  6.62 us
    all_to_all x1, starting transfers between devices, body(): lax.all_to_all(outgoing, 'seq', split_axis=0, concat_axis=0, tiled=True)  5.63 us
  transfers between devices with their start and end apart: 8, of which 6 were waited for; matrix products, arithmetic and copies ran while one was open for 20% of the time, Pallas kernels for 0%

profile of v12, /device:TPU:1, one launch (start us, length us, event | category | flops | bytes accessed | tf_op | source)
XLA Modules:
  0.0 134.2 jit_solution(1208367151582180324)
XLA Ops:
  4.3 18.4 %all-to-all-start = ((bf16[128,4,512]{2,1,0:T(4,128)(2,1)}), bf16[128,4,512]{2,1,0:T(4,128)(2,1)S(1)}, u32[]{:S(2)}, u32[]{:S(2)}) async-start(bf16[128,4,512]{2,1,0:T(4,128)(2,1)} %reshape.231), calls=%async_computation | async-start | bytes 1048576 | tf_op jit(solution)/shard_map/all_to_all | solution.py:160
  26.0 6.6 %fusion.4 = (bf16[2048,512]{1,0:T(8,128)(2,1)}, bf16[2048,512]{1,0:T(8,128)(2,1)}) fusion(s32[]{:T(128)S(6)} %select_n.94, bf16[2048,512]{1,0:T(8,128)(2,1)S(1)} %copy-done.1, bf16[2048,512]{1,0:T(8,128)(2,1)} %param.15), kind=kLoop, calls=%fused_computation.12 | loop fusion | flops 8388608 | bytes 8388612 | tf_op jit(solution)/shard_map/jit(_roll_dynamic)/concatenate | solution.py:173
  32.7 10.7 %all-to-all-done = bf16[128,4,512]{2,1,0:T(4,128)(2,1)S(1)} async-done(((bf16[128,4,512]{2,1,0:T(4,128)(2,1)}), bf16[128,4,512]{2,1,0:T(4,128)(2,1)S(1)}, u32[]{:S(2)}, u32[]{:S(2)}) %all-to-all-start) | async-done | bytes 524320 | tf_op jit(solution)/shard_map/all_to_all | solution.py:160
  43.9 4.5 %collective-permute-start = (bf16[512,512]{1,0:T(8,128)(2,1)S(1)}, bf16[512,512]{1,0:T(8,128)(2,1)S(1)}, u32[]{:S(2)}, u32[]{:S(2)}) collective-permute-start(bf16[512,512]{1,0:T(8,128)(2,1)S(1)} %bitcast.50), channel_id=1, source_target_pairs={{0,3},{1,0},{2,1},{3,2},{4,7},{5,4},{6,5},{7,6},{8,11},{9,8},{10,9... | collective-permute-start | bytes 1572872 | tf_op jit(solution)/shard_map/ppermute | solution.py:76
  48.4 2.4 %collective-permute-start.1 = (bf16[512,512]{1,0:T(8,128)(2,1)S(1)}, bf16[512,512]{1,0:T(8,128)(2,1)S(1)}, u32[]{:S(2)}, u32[]{:S(2)}) collective-permute-start(bf16[512,512]{1,0:T(8,128)(2,1)S(1)} %bitcast.51), channel_id=1, source_target_pairs={{0,2},{1,3},{2,0},{3,1},{4,6},{5,7},{6,4},{7,5},{8,10},{9,11},{10,... | collective-permute-start | bytes 1572872 | tf_op jit(solution)/shard_map/ppermute | solution.py:76
  50.8 2.7 %collective-permute-start.2 = (bf16[512,512]{1,0:T(8,128)(2,1)S(1)}, bf16[512,512]{1,0:T(8,128)(2,1)S(1)}, u32[]{:S(2)}, u32[]{:S(2)}) collective-permute-start(bf16[512,512]{1,0:T(8,128)(2,1)S(1)} %bitcast.52), channel_id=1, source_target_pairs={{0,1},{1,2},{2,3},{3,0},{4,5},{5,6},{6,7},{7,4},{8,9},{9,10},{10,1... | collective-permute-start | bytes 1572872 | tf_op jit(solution)/shard_map/ppermute | solution.py:76
  55.2 15.9 %collective-permute-done = bf16[512,512]{1,0:T(8,128)(2,1)S(1)} collective-permute-done((bf16[512,512]{1,0:T(8,128)(2,1)S(1)}, bf16[512,512]{1,0:T(8,128)(2,1)S(1)}, u32[]{:S(2)}, u32[]{:S(2)}) %collective-permute-start) | collective-permute-done | bytes 524320 | tf_op jit(solution)/shard_map/ppermute | solution.py:76
  71.2 5.7 %collective-permute-done.2 = bf16[512,512]{1,0:T(8,128)(2,1)S(1)} collective-permute-done((bf16[512,512]{1,0:T(8,128)(2,1)S(1)}, bf16[512,512]{1,0:T(8,128)(2,1)S(1)}, u32[]{:S(2)}, u32[]{:S(2)}) %collective-permute-start.2) | collective-permute-done | bytes 524320 | tf_op jit(solution)/shard_map/ppermute | solution.py:76
  77.4 1.4 %fusion.19 = f32[512,512]{0,1:T(8,128)S(1)} fusion(bf16[2048,512]{1,0:T(8,128)(2,1)S(1)} %copy-done.3, f32[2048]{0:T(1024)S(1)} %convert_element_type.85, f32[512]{0:T(512)S(1)} %add_rsqrt_fusion, bf16[512,512]{1,0:T(8,128)(2,1)S(1)} %collective-permute-done.2, bf16[512,512]{1,0:T(8,128)(2,1)S(1)} %collective-permute-done.1, ...), kind=kOutput, calls=%fused_computation.39 | convolution fusion | flops 1085276160 | bytes 5253120 | tf_op jit(solution)/shard_map/dot_general | solution.py:84
  78.9 1.2 fusion.37
  80.1 1.4 %fusion.21 = f32[512,512]{0,1:T(8,128)S(1)} fusion(bf16[2048,512]{1,0:T(8,128)(2,1)S(1)} %copy-done.2, f32[2048]{0:T(1024)S(1)} %convert_element_type.85, f32[512]{0:T(512)S(1)} %add_rsqrt_fusion, bf16[512,512]{1,0:T(8,128)(2,1)S(1)} %collective-permute-done.2, bf16[512,512]{1,0:T(8,128)(2,1)S(1)} %collective-permute-done.1, ...), kind=kOutput, calls=%fused_computation.40 | convolution fusion | flops 1085276160 | bytes 5253120 | tf_op jit(solution)/shard_map/dot_general | solution.py:83
  84.4 1.7 %fusion.23 = bf16[128,4,512]{2,1,0:T(4,128)(2,1)} fusion(s32[]{:T(128)S(6)} %select_n.111, bf16[128,4,512]{2,1,0:T(4,128)(2,1)S(1)} %bitcast.56), kind=kLoop, calls=%fused_computation.41 | loop fusion | flops 262144 | bytes 1048580 | tf_op jit(solution)/shard_map/jit(_roll_dynamic)/concatenate | solution.py:68
  86.0 5.6 %all-to-all-start.1 = ((bf16[128,4,512]{2,1,0:T(4,128)(2,1)}), bf16[128,4,512]{2,1,0:T(4,128)(2,1)S(1)}, u32[]{:S(2)}, u32[]{:S(2)}) async-start(bf16[128,4,512]{2,1,0:T(4,128)(2,1)} %fusion.23), calls=%async_computation.1 | async-start | bytes 1048576 | tf_op jit(solution)/shard_map/all_to_all | solution.py:208
  92.3 2.9 %copy.24 = bf16[512,2048]{0,1:T(8,128)(2,1)S(1)} copy(bf16[512,2048]{1,0:T(8,128)(2,1)} %param.17) | data formatting | bytes 4194304 | tf_op args[4]
  95.2 5.0 %fusion.3 = bf16[512,2048]{0,1:T(8,128)(2,1)} fusion(s32[]{:T(128)S(6)} %select_n.86, bf16[512,2048]{0,1:T(8,128)(2,1)S(1)} %copy.24), kind=kLoop, calls=%fused_computation.11 | loop fusion | flops 4194304 | bytes 4194308 | tf_op jit(solution)/shard_map/jit(_roll_dynamic)/concatenate | solution.py:92
  100.1 2.8 %copy.26 = bf16[512,4,512]{2,0,1:T(8,128)(2,1)S(1)} copy(bf16[512,4,512]{0,2,1:T(8,128)(2,1)} %bitcast.49) | data formatting | bytes 4194304 | tf_op jit(solution)/shard_map/reshape | solution.py:93
  106.4 1.3 copy.30
  107.7 4.7 %all-to-all-done.1 = bf16[128,4,512]{2,1,0:T(4,128)(2,1)S(1)} async-done(((bf16[128,4,512]{2,1,0:T(4,128)(2,1)}), bf16[128,4,512]{2,1,0:T(4,128)(2,1)S(1)}, u32[]{:S(2)}, u32[]{:S(2)}) %all-to-all-start.1) | async-done | bytes 524320 | tf_op jit(solution)/shard_map/all_to_all | solution.py:208
  113.3 1.5 %fusion.26 = bf16[256,512]{1,0:T(8,128)(2,1)S(1)} fusion(bf16[512,512]{1,0:T(8,128)(2,1)} %reshape.236, s32[512]{0:T(512)S(1)} %add.131, pred[512]{0:T(512)(128)(4,1)S(1)} %compare_and_fusion), kind=kOutput, calls=%fused_computation.52 | convolution fusion | flops 134479872 | bytes 788992 | tf_op jit(solution)/shard_map/dot_general | solution.py:212
  115.5 1.9 %collective-permute-start.3 = (bf16[224,512]{1,0:T(8,128)(2,1)S(1)}, bf16[224,512]{1,0:T(8,128)(2,1)S(1)}, u32[]{:S(2)}, u32[]{:S(2)}) collective-permute-start(bf16[224,512]{1,0:T(8,128)(2,1)S(1)} %get-tuple-element.19), channel_id=1, source_target_pairs={{0,1},{1,2},{2,3},{3,0},{4,5},{5,6},{6,7},{7,4},{8,9},{9,10},{10,1... | collective-permute-start | bytes 688136 | tf_op jit(solution)/shard_map/ppermute | solution.py:100
  117.5 3.4 %collective-permute-start.4 = (bf16[224,512]{1,0:T(8,128)(2,1)S(1)}, bf16[224,512]{1,0:T(8,128)(2,1)S(1)}, u32[]{:S(2)}, u32[]{:S(2)}) collective-permute-start(bf16[224,512]{1,0:T(8,128)(2,1)S(1)} %get-tuple-element.21), channel_id=1, source_target_pairs={{0,2},{1,3},{2,0},{3,1},{4,6},{5,7},{6,4},{7,5},{8,10},{9,11},{10,... | collective-permute-start | bytes 688136 | tf_op jit(solution)/shard_map/ppermute | solution.py:100
  120.9 3.1 %collective-permute-start.5 = (bf16[224,512]{1,0:T(8,128)(2,1)S(1)}, bf16[224,512]{1,0:T(8,128)(2,1)S(1)}, u32[]{:S(2)}, u32[]{:S(2)}) collective-permute-start(bf16[224,512]{1,0:T(8,128)(2,1)S(1)} %get-tuple-element.20), channel_id=1, source_target_pairs={{0,3},{1,0},{2,1},{3,2},{4,7},{5,4},{6,5},{7,6},{8,11},{9,8},{10,9... | collective-permute-start | bytes 688136 | tf_op jit(solution)/shard_map/ppermute | solution.py:100
  125.1 6.0 %collective-permute-done.3 = bf16[224,512]{1,0:T(8,128)(2,1)S(1)} collective-permute-done((bf16[224,512]{1,0:T(8,128)(2,1)S(1)}, bf16[224,512]{1,0:T(8,128)(2,1)S(1)}, u32[]{:S(2)}, u32[]{:S(2)}) %collective-permute-start.3) | collective-permute-done | bytes 229408 | tf_op jit(solution)/shard_map/ppermute | solution.py:100
  131.1 2.3 %collective-permute-done.5 = bf16[224,512]{1,0:T(8,128)(2,1)S(1)} collective-permute-done((bf16[224,512]{1,0:T(8,128)(2,1)S(1)}, bf16[224,512]{1,0:T(8,128)(2,1)S(1)}, u32[]{:S(2)}, u32[]{:S(2)}) %collective-permute-start.5) | collective-permute-done | bytes 229408 | tf_op jit(solution)/shard_map/ppermute | solution.py:100
  (64 shorter events, 18.1 us)
Async XLA Ops:
  0.6 2.4 %copy-start = (bf16[256,512]{1,0:T(8,128)(2,1)S(1)}, bf16[256,512]{1,0:T(8,128)(2,1)}, u32[]{:S(2)}) copy-start(bf16[256,512]{1,0:T(8,128)(2,1)} %param.13) | copy-start | bytes 786436
  0.6 25.3 %copy-start.6 = (bf16[2048]{0:T(1024)(128)(2,1)S(1)}, bf16[2048]{0:T(1024)(128)(2,1)}, u32[]{:S(2)}) copy-start(bf16[2048]{0:T(1024)(128)(2,1)} %param.14) | copy-start | bytes 12292
  0.7 25.4 %copy-start.1 = (bf16[2048,512]{1,0:T(8,128)(2,1)S(1)}, bf16[2048,512]{1,0:T(8,128)(2,1)}, u32[]{:S(2)}) copy-start(bf16[2048,512]{1,0:T(8,128)(2,1)} %param.16) | copy-start | bytes 6291460
  4.3 39.0 %all-to-all-start = ((bf16[128,4,512]{2,1,0:T(4,128)(2,1)}), bf16[128,4,512]{2,1,0:T(4,128)(2,1)S(1)}, u32[]{:S(2)}, u32[]{:S(2)}) async-start(bf16[128,4,512]{2,1,0:T(4,128)(2,1)} %reshape.231), calls=%async_computation | async-start | bytes 1048576 | tf_op jit(solution)/shard_map/all_to_all | solution.py:160
  43.4 34.0 %copy-start.3 = (bf16[2048,512]{1,0:T(8,128)(2,1)S(1)}, bf16[2048,512]{1,0:T(8,128)(2,1)}, u32[]{:S(2)}) copy-start(bf16[2048,512]{1,0:T(8,128)(2,1)} %get-tuple-element.11) | copy-start | bytes 6291460
  43.9 27.3 %collective-permute-start = (bf16[512,512]{1,0:T(8,128)(2,1)S(1)}, bf16[512,512]{1,0:T(8,128)(2,1)S(1)}, u32[]{:S(2)}, u32[]{:S(2)}) collective-permute-start(bf16[512,512]{1,0:T(8,128)(2,1)S(1)} %bitcast.50), channel_id=1, source_target_pairs={{0,3},{1,0},{2,1},{3,2},{4,7},{5,4},{6,5},{7,6},{8,11},{9,8},{10,9... | collective-permute-start | bytes 1572872 | tf_op jit(solution)/shard_map/ppermute | solution.py:76
  48.4 22.8 %collective-permute-start.1 = (bf16[512,512]{1,0:T(8,128)(2,1)S(1)}, bf16[512,512]{1,0:T(8,128)(2,1)S(1)}, u32[]{:S(2)}, u32[]{:S(2)}) collective-permute-start(bf16[512,512]{1,0:T(8,128)(2,1)S(1)} %bitcast.51), channel_id=1, source_target_pairs={{0,2},{1,3},{2,0},{3,1},{4,6},{5,7},{6,4},{7,5},{8,10},{9,11},{10,... | collective-permute-start | bytes 1572872 | tf_op jit(solution)/shard_map/ppermute | solution.py:76
  50.8 26.1 %collective-permute-start.2 = (bf16[512,512]{1,0:T(8,128)(2,1)S(1)}, bf16[512,512]{1,0:T(8,128)(2,1)S(1)}, u32[]{:S(2)}, u32[]{:S(2)}) collective-permute-start(bf16[512,512]{1,0:T(8,128)(2,1)S(1)} %bitcast.52), channel_id=1, source_target_pairs={{0,1},{1,2},{2,3},{3,0},{4,5},{5,6},{6,7},{7,4},{8,9},{9,10},{10,1... | collective-permute-start | bytes 1572872 | tf_op jit(solution)/shard_map/ppermute | solution.py:76
  77.4 2.6 %copy-start.2 = (bf16[2048,512]{1,0:T(8,128)(2,1)S(1)}, bf16[2048,512]{1,0:T(8,128)(2,1)}, u32[]{:S(2)}) copy-start(bf16[2048,512]{1,0:T(8,128)(2,1)} %get-tuple-element.10) | copy-start | bytes 6291460
  78.8 4.4 %copy-start.4 = (f32[512,512]{0,1:T(8,128)}, f32[512,512]{0,1:T(8,128)S(1)}, u32[]{:S(2)}) copy-start(f32[512,512]{0,1:T(8,128)S(1)} %fusion.19) | copy-start | bytes 3145732
  80.1 2.0 %copy-start.5 = (bf16[512,1,128]{0,2,1:T(8,128)(2,1)}, bf16[512,1,128]{0,2,1:T(8,128)(2,1)S(1)}, u32[]{:S(2)}) copy-start(bf16[512,1,128]{0,2,1:T(8,128)(2,1)S(1)} %get-tuple-element.23) | copy-start | bytes 393220
  86.0 26.3 %all-to-all-start.1 = ((bf16[128,4,512]{2,1,0:T(4,128)(2,1)}), bf16[128,4,512]{2,1,0:T(4,128)(2,1)S(1)}, u32[]{:S(2)}, u32[]{:S(2)}) async-start(bf16[128,4,512]{2,1,0:T(4,128)(2,1)} %fusion.23), calls=%async_computation.1 | async-start | bytes 1048576 | tf_op jit(solution)/shard_map/all_to_all | solution.py:208
  115.5 15.6 %collective-permute-start.3 = (bf16[224,512]{1,0:T(8,128)(2,1)S(1)}, bf16[224,512]{1,0:T(8,128)(2,1)S(1)}, u32[]{:S(2)}, u32[]{:S(2)}) collective-permute-start(bf16[224,512]{1,0:T(8,128)(2,1)S(1)} %get-tuple-element.19), channel_id=1, source_target_pairs={{0,1},{1,2},{2,3},{3,0},{4,5},{5,6},{6,7},{7,4},{8,9},{9,10},{10,1... | collective-permute-start | bytes 688136 | tf_op jit(solution)/shard_map/ppermute | solution.py:100
  117.5 13.7 %collective-permute-start.4 = (bf16[224,512]{1,0:T(8,128)(2,1)S(1)}, bf16[224,512]{1,0:T(8,128)(2,1)S(1)}, u32[]{:S(2)}, u32[]{:S(2)}) collective-permute-start(bf16[224,512]{1,0:T(8,128)(2,1)S(1)} %get-tuple-element.21), channel_id=1, source_target_pairs={{0,2},{1,3},{2,0},{3,1},{4,6},{5,7},{6,4},{7,5},{8,10},{9,11},{10,... | collective-permute-start | bytes 688136 | tf_op jit(solution)/shard_map/ppermute | solution.py:100
  120.9 12.5 %collective-permute-start.5 = (bf16[224,512]{1,0:T(8,128)(2,1)S(1)}, bf16[224,512]{1,0:T(8,128)(2,1)S(1)}, u32[]{:S(2)}, u32[]{:S(2)}) collective-permute-start(bf16[224,512]{1,0:T(8,128)(2,1)S(1)} %get-tuple-element.20), channel_id=1, source_target_pairs={{0,3},{1,0},{2,1},{3,2},{4,7},{5,4},{6,5},{7,6},{8,11},{9,8},{10,9... | collective-permute-start | bytes 688136 | tf_op jit(solution)/shard_map/ppermute | solution.py:100

commit v13 on v12

--- a/solution.py
+++ b/solution.py
@@ -77,12 +77,11 @@
     return blocks
 
 
-def project_blocks(blocks, gain, query_weight, keyval_weight):
+def project_blocks(blocks, gain, joint_weight, query_width):
     rows = jnp.concatenate(blocks, axis=1)
     normed = normalize(rows, gain)
-    queries = jnp.dot(normed, query_weight, preferred_element_type=jnp.float32)
-    keyvals = jnp.dot(normed, keyval_weight, preferred_element_type=jnp.float32)
-    return queries, keyvals
+    joint = jnp.dot(normed, joint_weight, preferred_element_type=jnp.float32)
+    return joint[:, :query_width], joint[:, query_width:]
 
 
 def ring_output(local_attention, output_weight, axis_name):
@@ -165,17 +164,18 @@
             tiled=True,
         )
         tensor_offset = lax.axis_index("tensor") * arrived.shape[2]
-        arrived, gain_rolled, query_rolled, keyval_rolled = lax.optimization_barrier(
+        arrived, gain_rolled, joint_rolled = lax.optimization_barrier(
             (
                 arrived,
                 jnp.roll(norm_gain, -tensor_offset),
-                jnp.roll(query_weight, -tensor_offset, axis=0),
-                jnp.roll(keyval_weight, -tensor_offset, axis=0),
+                jnp.roll(
+                    jnp.concatenate([query_weight, keyval_weight], axis=1), -tensor_offset, axis=0
+                ),
             )
         )
         narrow_rows = to_request(arrived, shift_by)
         queries, keyvals = project_blocks(
-            ring_blocks(narrow_rows, "tensor"), gain_rolled, query_rolled, keyval_rolled
+            ring_blocks(narrow_rows, "tensor"), gain_rolled, joint_rolled, query_weight.shape[1]
         )
         rotated_query = rotate_rows(queries, HD, chunk_first).astype(jnp.bfloat16)
         own_blocks = []

time: 135 us -> 141 us (1.044)
  other arithmetic: 23.2 us -> 28.5 us
  starting transfers between devices: 42.1 us -> 45.8 us
  waiting for transfers between devices: 45.4 us -> 42 us
    all_to_all x1, waiting for transfers between devices: 10.7 us -> 4.55 us  [body(): lax.all_to_all(picked[:, chunk * chunk_slots:(chunk + 1) * chunk_slots],...]
    concatenate x1, other arithmetic: 6.62 us -> 12.1 us  [body(): jnp.roll(jnp.concatenate([query_weight, keyval_weight], axis=1), -tensor_...]
    all_to_all x1, starting transfers between devices: 5.63 us -> 9.33 us  [body(): lax.all_to_all(outgoing, 'seq', split_axis=0, concat_axis=0, tiled=True)]
    all_to_all x1, waiting for transfers between devices: 4.7 us -> 7.53 us  [body(): lax.all_to_all(outgoing, 'seq', split_axis=0, concat_axis=0, tiled=True)]
    unnamed x15 -> x16, local copies, waits for them, and re-layouts: 2.9 us -> 4.19 us
  transfers between devices with their start and end apart: 8 -> 8, of which waited for: 6 -> 6; matrix products, arithmetic and copies ran while one was open for 20% -> 21% of each run, Pallas kernels for 0% -> 0%
where the time goes in v13:
time: 141 us; the launch traced here: 140 us
  starting transfers between devices  45.8 us (32%)
  waiting for transfers between devices  42 us (30%)
  other arithmetic  28.5 us (20%)
  local copies, waits for them, and re-layouts  14.5 us (10%)
  matrix products  6.42 us (5%)
  between operations  3.04 us (2%)
    ppermute x3, waiting for transfers between devices, ring_blocks(): blocks.append(lax.ppermute(narrow, axis_name, perm))  21.7 us
    all_to_all x1, starting transfers between devices, body(): lax.all_to_all(picked[:, chunk * chunk_slots:(chunk + 1) * chunk_slots],...  18.4 us
    concatenate x1, other arithmetic, body(): jnp.roll(jnp.concatenate([query_weight, keyval_weight], axis=1), -tensor_...  12.1 us
    ppermute x3, starting transfers between devices, ring_blocks(): blocks.append(lax.ppermute(narrow, axis_name, perm))  9.64 us
    all_to_all x1, starting transfers between devices, body(): lax.all_to_all(outgoing, 'seq', split_axis=0, concat_axis=0, tiled=True)  9.33 us
    ppermute x3, starting transfers between devices, ring_output(): lax.ppermute(parts[shift], axis_name, perm).astype(jnp.float32)  8.43 us
    ppermute x3, waiting for transfers between devices, ring_output(): lax.ppermute(parts[shift], axis_name, perm).astype(jnp.float32)  8.26 us
    all_to_all x1, waiting for transfers between devices, body(): lax.all_to_all(outgoing, 'seq', split_axis=0, concat_axis=0, tiled=True)  7.53 us
  transfers between devices with their start and end apart: 8, of which 6 were waited for; matrix products, arithmetic and copies ran while one was open for 21% of the time, Pallas kernels for 0%

profile of v13, /device:TPU:1, one launch (start us, length us, event | category | flops | bytes accessed | tf_op | source)
XLA Modules:
  0.0 140.3 jit_solution(10925127155073484647)
XLA Ops:
  4.3 18.4 %all-to-all-start = ((bf16[128,4,512]{2,1,0:T(4,128)(2,1)}), bf16[128,4,512]{2,1,0:T(4,128)(2,1)S(1)}, u32[]{:S(2)}, u32[]{:S(2)}) async-start(bf16[128,4,512]{2,1,0:T(4,128)(2,1)} %reshape.231), calls=%async_computation | async-start | bytes 1048576 | tf_op jit(solution)/shard_map/all_to_all | solution.py:159
  26.7 12.1 %fusion.4 = bf16[2048,1024]{1,0:T(8,128)(2,1)} fusion(s32[]{:T(128)S(6)} %select_n.93, bf16[2048,512]{1,0:T(8,128)(2,1)S(1)} %copy-done.2, bf16[2048,512]{1,0:T(8,128)(2,1)} %param.14), kind=kLoop, calls=%fused_computation.10 | loop fusion | flops 16777216 | bytes 8388612 | tf_op jit(solution)/shard_map/jit(_roll_dynamic)/concatenate | solution.py:171
  38.8 4.5 %all-to-all-done = bf16[128,4,512]{2,1,0:T(4,128)(2,1)S(1)} async-done(((bf16[128,4,512]{2,1,0:T(4,128)(2,1)}), bf16[128,4,512]{2,1,0:T(4,128)(2,1)S(1)}, u32[]{:S(2)}, u32[]{:S(2)}) %all-to-all-start) | async-done | bytes 524320 | tf_op jit(solution)/shard_map/all_to_all | solution.py:159
  43.9 4.5 %collective-permute-start = (bf16[512,512]{1,0:T(8,128)(2,1)S(1)}, bf16[512,512]{1,0:T(8,128)(2,1)S(1)}, u32[]{:S(2)}, u32[]{:S(2)}) collective-permute-start(bf16[512,512]{1,0:T(8,128)(2,1)S(1)} %bitcast.49), channel_id=1, source_target_pairs={{0,3},{1,0},{2,1},{3,2},{4,7},{5,4},{6,5},{7,6},{8,11},{9,8},{10,9... | collective-permute-start | bytes 1572872 | tf_op jit(solution)/shard_map/ppermute | solution.py:76
  48.4 2.4 %collective-permute-start.1 = (bf16[512,512]{1,0:T(8,128)(2,1)S(1)}, bf16[512,512]{1,0:T(8,128)(2,1)S(1)}, u32[]{:S(2)}, u32[]{:S(2)}) collective-permute-start(bf16[512,512]{1,0:T(8,128)(2,1)S(1)} %bitcast.50), channel_id=1, source_target_pairs={{0,2},{1,3},{2,0},{3,1},{4,6},{5,7},{6,4},{7,5},{8,10},{9,11},{10,... | collective-permute-start | bytes 1572872 | tf_op jit(solution)/shard_map/ppermute | solution.py:76
  50.8 2.7 %collective-permute-start.2 = (bf16[512,512]{1,0:T(8,128)(2,1)S(1)}, bf16[512,512]{1,0:T(8,128)(2,1)S(1)}, u32[]{:S(2)}, u32[]{:S(2)}) collective-permute-start(bf16[512,512]{1,0:T(8,128)(2,1)S(1)} %bitcast.51), channel_id=1, source_target_pairs={{0,1},{1,2},{2,3},{3,0},{4,5},{5,6},{6,7},{7,4},{8,9},{9,10},{10,1... | collective-permute-start | bytes 1572872 | tf_op jit(solution)/shard_map/ppermute | solution.py:76
  55.2 15.9 %collective-permute-done = bf16[512,512]{1,0:T(8,128)(2,1)S(1)} collective-permute-done((bf16[512,512]{1,0:T(8,128)(2,1)S(1)}, bf16[512,512]{1,0:T(8,128)(2,1)S(1)}, u32[]{:S(2)}, u32[]{:S(2)}) %collective-permute-start) | collective-permute-done | bytes 524320 | tf_op jit(solution)/shard_map/ppermute | solution.py:76
  71.1 5.8 %collective-permute-done.2 = bf16[512,512]{1,0:T(8,128)(2,1)S(1)} collective-permute-done((bf16[512,512]{1,0:T(8,128)(2,1)S(1)}, bf16[512,512]{1,0:T(8,128)(2,1)S(1)}, u32[]{:S(2)}, u32[]{:S(2)}) %collective-permute-start.2) | collective-permute-done | bytes 524320 | tf_op jit(solution)/shard_map/ppermute | solution.py:76
  77.4 2.4 %fusion.7 = f32[512,1024]{1,0:T(8,128)S(1)} fusion(bf16[2048,1024]{1,0:T(8,128)(2,1)S(1)} %copy-done.1, f32[2048]{0:T(1024)S(1)} %convert_element_type.85, f32[512]{0:T(512)S(1)} %add_rsqrt_fusion, bf16[512,512]{1,0:T(8,128)(2,1)S(1)} %collective-permute-done.2, bf16[512,512]{1,0:T(8,128)(2,1)S(1)} %collective-permute-done.1, ...), kind=kOutput, calls=%fused_computation.15 | convolution fusion | flops 2159017984 | bytes 8398848 | tf_op jit(solution)/shard_map/dot_general | solution.py:83
  80.0 1.2 copy-done.3
  81.2 1.2 fusion.38
  86.9 1.7 %fusion.24 = bf16[128,4,512]{2,1,0:T(4,128)(2,1)} fusion(s32[]{:T(128)S(6)} %select_n.104, bf16[128,4,512]{2,1,0:T(4,128)(2,1)S(1)} %bitcast.55), kind=kLoop, calls=%fused_computation.43 | loop fusion | flops 262144 | bytes 1048580 | tf_op jit(solution)/shard_map/jit(_roll_dynamic)/concatenate | solution.py:68
  88.6 9.3 %all-to-all-start.1 = ((bf16[128,4,512]{2,1,0:T(4,128)(2,1)}), bf16[128,4,512]{2,1,0:T(4,128)(2,1)S(1)}, u32[]{:S(2)}, u32[]{:S(2)}) async-start(bf16[128,4,512]{2,1,0:T(4,128)(2,1)} %fusion.24), calls=%async_computation.1 | async-start | bytes 1048576 | tf_op jit(solution)/shard_map/all_to_all | solution.py:208
  98.5 2.9 %copy.21 = bf16[512,2048]{0,1:T(8,128)(2,1)S(1)} copy(bf16[512,2048]{1,0:T(8,128)(2,1)} %param.15) | data formatting | bytes 4194304 | tf_op args[4]
  101.4 4.9 %fusion.6 = bf16[512,2048]{0,1:T(8,128)(2,1)} fusion(s32[]{:T(128)S(6)} %select_n.85, bf16[512,2048]{0,1:T(8,128)(2,1)S(1)} %copy.21), kind=kLoop, calls=%fused_computation.14 | loop fusion | flops 4194304 | bytes 4194308 | tf_op jit(solution)/shard_map/jit(_roll_dynamic)/concatenate | solution.py:91
  106.3 2.8 %copy.23 = bf16[512,4,512]{2,0,1:T(8,128)(2,1)S(1)} copy(bf16[512,4,512]{0,2,1:T(8,128)(2,1)} %bitcast.48) | data formatting | bytes 4194304 | tf_op jit(solution)/shard_map/reshape | solution.py:92
  110.9 7.5 %all-to-all-done.1 = bf16[128,4,512]{2,1,0:T(4,128)(2,1)S(1)} async-done(((bf16[128,4,512]{2,1,0:T(4,128)(2,1)}), bf16[128,4,512]{2,1,0:T(4,128)(2,1)S(1)}, u32[]{:S(2)}, u32[]{:S(2)}) %all-to-all-start.1) | async-done | bytes 524320 | tf_op jit(solution)/shard_map/all_to_all | solution.py:208
  119.4 1.5 %fusion.27 = bf16[256,512]{1,0:T(8,128)(2,1)S(1)} fusion(bf16[512,512]{1,0:T(8,128)(2,1)} %reshape.236, s32[512]{0:T(512)S(1)} %add.128, pred[512]{0:T(512)(128)(4,1)S(1)} %compare_and_fusion), kind=kOutput, calls=%fused_computation.54 | convolution fusion | flops 134479872 | bytes 788992 | tf_op jit(solution)/shard_map/dot_general | solution.py:212
  121.6 1.9 %collective-permute-start.3 = (bf16[224,512]{1,0:T(8,128)(2,1)S(1)}, bf16[224,512]{1,0:T(8,128)(2,1)S(1)}, u32[]{:S(2)}, u32[]{:S(2)}) collective-permute-start(bf16[224,512]{1,0:T(8,128)(2,1)S(1)} %get-tuple-element.16), channel_id=1, source_target_pairs={{0,1},{1,2},{2,3},{3,0},{4,5},{5,6},{6,7},{7,4},{8,9},{9,10},{10,1... | collective-permute-start | bytes 688136 | tf_op jit(solution)/shard_map/ppermute | solution.py:99
  123.6 3.4 %collective-permute-start.4 = (bf16[224,512]{1,0:T(8,128)(2,1)S(1)}, bf16[224,512]{1,0:T(8,128)(2,1)S(1)}, u32[]{:S(2)}, u32[]{:S(2)}) collective-permute-start(bf16[224,512]{1,0:T(8,128)(2,1)S(1)} %get-tuple-element.18), channel_id=1, source_target_pairs={{0,2},{1,3},{2,0},{3,1},{4,6},{5,7},{6,4},{7,5},{8,10},{9,11},{10,... | collective-permute-start | bytes 688136 | tf_op jit(solution)/shard_map/ppermute | solution.py:99
  127.0 3.1 %collective-permute-start.5 = (bf16[224,512]{1,0:T(8,128)(2,1)S(1)}, bf16[224,512]{1,0:T(8,128)(2,1)S(1)}, u32[]{:S(2)}, u32[]{:S(2)}) collective-permute-start(bf16[224,512]{1,0:T(8,128)(2,1)S(1)} %get-tuple-element.17), channel_id=1, source_target_pairs={{0,3},{1,0},{2,1},{3,2},{4,7},{5,4},{6,5},{7,6},{8,11},{9,8},{10,9... | collective-permute-start | bytes 688136 | tf_op jit(solution)/shard_map/ppermute | solution.py:99
  130.1 1.1 broadcast_select_fusion
  131.2 6.0 %collective-permute-done.3 = bf16[224,512]{1,0:T(8,128)(2,1)S(1)} collective-permute-done((bf16[224,512]{1,0:T(8,128)(2,1)S(1)}, bf16[224,512]{1,0:T(8,128)(2,1)S(1)}, u32[]{:S(2)}, u32[]{:S(2)}) %collective-permute-start.3) | collective-permute-done | bytes 229408 | tf_op jit(solution)/shard_map/ppermute | solution.py:99
  137.2 2.3 %collective-permute-done.5 = bf16[224,512]{1,0:T(8,128)(2,1)S(1)} collective-permute-done((bf16[224,512]{1,0:T(8,128)(2,1)S(1)}, bf16[224,512]{1,0:T(8,128)(2,1)S(1)}, u32[]{:S(2)}, u32[]{:S(2)}) %collective-permute-start.5) | collective-permute-done | bytes 229408 | tf_op jit(solution)/shard_map/ppermute | solution.py:99
  (65 shorter events, 17.6 us)
Async XLA Ops:
  0.6 2.4 %copy-start = (bf16[256,512]{1,0:T(8,128)(2,1)S(1)}, bf16[256,512]{1,0:T(8,128)(2,1)}, u32[]{:S(2)}) copy-start(bf16[256,512]{1,0:T(8,128)(2,1)} %param.11) | copy-start | bytes 786436
  0.6 26.1 %copy-start.2 = (bf16[2048,512]{1,0:T(8,128)(2,1)S(1)}, bf16[2048,512]{1,0:T(8,128)(2,1)}, u32[]{:S(2)}) copy-start(bf16[2048,512]{1,0:T(8,128)(2,1)} %param.13) | copy-start | bytes 6291460
  4.3 39.0 %all-to-all-start = ((bf16[128,4,512]{2,1,0:T(4,128)(2,1)}), bf16[128,4,512]{2,1,0:T(4,128)(2,1)S(1)}, u32[]{:S(2)}, u32[]{:S(2)}) async-start(bf16[128,4,512]{2,1,0:T(4,128)(2,1)} %reshape.231), calls=%async_computation | async-start | bytes 1048576 | tf_op jit(solution)/shard_map/all_to_all | solution.py:159
  43.3 34.1 %copy-start.1 = (bf16[2048,1024]{1,0:T(8,128)(2,1)S(1)}, bf16[2048,1024]{1,0:T(8,128)(2,1)}, u32[]{:S(2)}) copy-start(bf16[2048,1024]{1,0:T(8,128)(2,1)} %fusion.4) | copy-start | bytes 12582916
  43.9 27.3 %collective-permute-start = (bf16[512,512]{1,0:T(8,128)(2,1)S(1)}, bf16[512,512]{1,0:T(8,128)(2,1)S(1)}, u32[]{:S(2)}, u32[]{:S(2)}) collective-permute-start(bf16[512,512]{1,0:T(8,128)(2,1)S(1)} %bitcast.49), channel_id=1, source_target_pairs={{0,3},{1,0},{2,1},{3,2},{4,7},{5,4},{6,5},{7,6},{8,11},{9,8},{10,9... | collective-permute-start | bytes 1572872 | tf_op jit(solution)/shard_map/ppermute | solution.py:76
  48.4 22.8 %collective-permute-start.1 = (bf16[512,512]{1,0:T(8,128)(2,1)S(1)}, bf16[512,512]{1,0:T(8,128)(2,1)S(1)}, u32[]{:S(2)}, u32[]{:S(2)}) collective-permute-start(bf16[512,512]{1,0:T(8,128)(2,1)S(1)} %bitcast.50), channel_id=1, source_target_pairs={{0,2},{1,3},{2,0},{3,1},{4,6},{5,7},{6,4},{7,5},{8,10},{9,11},{10,... | collective-permute-start | bytes 1572872 | tf_op jit(solution)/shard_map/ppermute | solution.py:76
  50.8 26.1 %collective-permute-start.2 = (bf16[512,512]{1,0:T(8,128)(2,1)S(1)}, bf16[512,512]{1,0:T(8,128)(2,1)S(1)}, u32[]{:S(2)}, u32[]{:S(2)}) collective-permute-start(bf16[512,512]{1,0:T(8,128)(2,1)S(1)} %bitcast.51), channel_id=1, source_target_pairs={{0,1},{1,2},{2,3},{3,0},{4,5},{5,6},{6,7},{7,4},{8,9},{9,10},{10,1... | collective-permute-start | bytes 1572872 | tf_op jit(solution)/shard_map/ppermute | solution.py:76
  79.8 1.4 copy-start.3
  82.3 2.3 %copy-start.5 = (bf16[512,1,128]{2,0,1:T(8,128)(2,1)}, bf16[512,1,128]{2,0,1:T(8,128)(2,1)S(1)}, u32[]{:S(2)}) copy-start(bf16[512,1,128]{2,0,1:T(8,128)(2,1)S(1)} %get-tuple-element.20) | copy-start | bytes 393220
  83.6 1.6 %copy-start.4 = (f32[512,1024]{1,0:T(8,128)S(1)}, f32[512,1024]{1,0:T(8,128)}, u32[]{:S(2)}) copy-start(f32[512,1024]{1,0:T(8,128)} %copy-done.3) | copy-start | bytes 6291460
  88.6 29.9 %all-to-all-start.1 = ((bf16[128,4,512]{2,1,0:T(4,128)(2,1)}), bf16[128,4,512]{2,1,0:T(4,128)(2,1)S(1)}, u32[]{:S(2)}, u32[]{:S(2)}) async-start(bf16[128,4,512]{2,1,0:T(4,128)(2,1)} %fusion.24), calls=%async_computation.1 | async-start | bytes 1048576 | tf_op jit(solution)/shard_map/all_to_all | solution.py:208
  106.3 4.5 %copy-start.6 = (bf16[512,1,128]{2,0,1:T(8,128)(2,1)S(1)}, bf16[512,1,128]{2,0,1:T(8,128)(2,1)}, u32[]{:S(2)}) copy-start(bf16[512,1,128]{2,0,1:T(8,128)(2,1)} %copy-done.5) | copy-start | bytes 393220
  121.6 15.6 %collective-permute-start.3 = (bf16[224,512]{1,0:T(8,128)(2,1)S(1)}, bf16[224,512]{1,0:T(8,128)(2,1)S(1)}, u32[]{:S(2)}, u32[]{:S(2)}) collective-permute-start(bf16[224,512]{1,0:T(8,128)(2,1)S(1)} %get-tuple-element.16), channel_id=1, source_target_pairs={{0,1},{1,2},{2,3},{3,0},{4,5},{5,6},{6,7},{7,4},{8,9},{9,10},{10,1... | collective-permute-start | bytes 688136 | tf_op jit(solution)/shard_map/ppermute | solution.py:99
  123.6 13.7 %collective-permute-start.4 = (bf16[224,512]{1,0:T(8,128)(2,1)S(1)}, bf16[224,512]{1,0:T(8,128)(2,1)S(1)}, u32[]{:S(2)}, u32[]{:S(2)}) collective-permute-start(bf16[224,512]{1,0:T(8,128)(2,1)S(1)} %get-tuple-element.18), channel_id=1, source_target_pairs={{0,2},{1,3},{2,0},{3,1},{4,6},{5,7},{6,4},{7,5},{8,10},{9,11},{10,... | collective-permute-start | bytes 688136 | tf_op jit(solution)/shard_map/ppermute | solution.py:99
  127.0 12.5 %collective-permute-start.5 = (bf16[224,512]{1,0:T(8,128)(2,1)S(1)}, bf16[224,512]{1,0:T(8,128)(2,1)S(1)}, u32[]{:S(2)}, u32[]{:S(2)}) collective-permute-start(bf16[224,512]{1,0:T(8,128)(2,1)S(1)} %get-tuple-element.17), channel_id=1, source_target_pairs={{0,3},{1,0},{2,1},{3,2},{4,7},{5,4},{6,5},{7,6},{8,11},{9,8},{10,9... | collective-permute-start | bytes 688136 | tf_op jit(solution)/shard_map/ppermute | solution.py:99

commit v14 on v12

--- a/solution.py
+++ b/solution.py
@@ -51,6 +51,19 @@
     query_pos = start_row + jnp.arange(row_count, dtype=jnp.int32)[:, None]
     key_pos = jnp.arange(key_rows.shape[0], dtype=jnp.int32)[None, :]
     allowed = (key_pos <= query_pos) & (key_pos < length)
+    scores = jnp.where(allowed, scores, -jnp.inf)
+    row_top = jnp.max(scores, axis=-1, keepdims=True)
+    powered = jnp.exp(scores - row_top)
+    weights = (powered / jnp.sum(powered, axis=-1, keepdims=True)).astype(jnp.bfloat16)
+    return jnp.dot(weights, value_rows, preferred_element_type=jnp.float32).astype(jnp.bfloat16)
+
+
+def attend_rows(query_block, query_pos, key_rows, value_rows, length):
+    scores = jnp.dot(query_block, key_rows.T, preferred_element_type=jnp.float32) * key_rows.shape[
+        1
+    ] ** (-0.5)
+    key_pos = jnp.arange(key_rows.shape[0], dtype=jnp.int32)[None, :]
+    allowed = (key_pos <= query_pos[:, None]) & (key_pos < length)
     scores = jnp.where(allowed, scores, -jnp.inf)
     row_top = jnp.max(scores, axis=-1, keepdims=True)
     powered = jnp.exp(scores - row_top)
@@ -191,9 +204,21 @@
         value_chunks.append(own_cached[:, HD : 2 * HD])
         key_rows = jnp.concatenate(key_chunks, axis=0)
         value_rows = jnp.concatenate(value_chunks, axis=0)
-        head_outputs = []
-        for head_index in range(head_count):
-            head_outputs.append(
+        stacked_query = jnp.concatenate(
+            [rotated_query[:, head_index * HD : (head_index + 1) * HD] for head_index in range(head_count)],
+            axis=0,
+        )
+        if head_count == per_group:
+            stacked_out = attend_rows(
+                stacked_query, jnp.tile(chunk_first + jnp.arange(chunk_rows, dtype=jnp.int32), head_count),
+                key_rows, value_rows, own_length,
+            )
+            head_outputs = [
+                stacked_out[head_index * chunk_rows : (head_index + 1) * chunk_rows]
+                for head_index in range(head_count)
+            ]
+        else:
+            head_outputs = [
                 attend(
                     rotated_query[:, head_index * HD : (head_index + 1) * HD],
                     chunk_first,
@@ -201,7 +226,8 @@
                     value_rows,
                     own_length,
                 )
-            )
+                for head_index in range(head_count)
+            ]
         attention_rows = jnp.concatenate(head_outputs, axis=1)
         outgoing = from_request(attention_rows, shift_by, source_count)
         returned_chunks.append(

time: 135 us -> 135 us (level)
    unnamed x15 -> x17, local copies, waits for them, and re-layouts: 2.9 us -> 2.91 us
where the time goes in v14:
time: 135 us; the launch traced here: 134 us
  waiting for transfers between devices  45.2 us (33%)
  starting transfers between devices  42.1 us (31%)
  other arithmetic  23.2 us (17%)
  local copies, waits for them, and re-layouts  13.8 us (10%)
  matrix products  6.62 us (5%)
  between operations  3.06 us (2%)
    ppermute x3, waiting for transfers between devices, ring_blocks(): blocks.append(lax.ppermute(narrow, axis_name, perm))  21.7 us
    all_to_all x1, starting transfers between devices, body(): lax.all_to_all(picked[:, chunk * chunk_slots:(chunk + 1) * chunk_slots],...  18.4 us
    all_to_all x1, waiting for transfers between devices, body(): lax.all_to_all(picked[:, chunk * chunk_slots:(chunk + 1) * chunk_slots],...  10.7 us
    ppermute x3, starting transfers between devices, ring_blocks(): blocks.append(lax.ppermute(narrow, axis_name, perm))  9.64 us
    ppermute x3, starting transfers between devices, ring_output(): lax.ppermute(parts[shift], axis_name, perm).astype(jnp.float32)  8.41 us
    ppermute x3, waiting for transfers between devices, ring_output(): lax.ppermute(parts[shift], axis_name, perm).astype(jnp.float32)  8.28 us
    concatenate x1, other arithmetic, body(): jnp.roll(keyval_weight, -tensor_offset, axis=0)  6.61 us
    all_to_all x1, starting transfers between devices, body(): lax.all_to_all(outgoing, 'seq', split_axis=0, concat_axis=0, tiled=True)  5.63 us
  transfers between devices with their start and end apart: 8, of which 6 were waited for; matrix products, arithmetic and copies ran while one was open for 20% of the time, Pallas kernels for 0%

profile of v14, /device:TPU:1, one launch (start us, length us, event | category | flops | bytes accessed | tf_op | source)
XLA Modules:
  0.0 134.1 jit_solution(14207295105469510761)
XLA Ops:
  4.3 18.4 %all-to-all-start = ((bf16[128,4,512]{2,1,0:T(4,128)(2,1)}), bf16[128,4,512]{2,1,0:T(4,128)(2,1)S(1)}, u32[]{:S(2)}, u32[]{:S(2)}) async-start(bf16[128,4,512]{2,1,0:T(4,128)(2,1)} %reshape.230), calls=%async_computation | async-start | bytes 1048576 | tf_op jit(solution)/shard_map/all_to_all | solution.py:173
  26.1 6.6 %fusion.4 = (bf16[2048,512]{1,0:T(8,128)(2,1)}, bf16[2048,512]{1,0:T(8,128)(2,1)}) fusion(s32[]{:T(128)S(6)} %select_n.91, bf16[2048,512]{1,0:T(8,128)(2,1)S(1)} %copy-done.1, bf16[2048,512]{1,0:T(8,128)(2,1)} %param.15), kind=kLoop, calls=%fused_computation.12 | loop fusion | flops 8388608 | bytes 8388612 | tf_op jit(solution)/shard_map/jit(_roll_dynamic)/concatenate | solution.py:186
  32.7 10.7 %all-to-all-done = bf16[128,4,512]{2,1,0:T(4,128)(2,1)S(1)} async-done(((bf16[128,4,512]{2,1,0:T(4,128)(2,1)}), bf16[128,4,512]{2,1,0:T(4,128)(2,1)S(1)}, u32[]{:S(2)}, u32[]{:S(2)}) %all-to-all-start) | async-done | bytes 524320 | tf_op jit(solution)/shard_map/all_to_all | solution.py:173
  43.9 4.5 %collective-permute-start = (bf16[512,512]{1,0:T(8,128)(2,1)S(1)}, bf16[512,512]{1,0:T(8,128)(2,1)S(1)}, u32[]{:S(2)}, u32[]{:S(2)}) collective-permute-start(bf16[512,512]{1,0:T(8,128)(2,1)S(1)} %bitcast.50), channel_id=1, source_target_pairs={{0,3},{1,0},{2,1},{3,2},{4,7},{5,4},{6,5},{7,6},{8,11},{9,8},{10,9... | collective-permute-start | bytes 1572872 | tf_op jit(solution)/shard_map/ppermute | solution.py:89
  48.4 2.4 %collective-permute-start.1 = (bf16[512,512]{1,0:T(8,128)(2,1)S(1)}, bf16[512,512]{1,0:T(8,128)(2,1)S(1)}, u32[]{:S(2)}, u32[]{:S(2)}) collective-permute-start(bf16[512,512]{1,0:T(8,128)(2,1)S(1)} %bitcast.51), channel_id=1, source_target_pairs={{0,2},{1,3},{2,0},{3,1},{4,6},{5,7},{6,4},{7,5},{8,10},{9,11},{10,... | collective-permute-start | bytes 1572872 | tf_op jit(solution)/shard_map/ppermute | solution.py:89
  50.8 2.7 %collective-permute-start.2 = (bf16[512,512]{1,0:T(8,128)(2,1)S(1)}, bf16[512,512]{1,0:T(8,128)(2,1)S(1)}, u32[]{:S(2)}, u32[]{:S(2)}) collective-permute-start(bf16[512,512]{1,0:T(8,128)(2,1)S(1)} %bitcast.52), channel_id=1, source_target_pairs={{0,1},{1,2},{2,3},{3,0},{4,5},{5,6},{6,7},{7,4},{8,9},{9,10},{10,1... | collective-permute-start | bytes 1572872 | tf_op jit(solution)/shard_map/ppermute | solution.py:89
  55.2 15.9 %collective-permute-done = bf16[512,512]{1,0:T(8,128)(2,1)S(1)} collective-permute-done((bf16[512,512]{1,0:T(8,128)(2,1)S(1)}, bf16[512,512]{1,0:T(8,128)(2,1)S(1)}, u32[]{:S(2)}, u32[]{:S(2)}) %collective-permute-start) | collective-permute-done | bytes 524320 | tf_op jit(solution)/shard_map/ppermute | solution.py:89
  71.2 5.7 %collective-permute-done.2 = bf16[512,512]{1,0:T(8,128)(2,1)S(1)} collective-permute-done((bf16[512,512]{1,0:T(8,128)(2,1)S(1)}, bf16[512,512]{1,0:T(8,128)(2,1)S(1)}, u32[]{:S(2)}, u32[]{:S(2)}) %collective-permute-start.2) | collective-permute-done | bytes 524320 | tf_op jit(solution)/shard_map/ppermute | solution.py:89
  77.4 1.4 %fusion.16 = f32[512,512]{0,1:T(8,128)S(1)} fusion(bf16[2048,512]{1,0:T(8,128)(2,1)S(1)} %copy-done.3, f32[2048]{0:T(1024)S(1)} %convert_element_type.79, f32[512]{0:T(512)S(1)} %add_rsqrt_fusion, bf16[512,512]{1,0:T(8,128)(2,1)S(1)} %collective-permute-done.2, bf16[512,512]{1,0:T(8,128)(2,1)S(1)} %collective-permute-done.1, ...), kind=kOutput, calls=%fused_computation.32 | convolution fusion | flops 1085276160 | bytes 5253120 | tf_op jit(solution)/shard_map/dot_general | solution.py:97
  78.9 1.2 fusion.37
  80.1 1.4 %fusion.18 = f32[512,512]{0,1:T(8,128)S(1)} fusion(bf16[2048,512]{1,0:T(8,128)(2,1)S(1)} %copy-done.2, f32[2048]{0:T(1024)S(1)} %convert_element_type.79, f32[512]{0:T(512)S(1)} %add_rsqrt_fusion, bf16[512,512]{1,0:T(8,128)(2,1)S(1)} %collective-permute-done.2, bf16[512,512]{1,0:T(8,128)(2,1)S(1)} %collective-permute-done.1, ...), kind=kOutput, calls=%fused_computation.33 | convolution fusion | flops 1085276160 | bytes 5253120 | tf_op jit(solution)/shard_map/dot_general | solution.py:96
  84.2 1.7 %fusion.20 = bf16[128,4,512]{2,1,0:T(4,128)(2,1)} fusion(s32[]{:T(128)S(6)} %select_n.107, bf16[128,4,512]{2,1,0:T(4,128)(2,1)S(1)} %bitcast.57), kind=kLoop, calls=%fused_computation.34 | loop fusion | flops 262144 | bytes 1048580 | tf_op jit(solution)/shard_map/jit(_roll_dynamic)/concatenate | solution.py:81
  85.9 5.6 %all-to-all-start.1 = ((bf16[128,4,512]{2,1,0:T(4,128)(2,1)}), bf16[128,4,512]{2,1,0:T(4,128)(2,1)S(1)}, u32[]{:S(2)}, u32[]{:S(2)}) async-start(bf16[128,4,512]{2,1,0:T(4,128)(2,1)} %fusion.20), calls=%async_computation.1 | async-start | bytes 1048576 | tf_op jit(solution)/shard_map/all_to_all | solution.py:234
  92.2 2.9 %copy.24 = bf16[512,2048]{0,1:T(8,128)(2,1)S(1)} copy(bf16[512,2048]{1,0:T(8,128)(2,1)} %param.17) | data formatting | bytes 4194304 | tf_op args[4]
  95.1 5.0 %fusion.3 = bf16[512,2048]{0,1:T(8,128)(2,1)} fusion(s32[]{:T(128)S(6)} %select_n.83, bf16[512,2048]{0,1:T(8,128)(2,1)S(1)} %copy.24), kind=kLoop, calls=%fused_computation.11 | loop fusion | flops 4194304 | bytes 4194308 | tf_op jit(solution)/shard_map/jit(_roll_dynamic)/concatenate | solution.py:105
  100.1 2.8 %copy.26 = bf16[512,4,512]{2,0,1:T(8,128)(2,1)S(1)} copy(bf16[512,4,512]{0,2,1:T(8,128)(2,1)} %bitcast.49) | data formatting | bytes 4194304 | tf_op jit(solution)/shard_map/reshape | solution.py:106
  106.4 1.3 copy.30
  107.6 4.6 %all-to-all-done.1 = bf16[128,4,512]{2,1,0:T(4,128)(2,1)S(1)} async-done(((bf16[128,4,512]{2,1,0:T(4,128)(2,1)}), bf16[128,4,512]{2,1,0:T(4,128)(2,1)S(1)}, u32[]{:S(2)}, u32[]{:S(2)}) %all-to-all-start.1) | async-done | bytes 524320 | tf_op jit(solution)/shard_map/all_to_all | solution.py:234
  113.1 1.5 %fusion.26 = bf16[256,512]{1,0:T(8,128)(2,1)S(1)} fusion(bf16[512,512]{1,0:T(8,128)(2,1)} %reshape.235, s32[512]{0:T(512)S(1)} %add.131, pred[512]{0:T(512)(128)(4,1)S(1)} %compare_and_fusion), kind=kOutput, calls=%fused_computation.48 | convolution fusion | flops 134479872 | bytes 788992 | tf_op jit(solution)/shard_map/dot_general | solution.py:238
  115.4 1.9 %collective-permute-start.3 = (bf16[224,512]{1,0:T(8,128)(2,1)S(1)}, bf16[224,512]{1,0:T(8,128)(2,1)S(1)}, u32[]{:S(2)}, u32[]{:S(2)}) collective-permute-start(bf16[224,512]{1,0:T(8,128)(2,1)S(1)} %get-tuple-element.19), channel_id=1, source_target_pairs={{0,1},{1,2},{2,3},{3,0},{4,5},{5,6},{6,7},{7,4},{8,9},{9,10},{10,1... | collective-permute-start | bytes 688136 | tf_op jit(solution)/shard_map/ppermute | solution.py:113
  117.3 3.4 %collective-permute-start.4 = (bf16[224,512]{1,0:T(8,128)(2,1)S(1)}, bf16[224,512]{1,0:T(8,128)(2,1)S(1)}, u32[]{:S(2)}, u32[]{:S(2)}) collective-permute-start(bf16[224,512]{1,0:T(8,128)(2,1)S(1)} %get-tuple-element.21), channel_id=1, source_target_pairs={{0,2},{1,3},{2,0},{3,1},{4,6},{5,7},{6,4},{7,5},{8,10},{9,11},{10,... | collective-permute-start | bytes 688136 | tf_op jit(solution)/shard_map/ppermute | solution.py:113
  120.7 3.1 %collective-permute-start.5 = (bf16[224,512]{1,0:T(8,128)(2,1)S(1)}, bf16[224,512]{1,0:T(8,128)(2,1)S(1)}, u32[]{:S(2)}, u32[]{:S(2)}) collective-permute-start(bf16[224,512]{1,0:T(8,128)(2,1)S(1)} %get-tuple-element.20), channel_id=1, source_target_pairs={{0,3},{1,0},{2,1},{3,2},{4,7},{5,4},{6,5},{7,6},{8,11},{9,8},{10,9... | collective-permute-start | bytes 688136 | tf_op jit(solution)/shard_map/ppermute | solution.py:113
  125.0 6.0 %collective-permute-done.3 = bf16[224,512]{1,0:T(8,128)(2,1)S(1)} collective-permute-done((bf16[224,512]{1,0:T(8,128)(2,1)S(1)}, bf16[224,512]{1,0:T(8,128)(2,1)S(1)}, u32[]{:S(2)}, u32[]{:S(2)}) %collective-permute-start.3) | collective-permute-done | bytes 229408 | tf_op jit(solution)/shard_map/ppermute | solution.py:113
  131.0 2.3 %collective-permute-done.5 = bf16[224,512]{1,0:T(8,128)(2,1)S(1)} collective-permute-done((bf16[224,512]{1,0:T(8,128)(2,1)S(1)}, bf16[224,512]{1,0:T(8,128)(2,1)S(1)}, u32[]{:S(2)}, u32[]{:S(2)}) %collective-permute-start.5) | collective-permute-done | bytes 229408 | tf_op jit(solution)/shard_map/ppermute | solution.py:113
  (65 shorter events, 18.1 us)
Async XLA Ops:
  0.6 2.4 %copy-start = (bf16[256,512]{1,0:T(8,128)(2,1)S(1)}, bf16[256,512]{1,0:T(8,128)(2,1)}, u32[]{:S(2)}) copy-start(bf16[256,512]{1,0:T(8,128)(2,1)} %param.13) | copy-start | bytes 786436
  0.6 25.3 %copy-start.6 = (bf16[2048]{0:T(1024)(128)(2,1)S(1)}, bf16[2048]{0:T(1024)(128)(2,1)}, u32[]{:S(2)}) copy-start(bf16[2048]{0:T(1024)(128)(2,1)} %param.14) | copy-start | bytes 12292
  0.7 25.4 %copy-start.1 = (bf16[2048,512]{1,0:T(8,128)(2,1)S(1)}, bf16[2048,512]{1,0:T(8,128)(2,1)}, u32[]{:S(2)}) copy-start(bf16[2048,512]{1,0:T(8,128)(2,1)} %param.16) | copy-start | bytes 6291460
  4.3 39.0 %all-to-all-start = ((bf16[128,4,512]{2,1,0:T(4,128)(2,1)}), bf16[128,4,512]{2,1,0:T(4,128)(2,1)S(1)}, u32[]{:S(2)}, u32[]{:S(2)}) async-start(bf16[128,4,512]{2,1,0:T(4,128)(2,1)} %reshape.230), calls=%async_computation | async-start | bytes 1048576 | tf_op jit(solution)/shard_map/all_to_all | solution.py:173
  43.4 34.0 %copy-start.3 = (bf16[2048,512]{1,0:T(8,128)(2,1)S(1)}, bf16[2048,512]{1,0:T(8,128)(2,1)}, u32[]{:S(2)}) copy-start(bf16[2048,512]{1,0:T(8,128)(2,1)} %get-tuple-element.11) | copy-start | bytes 6291460
  43.9 27.3 %collective-permute-start = (bf16[512,512]{1,0:T(8,128)(2,1)S(1)}, bf16[512,512]{1,0:T(8,128)(2,1)S(1)}, u32[]{:S(2)}, u32[]{:S(2)}) collective-permute-start(bf16[512,512]{1,0:T(8,128)(2,1)S(1)} %bitcast.50), channel_id=1, source_target_pairs={{0,3},{1,0},{2,1},{3,2},{4,7},{5,4},{6,5},{7,6},{8,11},{9,8},{10,9... | collective-permute-start | bytes 1572872 | tf_op jit(solution)/shard_map/ppermute | solution.py:89
  48.4 22.8 %collective-permute-start.1 = (bf16[512,512]{1,0:T(8,128)(2,1)S(1)}, bf16[512,512]{1,0:T(8,128)(2,1)S(1)}, u32[]{:S(2)}, u32[]{:S(2)}) collective-permute-start(bf16[512,512]{1,0:T(8,128)(2,1)S(1)} %bitcast.51), channel_id=1, source_target_pairs={{0,2},{1,3},{2,0},{3,1},{4,6},{5,7},{6,4},{7,5},{8,10},{9,11},{10,... | collective-permute-start | bytes 1572872 | tf_op jit(solution)/shard_map/ppermute | solution.py:89
  50.8 26.1 %collective-permute-start.2 = (bf16[512,512]{1,0:T(8,128)(2,1)S(1)}, bf16[512,512]{1,0:T(8,128)(2,1)S(1)}, u32[]{:S(2)}, u32[]{:S(2)}) collective-permute-start(bf16[512,512]{1,0:T(8,128)(2,1)S(1)} %bitcast.52), channel_id=1, source_target_pairs={{0,1},{1,2},{2,3},{3,0},{4,5},{5,6},{6,7},{7,4},{8,9},{9,10},{10,1... | collective-permute-start | bytes 1572872 | tf_op jit(solution)/shard_map/ppermute | solution.py:89
  77.4 2.6 %copy-start.2 = (bf16[2048,512]{1,0:T(8,128)(2,1)S(1)}, bf16[2048,512]{1,0:T(8,128)(2,1)}, u32[]{:S(2)}) copy-start(bf16[2048,512]{1,0:T(8,128)(2,1)} %get-tuple-element.10) | copy-start | bytes 6291460
  78.8 4.0 %copy-start.4 = (f32[512,512]{0,1:T(8,128)}, f32[512,512]{0,1:T(8,128)S(1)}, u32[]{:S(2)}) copy-start(f32[512,512]{0,1:T(8,128)S(1)} %fusion.16) | copy-start | bytes 3145732
  80.1 1.7 %copy-start.5 = (bf16[512,1,128]{0,2,1:T(8,128)(2,1)}, bf16[512,1,128]{0,2,1:T(8,128)(2,1)S(1)}, u32[]{:S(2)}) copy-start(bf16[512,1,128]{0,2,1:T(8,128)(2,1)S(1)} %get-tuple-element.23) | copy-start | bytes 393220
  85.9 26.3 %all-to-all-start.1 = ((bf16[128,4,512]{2,1,0:T(4,128)(2,1)}), bf16[128,4,512]{2,1,0:T(4,128)(2,1)S(1)}, u32[]{:S(2)}, u32[]{:S(2)}) async-start(bf16[128,4,512]{2,1,0:T(4,128)(2,1)} %fusion.20), calls=%async_computation.1 | async-start | bytes 1048576 | tf_op jit(solution)/shard_map/all_to_all | solution.py:234
  115.4 15.6 %collective-permute-start.3 = (bf16[224,512]{1,0:T(8,128)(2,1)S(1)}, bf16[224,512]{1,0:T(8,128)(2,1)S(1)}, u32[]{:S(2)}, u32[]{:S(2)}) collective-permute-start(bf16[224,512]{1,0:T(8,128)(2,1)S(1)} %get-tuple-element.19), channel_id=1, source_target_pairs={{0,1},{1,2},{2,3},{3,0},{4,5},{5,6},{6,7},{7,4},{8,9},{9,10},{10,1... | collective-permute-start | bytes 688136 | tf_op jit(solution)/shard_map/ppermute | solution.py:113
  117.3 13.7 %collective-permute-start.4 = (bf16[224,512]{1,0:T(8,128)(2,1)S(1)}, bf16[224,512]{1,0:T(8,128)(2,1)S(1)}, u32[]{:S(2)}, u32[]{:S(2)}) collective-permute-start(bf16[224,512]{1,0:T(8,128)(2,1)S(1)} %get-tuple-element.21), channel_id=1, source_target_pairs={{0,2},{1,3},{2,0},{3,1},{4,6},{5,7},{6,4},{7,5},{8,10},{9,11},{10,... | collective-permute-start | bytes 688136 | tf_op jit(solution)/shard_map/ppermute | solution.py:113
  120.7 12.5 %collective-permute-start.5 = (bf16[224,512]{1,0:T(8,128)(2,1)S(1)}, bf16[224,512]{1,0:T(8,128)(2,1)S(1)}, u32[]{:S(2)}, u32[]{:S(2)}) collective-permute-start(bf16[224,512]{1,0:T(8,128)(2,1)S(1)} %get-tuple-element.20), channel_id=1, source_target_pairs={{0,3},{1,0},{2,1},{3,2},{4,7},{5,4},{6,5},{7,6},{8,11},{9,8},{10,9... | collective-permute-start | bytes 688136 | tf_op jit(solution)/shard_map/ppermute | solution.py:113

commit v15 on v14

--- a/solution.py
+++ b/solution.py
@@ -98,19 +98,24 @@
     return queries, keyvals
 
 
-def ring_output(local_attention, output_weight, axis_name):
+def ring_output(local_attention, output_weight, axis_name, sent_rows):
     count = lax.axis_size(axis_name)
     position = lax.axis_index(axis_name)
     width = output_weight.shape[1] // count
     rotated = jnp.roll(output_weight, -position * width, axis=1)
     stacked = jnp.transpose(rotated.reshape(rotated.shape[0], count, width), (1, 0, 2))
+    own = jnp.dot(
+        local_attention, stacked[0], preferred_element_type=jnp.float32
+    ).astype(jnp.bfloat16)
     parts = jnp.einsum(
-        "id,kdc->kic", local_attention, stacked, preferred_element_type=jnp.float32
-    ).astype(jnp.bfloat16)
-    total = parts[0].astype(jnp.float32)
+        "id,kdc->kic", local_attention[:sent_rows], stacked[1:], preferred_element_type=jnp.float32
+    ).astype(jnp.bfloat16)
+    pad_rows = local_attention.shape[0] - sent_rows
+    total = own.astype(jnp.float32)
     for shift in range(1, count):
         perm = [(index, (index + shift) % count) for index in range(count)]
-        total = total + lax.ppermute(parts[shift], axis_name, perm).astype(jnp.float32)
+        arrived = lax.ppermute(parts[shift - 1], axis_name, perm).astype(jnp.float32)
+        total = total + jnp.pad(arrived, ((0, pad_rows), (0, 0)))
     return total.astype(jnp.bfloat16)
 
 
@@ -239,12 +244,7 @@
         select, flattened, (((0,), (0,)), ((), ())), preferred_element_type=jnp.float32
     ).astype(jnp.bfloat16)
     filled_rows = min(-(-FILLED // source_count), local_rows)
-    attended = ring_output(local_attention[:filled_rows], output_weight, "tensor")
-    if filled_rows < local_rows:
-        attended = jnp.concatenate(
-            [attended, jnp.zeros((local_rows - filled_rows, attended.shape[1]), attended.dtype)],
-            axis=0,
-        )
+    attended = ring_output(local_attention, output_weight, "tensor", filled_rows)
     all_cached = jnp.concatenate(cached_chunks, axis=0)
     slot_ids = jnp.arange(SLOTS_DEV, dtype=jnp.int32)
     cache_table = jnp.where(

time: 135 us -> 135 us (level)
    unnamed x17 -> x15, local copies, waits for them, and re-layouts: 2.91 us -> 2.9 us
  transfers between devices with their start and end apart: 8 -> 8, of which waited for: 6 -> 6; matrix products, arithmetic and copies ran while one was open for 20% -> 19% of each run, Pallas kernels for 0% -> 0%
where the time goes in v15:
time: 135 us; the launch traced here: 134 us
  waiting for transfers between devices  46.2 us (34%)
  starting transfers between devices  42.1 us (31%)
  other arithmetic  22.2 us (16%)
  local copies, waits for them, and re-layouts  13 us (10%)
  matrix products  7.53 us (6%)
  between operations  3.05 us (2%)
    ppermute x3, waiting for transfers between devices, ring_blocks(): blocks.append(lax.ppermute(narrow, axis_name, perm))  21.7 us
    all_to_all x1, starting transfers between devices, body(): lax.all_to_all(picked[:, chunk * chunk_slots:(chunk + 1) * chunk_slots],...  18.4 us
    all_to_all x1, waiting for transfers between devices, body(): lax.all_to_all(picked[:, chunk * chunk_slots:(chunk + 1) * chunk_slots],...  10.7 us
    ppermute x3, starting transfers between devices, ring_blocks(): blocks.append(lax.ppermute(narrow, axis_name, perm))  9.64 us
    ppermute x3, starting transfers between devices, ring_output(): lax.ppermute(parts[shift - 1], axis_name, perm).astype(jnp.float32)  8.41 us
    ppermute x3, waiting for transfers between devices, ring_output(): lax.ppermute(parts[shift - 1], axis_name, perm).astype(jnp.float32)  8.28 us
    concatenate x1, other arithmetic, body(): jnp.roll(keyval_weight, -tensor_offset, axis=0)  6.61 us
    all_to_all x1, starting transfers between devices, body(): lax.all_to_all(outgoing, 'seq', split_axis=0, concat_axis=0, tiled=True)  5.63 us
  transfers between devices with their start and end apart: 8, of which 6 were waited for; matrix products, arithmetic and copies ran while one was open for 19% of the time, Pallas kernels for 0%

profile of v15, /device:TPU:1, one launch (start us, length us, event | category | flops | bytes accessed | tf_op | source)
XLA Modules:
  0.0 134.1 jit_solution(10317688928392401453)
XLA Ops:
  4.3 18.4 %all-to-all-start = ((bf16[128,4,512]{2,1,0:T(4,128)(2,1)}), bf16[128,4,512]{2,1,0:T(4,128)(2,1)S(1)}, u32[]{:S(2)}, u32[]{:S(2)}) async-start(bf16[128,4,512]{2,1,0:T(4,128)(2,1)} %reshape.227), calls=%async_computation | async-start | bytes 1048576 | tf_op jit(solution)/shard_map/all_to_all | solution.py:178
  26.1 6.6 %fusion.4 = (bf16[2048,512]{1,0:T(8,128)(2,1)}, bf16[2048,512]{1,0:T(8,128)(2,1)}) fusion(s32[]{:T(128)S(6)} %select_n.89, bf16[2048,512]{1,0:T(8,128)(2,1)S(1)} %copy-done.1, bf16[2048,512]{1,0:T(8,128)(2,1)} %param.15), kind=kLoop, calls=%fused_computation.12 | loop fusion | flops 8388608 | bytes 8388612 | tf_op jit(solution)/shard_map/jit(_roll_dynamic)/concatenate | solution.py:191
  32.7 10.7 %all-to-all-done = bf16[128,4,512]{2,1,0:T(4,128)(2,1)S(1)} async-done(((bf16[128,4,512]{2,1,0:T(4,128)(2,1)}), bf16[128,4,512]{2,1,0:T(4,128)(2,1)S(1)}, u32[]{:S(2)}, u32[]{:S(2)}) %all-to-all-start) | async-done | bytes 524320 | tf_op jit(solution)/shard_map/all_to_all | solution.py:178
  43.9 4.5 %collective-permute-start = (bf16[512,512]{1,0:T(8,128)(2,1)S(1)}, bf16[512,512]{1,0:T(8,128)(2,1)S(1)}, u32[]{:S(2)}, u32[]{:S(2)}) collective-permute-start(bf16[512,512]{1,0:T(8,128)(2,1)S(1)} %bitcast.45), channel_id=1, source_target_pairs={{0,3},{1,0},{2,1},{3,2},{4,7},{5,4},{6,5},{7,6},{8,11},{9,8},{10,9... | collective-permute-start | bytes 1572872 | tf_op jit(solution)/shard_map/ppermute | solution.py:89
  48.4 2.4 %collective-permute-start.1 = (bf16[512,512]{1,0:T(8,128)(2,1)S(1)}, bf16[512,512]{1,0:T(8,128)(2,1)S(1)}, u32[]{:S(2)}, u32[]{:S(2)}) collective-permute-start(bf16[512,512]{1,0:T(8,128)(2,1)S(1)} %bitcast.46), channel_id=1, source_target_pairs={{0,2},{1,3},{2,0},{3,1},{4,6},{5,7},{6,4},{7,5},{8,10},{9,11},{10,... | collective-permute-start | bytes 1572872 | tf_op jit(solution)/shard_map/ppermute | solution.py:89
  50.8 2.7 %collective-permute-start.2 = (bf16[512,512]{1,0:T(8,128)(2,1)S(1)}, bf16[512,512]{1,0:T(8,128)(2,1)S(1)}, u32[]{:S(2)}, u32[]{:S(2)}) collective-permute-start(bf16[512,512]{1,0:T(8,128)(2,1)S(1)} %bitcast.47), channel_id=1, source_target_pairs={{0,1},{1,2},{2,3},{3,0},{4,5},{5,6},{6,7},{7,4},{8,9},{9,10},{10,1... | collective-permute-start | bytes 1572872 | tf_op jit(solution)/shard_map/ppermute | solution.py:89
  55.2 15.9 %collective-permute-done = bf16[512,512]{1,0:T(8,128)(2,1)S(1)} collective-permute-done((bf16[512,512]{1,0:T(8,128)(2,1)S(1)}, bf16[512,512]{1,0:T(8,128)(2,1)S(1)}, u32[]{:S(2)}, u32[]{:S(2)}) %collective-permute-start) | collective-permute-done | bytes 524320 | tf_op jit(solution)/shard_map/ppermute | solution.py:89
  71.2 5.8 %collective-permute-done.2 = bf16[512,512]{1,0:T(8,128)(2,1)S(1)} collective-permute-done((bf16[512,512]{1,0:T(8,128)(2,1)S(1)}, bf16[512,512]{1,0:T(8,128)(2,1)S(1)}, u32[]{:S(2)}, u32[]{:S(2)}) %collective-permute-start.2) | collective-permute-done | bytes 524320 | tf_op jit(solution)/shard_map/ppermute | solution.py:89
  77.4 1.4 %fusion.17 = f32[512,512]{0,1:T(8,128)S(1)} fusion(bf16[2048,512]{1,0:T(8,128)(2,1)S(1)} %copy-done.3, f32[2048]{0:T(1024)S(1)} %convert_element_type.77, f32[512]{0:T(512)S(1)} %add_rsqrt_fusion, bf16[512,512]{1,0:T(8,128)(2,1)S(1)} %collective-permute-done.2, bf16[512,512]{1,0:T(8,128)(2,1)S(1)} %collective-permute-done.1, ...), kind=kOutput, calls=%fused_computation.35 | convolution fusion | flops 1085276160 | bytes 5253120 | tf_op jit(solution)/shard_map/dot_general | solution.py:97
  78.9 1.2 fusion.34
  80.1 1.4 %fusion.19 = f32[512,512]{0,1:T(8,128)S(1)} fusion(bf16[2048,512]{1,0:T(8,128)(2,1)S(1)} %copy-done.2, f32[2048]{0:T(1024)S(1)} %convert_element_type.77, f32[512]{0:T(512)S(1)} %add_rsqrt_fusion, bf16[512,512]{1,0:T(8,128)(2,1)S(1)} %collective-permute-done.2, bf16[512,512]{1,0:T(8,128)(2,1)S(1)} %collective-permute-done.1, ...), kind=kOutput, calls=%fused_computation.36 | convolution fusion | flops 1085276160 | bytes 5253120 | tf_op jit(solution)/shard_map/dot_general | solution.py:96
  84.2 1.7 %fusion.21 = bf16[128,4,512]{2,1,0:T(4,128)(2,1)} fusion(s32[]{:T(128)S(6)} %select_n.107, bf16[128,4,512]{2,1,0:T(4,128)(2,1)S(1)} %bitcast.54), kind=kLoop, calls=%fused_computation.37 | loop fusion | flops 262144 | bytes 1048580 | tf_op jit(solution)/shard_map/jit(_roll_dynamic)/concatenate | solution.py:81
  85.9 5.6 %all-to-all-start.1 = ((bf16[128,4,512]{2,1,0:T(4,128)(2,1)}), bf16[128,4,512]{2,1,0:T(4,128)(2,1)S(1)}, u32[]{:S(2)}, u32[]{:S(2)}) async-start(bf16[128,4,512]{2,1,0:T(4,128)(2,1)} %fusion.21), calls=%async_computation.1 | async-start | bytes 1048576 | tf_op jit(solution)/shard_map/all_to_all | solution.py:239
  92.1 2.9 %copy.27 = bf16[512,2048]{0,1:T(8,128)(2,1)S(1)} copy(bf16[512,2048]{1,0:T(8,128)(2,1)} %param.17) | data formatting | bytes 4194304 | tf_op args[4]
  95.0 5.0 %fusion.3 = bf16[512,2048]{0,1:T(8,128)(2,1)} fusion(s32[]{:T(128)S(6)} %select_n.93, bf16[512,2048]{0,1:T(8,128)(2,1)S(1)} %copy.27), kind=kLoop, calls=%fused_computation.11 | loop fusion | flops 4194304 | bytes 4194308 | tf_op jit(solution)/shard_map/jit(_roll_dynamic)/concatenate | solution.py:105
  99.9 2.8 %copy.29 = bf16[512,4,512]{2,0,1:T(8,128)(2,1)S(1)} copy(bf16[512,4,512]{0,2,1:T(8,128)(2,1)} %bitcast.44) | data formatting | bytes 4194304 | tf_op jit(solution)/shard_map/reshape | solution.py:106
  105.3 1.3 copy.30
  106.6 5.6 %all-to-all-done.1 = bf16[128,4,512]{2,1,0:T(4,128)(2,1)S(1)} async-done(((bf16[128,4,512]{2,1,0:T(4,128)(2,1)}), bf16[128,4,512]{2,1,0:T(4,128)(2,1)S(1)}, u32[]{:S(2)}, u32[]{:S(2)}) %all-to-all-start.1) | async-done | bytes 524320 | tf_op jit(solution)/shard_map/all_to_all | solution.py:239
  113.1 1.5 %convolution_convert_fusion.3 = bf16[256,512]{1,0:T(8,128)(2,1)S(1)} fusion(bf16[512,512]{1,0:T(8,128)(2,1)} %reshape.232, s32[512]{0:T(512)S(1)} %add.133, pred[512]{0:T(512)(128)(4,1)S(1)} %compare_and_fusion), kind=kOutput, calls=%fused_computation.29 | convolution fusion | flops 134610944 | bytes 788992 | tf_op jit(solution)/shard_map/dot_general | solution.py:243
  115.2 1.9 %collective-permute-start.3 = (bf16[224,512]{1,0:T(8,128)(2,1)S(1)}, bf16[224,512]{1,0:T(8,128)(2,1)S(1)}, u32[]{:S(2)}, u32[]{:S(2)}) collective-permute-start(bf16[224,512]{1,0:T(8,128)(2,1)S(1)} %get-tuple-element.19), channel_id=1, source_target_pairs={{0,1},{1,2},{2,3},{3,0},{4,5},{5,6},{6,7},{7,4},{8,9},{9,10},{10,1... | collective-permute-start | bytes 688136 | tf_op jit(solution)/shard_map/ppermute | solution.py:117
  117.2 3.4 %collective-permute-start.4 = (bf16[224,512]{1,0:T(8,128)(2,1)S(1)}, bf16[224,512]{1,0:T(8,128)(2,1)S(1)}, u32[]{:S(2)}, u32[]{:S(2)}) collective-permute-start(bf16[224,512]{1,0:T(8,128)(2,1)S(1)} %get-tuple-element.21), channel_id=1, source_target_pairs={{0,2},{1,3},{2,0},{3,1},{4,6},{5,7},{6,4},{7,5},{8,10},{9,11},{10,... | collective-permute-start | bytes 688136 | tf_op jit(solution)/shard_map/ppermute | solution.py:117
  120.6 3.1 %collective-permute-start.5 = (bf16[224,512]{1,0:T(8,128)(2,1)S(1)}, bf16[224,512]{1,0:T(8,128)(2,1)S(1)}, u32[]{:S(2)}, u32[]{:S(2)}) collective-permute-start(bf16[224,512]{1,0:T(8,128)(2,1)S(1)} %get-tuple-element.20), channel_id=1, source_target_pairs={{0,3},{1,0},{2,1},{3,2},{4,7},{5,4},{6,5},{7,6},{8,11},{9,8},{10,9... | collective-permute-start | bytes 688136 | tf_op jit(solution)/shard_map/ppermute | solution.py:117
  124.8 6.0 %collective-permute-done.3 = bf16[224,512]{1,0:T(8,128)(2,1)S(1)} collective-permute-done((bf16[224,512]{1,0:T(8,128)(2,1)S(1)}, bf16[224,512]{1,0:T(8,128)(2,1)S(1)}, u32[]{:S(2)}, u32[]{:S(2)}) %collective-permute-start.3) | collective-permute-done | bytes 229408 | tf_op jit(solution)/shard_map/ppermute | solution.py:117
  130.8 2.3 %collective-permute-done.5 = bf16[224,512]{1,0:T(8,128)(2,1)S(1)} collective-permute-done((bf16[224,512]{1,0:T(8,128)(2,1)S(1)}, bf16[224,512]{1,0:T(8,128)(2,1)S(1)}, u32[]{:S(2)}, u32[]{:S(2)}) %collective-permute-start.5) | collective-permute-done | bytes 229408 | tf_op jit(solution)/shard_map/ppermute | solution.py:117
  (62 shorter events, 17.1 us)
Async XLA Ops:
  0.6 2.4 %copy-start = (bf16[256,512]{1,0:T(8,128)(2,1)S(1)}, bf16[256,512]{1,0:T(8,128)(2,1)}, u32[]{:S(2)}) copy-start(bf16[256,512]{1,0:T(8,128)(2,1)} %param.13) | copy-start | bytes 786436
  0.6 25.3 %copy-start.5 = (bf16[2048]{0:T(1024)(128)(2,1)S(1)}, bf16[2048]{0:T(1024)(128)(2,1)}, u32[]{:S(2)}) copy-start(bf16[2048]{0:T(1024)(128)(2,1)} %param.14) | copy-start | bytes 12292
  0.7 25.4 %copy-start.1 = (bf16[2048,512]{1,0:T(8,128)(2,1)S(1)}, bf16[2048,512]{1,0:T(8,128)(2,1)}, u32[]{:S(2)}) copy-start(bf16[2048,512]{1,0:T(8,128)(2,1)} %param.16) | copy-start | bytes 6291460
  4.3 39.0 %all-to-all-start = ((bf16[128,4,512]{2,1,0:T(4,128)(2,1)}), bf16[128,4,512]{2,1,0:T(4,128)(2,1)S(1)}, u32[]{:S(2)}, u32[]{:S(2)}) async-start(bf16[128,4,512]{2,1,0:T(4,128)(2,1)} %reshape.227), calls=%async_computation | async-start | bytes 1048576 | tf_op jit(solution)/shard_map/all_to_all | solution.py:178
  43.4 34.0 %copy-start.3 = (bf16[2048,512]{1,0:T(8,128)(2,1)S(1)}, bf16[2048,512]{1,0:T(8,128)(2,1)}, u32[]{:S(2)}) copy-start(bf16[2048,512]{1,0:T(8,128)(2,1)} %get-tuple-element.11) | copy-start | bytes 6291460
  43.9 27.3 %collective-permute-start = (bf16[512,512]{1,0:T(8,128)(2,1)S(1)}, bf16[512,512]{1,0:T(8,128)(2,1)S(1)}, u32[]{:S(2)}, u32[]{:S(2)}) collective-permute-start(bf16[512,512]{1,0:T(8,128)(2,1)S(1)} %bitcast.45), channel_id=1, source_target_pairs={{0,3},{1,0},{2,1},{3,2},{4,7},{5,4},{6,5},{7,6},{8,11},{9,8},{10,9... | collective-permute-start | bytes 1572872 | tf_op jit(solution)/shard_map/ppermute | solution.py:89
  48.4 22.8 %collective-permute-start.1 = (bf16[512,512]{1,0:T(8,128)(2,1)S(1)}, bf16[512,512]{1,0:T(8,128)(2,1)S(1)}, u32[]{:S(2)}, u32[]{:S(2)}) collective-permute-start(bf16[512,512]{1,0:T(8,128)(2,1)S(1)} %bitcast.46), channel_id=1, source_target_pairs={{0,2},{1,3},{2,0},{3,1},{4,6},{5,7},{6,4},{7,5},{8,10},{9,11},{10,... | collective-permute-start | bytes 1572872 | tf_op jit(solution)/shard_map/ppermute | solution.py:89
  50.8 26.1 %collective-permute-start.2 = (bf16[512,512]{1,0:T(8,128)(2,1)S(1)}, bf16[512,512]{1,0:T(8,128)(2,1)S(1)}, u32[]{:S(2)}, u32[]{:S(2)}) collective-permute-start(bf16[512,512]{1,0:T(8,128)(2,1)S(1)} %bitcast.47), channel_id=1, source_target_pairs={{0,1},{1,2},{2,3},{3,0},{4,5},{5,6},{6,7},{7,4},{8,9},{9,10},{10,1... | collective-permute-start | bytes 1572872 | tf_op jit(solution)/shard_map/ppermute | solution.py:89
  77.4 2.6 %copy-start.2 = (bf16[2048,512]{1,0:T(8,128)(2,1)S(1)}, bf16[2048,512]{1,0:T(8,128)(2,1)}, u32[]{:S(2)}) copy-start(bf16[2048,512]{1,0:T(8,128)(2,1)} %get-tuple-element.10) | copy-start | bytes 6291460
  78.8 4.0 %copy-start.4 = (f32[512,512]{0,1:T(8,128)}, f32[512,512]{0,1:T(8,128)S(1)}, u32[]{:S(2)}) copy-start(f32[512,512]{0,1:T(8,128)S(1)} %fusion.17) | copy-start | bytes 3145732
  85.9 26.3 %all-to-all-start.1 = ((bf16[128,4,512]{2,1,0:T(4,128)(2,1)}), bf16[128,4,512]{2,1,0:T(4,128)(2,1)S(1)}, u32[]{:S(2)}, u32[]{:S(2)}) async-start(bf16[128,4,512]{2,1,0:T(4,128)(2,1)} %fusion.21), calls=%async_computation.1 | async-start | bytes 1048576 | tf_op jit(solution)/shard_map/all_to_all | solution.py:239
  115.2 15.6 %collective-permute-start.3 = (bf16[224,512]{1,0:T(8,128)(2,1)S(1)}, bf16[224,512]{1,0:T(8,128)(2,1)S(1)}, u32[]{:S(2)}, u32[]{:S(2)}) collective-permute-start(bf16[224,512]{1,0:T(8,128)(2,1)S(1)} %get-tuple-element.19), channel_id=1, source_target_pairs={{0,1},{1,2},{2,3},{3,0},{4,5},{5,6},{6,7},{7,4},{8,9},{9,10},{10,1... | collective-permute-start | bytes 688136 | tf_op jit(solution)/shard_map/ppermute | solution.py:117
  117.2 13.7 %collective-permute-start.4 = (bf16[224,512]{1,0:T(8,128)(2,1)S(1)}, bf16[224,512]{1,0:T(8,128)(2,1)S(1)}, u32[]{:S(2)}, u32[]{:S(2)}) collective-permute-start(bf16[224,512]{1,0:T(8,128)(2,1)S(1)} %get-tuple-element.21), channel_id=1, source_target_pairs={{0,2},{1,3},{2,0},{3,1},{4,6},{5,7},{6,4},{7,5},{8,10},{9,11},{10,... | collective-permute-start | bytes 688136 | tf_op jit(solution)/shard_map/ppermute | solution.py:117
  120.6 12.5 %collective-permute-start.5 = (bf16[224,512]{1,0:T(8,128)(2,1)S(1)}, bf16[224,512]{1,0:T(8,128)(2,1)S(1)}, u32[]{:S(2)}, u32[]{:S(2)}) collective-permute-start(bf16[224,512]{1,0:T(8,128)(2,1)S(1)} %get-tuple-element.20), channel_id=1, source_target_pairs={{0,3},{1,0},{2,1},{3,2},{4,7},{5,4},{6,5},{7,6},{8,11},{9,8},{10,9... | collective-permute-start | bytes 688136 | tf_op jit(solution)/shard_map/ppermute | solution.py:117
